TPU v7x, 256 devices: a whole 4x4x8 slice. The times are simulated.
256 devices in a mesh: lat: 8 (over x, y_hi), lon: 32 (over z, y_lo, core).
Axes of the slice: x: 4, y: 4 (y_hi: 2, y_lo: 2; y = y_hi * 2 + y_lo), z: 8, core: 2. Of those that a mesh axis runs over, the one named last changes fastest.
Arguments:
- probes: float32 [8, 4, 2048, 1024], P(None, None, 'lon', 'lat'), may hold values from -6 to 6
- wind: float32 [2, 4, 2048, 1024], P(None, None, 'lon', 'lat'), may hold values from -0.45 to 0.45
- wind_tend: float32 [2, 4, 2048, 1024], P(None, None, 'lon', 'lat'), may hold values from -0.05 to 0.05
- obs_weight: float32 [4, 2048, 1024], P(None, 'lon', 'lat'), may hold values from 0.5 to 18
Outputs:
- basis: float32 [8, 4, 2048, 1024], P(None, None, 'lon', 'lat')
- factor: float32 [8, 8], replicated
All inputs are finite; a program needn't handle non-finite values.
Results may differ from a plain program's by a relative error of at most 0.00012.
Values sent between devices are 32-bit elements; how exact they have to be, the bound alone decides.
No kernel may reach another device: no remote copies, remote signals or barrier semaphores. Data moves between devices by JAX's collectives and lax.ppermute only.
A program may use at most 64 MiB of HBM per device.

v0:
```python
import jax
import jax.numpy as jnp
from jax import lax
from jax.experimental import pallas as pl
from jax.experimental.pallas import tpu as pltpu
from jax.sharding import PartitionSpec as P

STEPS = 4
HALO = 2 * STEPS

diffuse = 0.24


def lower_inverse(lower):
    eye = jnp.eye(lower.shape[0], dtype=lower.dtype)
    return lax.linalg.triangular_solve(lower, eye, left_side=True, lower=True)


def neighbours(cells, axis, dim, closed):
    count = lax.axis_size(axis)
    ends = count if closed else count - 1
    size = cells.shape[dim]
    head = lax.slice_in_dim(cells, 0, HALO, axis=dim)
    tail = lax.slice_in_dim(cells, size - HALO, size, axis=dim)
    from_next = lax.ppermute(head, axis, [((i + 1) % count, i) for i in range(ends)])
    from_prev = lax.ppermute(tail, axis, [(i, (i + 1) % count) for i in range(ends)])
    return from_next, from_prev


def shifted(x, offset, axis):
    n = x.shape[axis]
    return pltpu.roll(x, (-offset) % n, axis)


def transport_kernel(mask_ref, x_ref, o_ref, coef_ref):
    k = diffuse
    c0 = 1.0 - 4.0 * diffuse
    probes = o_ref.shape[0]
    rows = o_ref.shape[2]
    lanes = o_ref.shape[3]
    base = probes
    mask = jnp.broadcast_to(mask_ref[...], x_ref.shape[2:])
    for s in range(STEPS):
        east = 0.5 * (x_ref[0, base + 0] + s * x_ref[0, base + 2])
        north = 0.5 * (x_ref[0, base + 1] + s * x_ref[0, base + 3])
        coef_ref[s, 0] = k - east
        coef_ref[s, 1] = k + east
        coef_ref[s, 2] = k - north
        coef_ref[s, 3] = k + north
        coef_ref[s, 4] = shifted(k - east, -1, 0)
        coef_ref[s, 5] = shifted(k + east, 1, 0)
        coef_ref[s, 6] = shifted(k - north, -1, 1)
        coef_ref[s, 7] = shifted(k + north, 1, 1)

    def one_probe(p, carry):
        f = x_ref[0, p]
        for s in range(STEPS):
            f = (
                c0 * f
                + coef_ref[s, 0] * shifted(f, 1, 0)
                + coef_ref[s, 1] * shifted(f, -1, 0)
                + coef_ref[s, 2] * shifted(f, 1, 1)
                + coef_ref[s, 3] * shifted(f, -1, 1)
            )
            f = f * mask
        f = f * x_ref[0, base + 4]
        for s in reversed(range(STEPS)):
            f = (
                c0 * f
                + coef_ref[s, 4] * shifted(f, -1, 0)
                + coef_ref[s, 5] * shifted(f, 1, 0)
                + coef_ref[s, 6] * shifted(f, -1, 1)
                + coef_ref[s, 7] * shifted(f, 1, 1)
            )
            f = f * mask
        o_ref[p, 0] = f[:rows, :lanes]
        return carry

    lax.fori_loop(0, probes, one_probe, 0)


def transport(mask, stack, probes):
    levels, planes, rows, lanes = stack.shape
    out_rows = rows - 2 * HALO
    out_lanes = 128
    return pl.pallas_call(
        transport_kernel,
        grid=(levels,),
        in_specs=[
            pl.BlockSpec((1, lanes), lambda l: (0, 0)),
            pl.BlockSpec((1, planes, rows, lanes), lambda l: (l, 0, 0, 0)),
        ],
        out_specs=pl.BlockSpec((probes, 1, out_rows, out_lanes), lambda l: (0, l, 0, 0)),
        out_shape=jax.ShapeDtypeStruct((probes, levels, out_rows, out_lanes), jnp.float32),
        scratch_shapes=[pltpu.VMEM((STEPS, 8, rows, lanes), jnp.float32)],
    )(mask, stack)


def body(probes, wind, wind_tend, obs_weight):
    n_probes, levels, width_lon, width_lat = probes.shape
    stack = jnp.concatenate(
        (
            jnp.swapaxes(probes, 0, 1),
            jnp.swapaxes(wind, 0, 1),
            jnp.swapaxes(wind_tend, 0, 1),
            obs_weight[:, None],
        ),
        axis=1,
    )
    lon_next, lon_prev = neighbours(stack, "lon", 2, True)
    stack = jnp.concatenate((stack, lon_next, lon_prev), axis=2)
    lat_in = jnp.swapaxes(stack, 2, 3)
    lat_next, lat_prev = neighbours(lat_in, "lat", 2, False)
    lanes = 256
    gap = jnp.zeros(stack.shape[:3] + (lanes - width_lat - 2 * HALO,), stack.dtype)
    stack = jnp.concatenate(
        (stack, jnp.swapaxes(lat_next, 2, 3), gap, jnp.swapaxes(lat_prev, 2, 3)), axis=3
    )
    lane = lax.broadcasted_iota(jnp.int32, (1, lanes), 1)
    start = lax.axis_index("lat") * width_lat
    cell = jnp.where(lane < width_lat + HALO, start + lane, start + lane - lanes)
    inside = ((lane < width_lat + HALO) | (lane >= lanes - HALO)) & (cell >= 0)
    inside = inside & (cell < width_lat * lax.axis_size("lat"))
    mask = inside.astype(jnp.float32)

    field = transport(mask, stack, n_probes)

    high = lax.Precision.HIGHEST
    flat = field.reshape(field.shape[0], -1)
    gram = lax.psum(jnp.einsum("pc,qc->pq", flat, flat, precision=high), ("lat", "lon"))
    lower = jnp.linalg.cholesky(gram)
    result = jnp.dot(lower_inverse(lower), flat, precision=high)
    upper = lower.T
    cells = field.shape[1] * width_lon * width_lat * lax.axis_size("lat") * lax.axis_size("lon")
    scale = jnp.sqrt(jnp.float32(cells))
    return ((result * scale).reshape(field.shape), upper / scale)


def solution(mesh):
    placed = (
        P(None, None, "lon", "lat"),
        P(None, None, "lon", "lat"),
        P(None, None, "lon", "lat"),
        P(None, "lon", "lat"),
    )
    return jax.shard_map(
        body,
        mesh=mesh,
        in_specs=placed,
        out_specs=(P(None, None, "lon", "lat"), P()),
        check_vma=False,
    )
```

profile of v0, /device:TPU:6, one launch (start us, length us, event | category | flops | bytes accessed | tf_op | source)
XLA Modules:
  0.0 160.0 jit_solution(13409362234087477580)
XLA Ops:
  0.6 0.0 copy-start.1
  0.7 1.4 copy.42
  2.2 6.4 %collective-permute-start = (f32[4,13,8,128]{3,2,1,0:T(8,128)S(1)}, f32[4,13,8,128]{3,2,1,0:T(8,128)S(1)}, u32[]{:S(2)}, u32[]{:S(2)}) collective-permute-start(f32[4,13,8,128]{3,2,1,0:T(8,128)S(1)} %get-tuple-element.8), channel_id=1, source_target_pairs={{1,0},{2,1},{3,2},{4,3},{5,4},{6,5},{7,6},{8,7},{9,8},{10,9},{11,1... | collective-permute-start | bytes 638984 | tf_op jit(solution)/shard_map/ppermute | solution.py:25
  8.6 3.4 %collective-permute-done = f32[4,13,8,128]{3,2,1,0:T(8,128)S(1)} collective-permute-done((f32[4,13,8,128]{3,2,1,0:T(8,128)S(1)}, f32[4,13,8,128]{3,2,1,0:T(8,128)S(1)}, u32[]{:S(2)}, u32[]{:S(2)}) %collective-permute-start) | collective-permute-done | bytes 213024 | tf_op jit(solution)/shard_map/ppermute | solution.py:25
  12.0 4.0 %collective-permute-done.1 = f32[4,13,8,128]{3,2,1,0:T(8,128)S(1)} collective-permute-done((f32[4,13,8,128]{3,2,1,0:T(8,128)S(1)}, f32[4,13,8,128]{3,2,1,0:T(8,128)S(1)}, u32[]{:S(2)}, u32[]{:S(2)}) %collective-permute-start.1) | collective-permute-done | bytes 213024 | tf_op jit(solution)/shard_map/ppermute | solution.py:26
  16.0 0.7 copy-done.3
  16.6 0.2 maximum_bitcast_fusion
  16.8 2.1 %fusion.6 = (f32[4,13,8,80]{2,3,1,0:T(8,128)}, f32[4,13,8,80]{2,3,1,0:T(8,128)S(1)}) fusion(f32[4,13,128,80]{2,3,1,0:T(8,128)S(1)} %maximum_bitcast_fusion), kind=kLoop, calls=%fused_computation.27 | loop fusion | bytes 532480 | tf_op jit(solution)/shard_map/slice | solution.py:23
  18.9 2.9 %copy.19 = f32[4,13,8,80]{3,2,1,0:T(8,128)} copy(f32[4,13,8,80]{2,3,1,0:T(8,128)} %get-tuple-element.6) | data formatting | bytes 266240 | tf_op jit(solution)/shard_map/slice | solution.py:23
  21.7 5.1 %collective-permute-start.2 = (f32[4,13,8,80]{3,2,1,0:T(8,128)}, f32[4,13,8,80]{3,2,1,0:T(8,128)}, u32[]{:S(2)}, u32[]{:S(2)}) collective-permute-start(f32[4,13,8,80]{3,2,1,0:T(8,128)} %copy.19), channel_id=1, source_target_pairs={{32,0},{64,32},{96,64},{128,96},{160,128},{192,160},{224,192},{33,... | collective-permute-start | bytes 399368 | tf_op jit(solution)/shard_map/ppermute | solution.py:25
  26.8 1.3 copy.21
  28.1 2.9 %collective-permute-start.3 = (f32[4,13,8,80]{3,2,1,0:T(8,128)}, f32[4,13,8,80]{3,2,1,0:T(8,128)}, u32[]{:S(2)}, u32[]{:S(2)}) collective-permute-start(f32[4,13,8,80]{3,2,1,0:T(8,128)} %copy.21), channel_id=1, source_target_pairs={{0,32},{32,64},{64,96},{96,128},{128,160},{160,192},{192,224},{1,3... | collective-permute-start | bytes 399368 | tf_op jit(solution)/shard_map/ppermute | solution.py:26
  31.1 0.1 pad.7.clone
  31.1 0.6 and_convert_fusion.mask_ref
  31.7 1.9 %collective-permute-done.2 = f32[4,13,8,80]{3,2,1,0:T(8,128)} collective-permute-done((f32[4,13,8,80]{3,2,1,0:T(8,128)}, f32[4,13,8,80]{3,2,1,0:T(8,128)}, u32[]{:S(2)}, u32[]{:S(2)}) %collective-permute-start.2) | collective-permute-done | bytes 133152 | tf_op jit(solution)/shard_map/ppermute | solution.py:25
  33.6 1.6 copy.20
  35.1 3.4 %collective-permute-done.3 = f32[4,13,8,80]{3,2,1,0:T(8,128)} collective-permute-done((f32[4,13,8,80]{3,2,1,0:T(8,128)}, f32[4,13,8,80]{3,2,1,0:T(8,128)}, u32[]{:S(2)}, u32[]{:S(2)}) %collective-permute-start.3) | collective-permute-done | bytes 133152 | tf_op jit(solution)/shard_map/ppermute | solution.py:26
  38.5 2.9 %copy.22 = f32[4,13,8,80]{2,3,1,0:T(8,128)} copy(f32[4,13,8,80]{3,2,1,0:T(8,128)} %collective-permute-done.3) | data formatting | bytes 266240 | tf_op jit(solution)/shard_map/ppermute | solution.py:26
  41.4 3.8 %pad_maximum_fusion.x_ref = f32[4,13,80,256]{3,2,1,0:T(8,128)} fusion(f32[4,13,80,8]{3,2,1,0:T(8,128)} %bitcast.38, f32[4,13,80,8]{3,2,1,0:T(8,128)S(1)} %bitcast.37, f32[4,13,8,128]{3,2,1,0:T(8,128)} %copy-done.3, f32[4,13,8,128]{3,2,1,0:T(8,128)} %copy-done.2, f32[4,1,64,128]{3,2,1,0:T(8,128)} %bitcast.40, f32[4,2,64,128]{3,2,1,0:T(8,128)S(1)} %get-tuple-element.12, ...), kind=kLoop, calls=%fused_computation.1 | loop fusion | flops 8519680 | bytes 6657024 | tf_op jit(solution)/shard_map/concatenate | solution.py:116
  45.2 29.1 %shard_map.59 = f32[8,4,64,128]{3,2,1,0:T(8,128)} custom-call(f32[1,256]{1,0:T(1,128)} %and_convert_fusion.mask_ref, f32[4,13,80,256]{3,2,1,0:T(8,128)} %pad_maximum_fusion.x_ref), custom_call_target="tpu_custom_call" | custom-call | tf_op jit(solution)/shard_map/pallas_call | solution.py:86
  74.3 4.5 %convolution_bitcast_fusion = f32[8,8]{0,1:T(8,128)S(1)} fusion(f32[8,4,64,128]{3,2,1,0:T(8,128)} %shard_map.59), kind=kOutput, calls=%fused_computation.3 | convolution fusion | flops 25165824 | bytes 1048832 | tf_op jit(solution)/shard_map/pc,qc->pq/dot_general | solution.py:130
  78.8 73.7 %psum.7 = f32[8,8]{0,1:T(8,128)S(1)} all-reduce(f32[8,8]{0,1:T(8,128)S(1)} %convolution_bitcast_fusion), channel_id=1, replica_groups=mesh['lat'=8,'lon'=32] {'lat','lon'}, use_global_device_ids=true, to_apply=%region_0.1 | all-reduce | flops 64 | bytes 512 | tf_op jit(solution)/shard_map/psum | solution.py:130
  152.5 0.1 copy.26
  152.6 0.7 cholesky.17
  153.3 0.1 select_reduce_fusion
  153.4 0.6 compare_reduce_fusion
  154.0 0.6 multiply_bitcast_fusion
  154.7 0.6 custom-call.6
  155.3 0.2 fusion.3
  155.5 2.7 %convolution_multiply_fusion = f32[8,32768]{1,0:T(8,128)S(1)} fusion(f32[8,8]{1,0:T(8,128)S(1)} %fusion.3, f32[1,8,256,128]{3,2,1,0:T(8,128)} %bitcast.36), kind=kOutput, calls=%fused_computation | convolution fusion | flops 25427968 | bytes 2097408 | tf_op jit(solution)/shard_map/dot_general | solution.py:132
  158.2 1.2 copy.28
  159.4 0.7 copy.29
  (15 shorter events, 0.1 us)
Async XLA Ops:
  0.6 1.4 copy-start.5
  0.6 1.4 copy-start.4
  0.6 1.5 copy-start.1
  2.1 13.8 %copy-start = (f32[4,2,64,128]{3,2,1,0:T(8,128)}, f32[4,2,64,128]{3,2,1,0:T(8,128)S(1)}, u32[]{:S(2)}) copy-start(f32[4,2,64,128]{3,2,1,0:T(8,128)S(1)} %get-tuple-element.13) | copy-start | bytes 786436
  2.2 9.8 %collective-permute-start = (f32[4,13,8,128]{3,2,1,0:T(8,128)S(1)}, f32[4,13,8,128]{3,2,1,0:T(8,128)S(1)}, u32[]{:S(2)}, u32[]{:S(2)}) collective-permute-start(f32[4,13,8,128]{3,2,1,0:T(8,128)S(1)} %get-tuple-element.8), channel_id=1, source_target_pairs={{1,0},{2,1},{3,2},{4,3},{5,4},{6,5},{7,6},{8,7},{9,8},{10,9},{11,1... | collective-permute-start | bytes 638984 | tf_op jit(solution)/shard_map/ppermute | solution.py:25
  8.6 7.4 %collective-permute-start.1 = (f32[4,13,8,128]{3,2,1,0:T(8,128)S(1)}, f32[4,13,8,128]{3,2,1,0:T(8,128)S(1)}, u32[]{:S(2)}, u32[]{:S(2)}) collective-permute-start(f32[4,13,8,128]{3,2,1,0:T(8,128)S(1)} %get-tuple-element.9), channel_id=1, source_target_pairs={{0,1},{1,2},{2,3},{3,4},{4,5},{5,6},{6,7},{7,8},{8,9},{9,10},{10,1... | collective-permute-start | bytes 638984 | tf_op jit(solution)/shard_map/ppermute | solution.py:26
  12.0 4.0 %copy-start.2 = (f32[4,13,8,128]{3,2,1,0:T(8,128)}, f32[4,13,8,128]{3,2,1,0:T(8,128)S(1)}, u32[]{:S(2)}) copy-start(f32[4,13,8,128]{3,2,1,0:T(8,128)S(1)} %collective-permute-done) | copy-start | bytes 638980
  16.0 0.7 copy-start.3
  21.7 11.8 %collective-permute-start.2 = (f32[4,13,8,80]{3,2,1,0:T(8,128)}, f32[4,13,8,80]{3,2,1,0:T(8,128)}, u32[]{:S(2)}, u32[]{:S(2)}) collective-permute-start(f32[4,13,8,80]{3,2,1,0:T(8,128)} %copy.19), channel_id=1, source_target_pairs={{32,0},{64,32},{96,64},{128,96},{160,128},{192,160},{224,192},{33,... | collective-permute-start | bytes 399368 | tf_op jit(solution)/shard_map/ppermute | solution.py:25
  28.1 10.4 %collective-permute-start.3 = (f32[4,13,8,80]{3,2,1,0:T(8,128)}, f32[4,13,8,80]{3,2,1,0:T(8,128)}, u32[]{:S(2)}, u32[]{:S(2)}) collective-permute-start(f32[4,13,8,80]{3,2,1,0:T(8,128)} %copy.21), channel_id=1, source_target_pairs={{0,32},{32,64},{64,96},{96,128},{128,160},{160,192},{192,224},{1,3... | collective-permute-start | bytes 399368 | tf_op jit(solution)/shard_map/ppermute | solution.py:26
where the time goes:
time: 162 us; the launch traced here: 160 us
  blocking collectives  73.7 us (45%)
  Pallas kernels  29.1 us (18%)
  local copies, waits for them, and re-layouts  14.8 us (9%)
  starting transfers between devices  14.4 us (9%)
  waiting for transfers between devices  12.7 us (8%)
  matrix products  7.42 us (5%)
  other arithmetic  7.25 us (4%)
    psum x1, blocking collectives, body(): lax.psum(jnp.einsum('pc,qc->pq', flat, flat, precision=high), ('lat', 'lo...  73.7 us
    pallas_call x1, Pallas kernels, transport(): pl.pallas_call(transport_kernel, grid=(levels,), in_specs=[pl.BlockSpec((...  29.1 us
    ppermute x2, starting transfers between devices, neighbours(): lax.ppermute(head, axis, [((i + 1) % count, i) for i in range(ends)])  11.4 us
    ppermute x2, waiting for transfers between devices, neighbours(): lax.ppermute(tail, axis, [(i, (i + 1) % count) for i in range(ends)])  7.38 us
    ppermute x2, waiting for transfers between devices, neighbours(): lax.ppermute(head, axis, [((i + 1) % count, i) for i in range(ends)])  5.27 us
    slice x2, local copies, waits for them, and re-layouts, neighbours(): head = lax.slice_in_dim(cells, 0, HALO, axis=dim)  4.93 us
    dot_general x1, matrix products, body(): jnp.einsum('pc,qc->pq', flat, flat, precision=high)  4.51 us
    unnamed x15, local copies, waits for them, and re-layouts  3.91 us
  transfers between devices with their start and end apart: 4, of which 4 were waited for; matrix products, arithmetic and copies ran while one was open for 2% of the time, Pallas kernels for 0%

commit v1 on v0

--- a/solution.py
+++ b/solution.py
@@ -14,6 +14,19 @@
 def lower_inverse(lower):
     eye = jnp.eye(lower.shape[0], dtype=lower.dtype)
     return lax.linalg.triangular_solve(lower, eye, left_side=True, lower=True)
+
+
+def all_sum(value, axes):
+    for axis in axes:
+        count = lax.axis_size(axis)
+        if count & (count - 1):
+            value = lax.psum(value, axis)
+            continue
+        stride = 1
+        while stride < count:
+            value = value + lax.ppermute(value, axis, [(i, i ^ stride) for i in range(count)])
+            stride *= 2
+    return value
 
 
 def neighbours(cells, axis, dim, closed):
@@ -127,7 +140,7 @@
 
     high = lax.Precision.HIGHEST
     flat = field.reshape(field.shape[0], -1)
-    gram = lax.psum(jnp.einsum("pc,qc->pq", flat, flat, precision=high), ("lat", "lon"))
+    gram = all_sum(jnp.einsum("pc,qc->pq", flat, flat, precision=high), ("lon", "lat"))
     lower = jnp.linalg.cholesky(gram)
     result = jnp.dot(lower_inverse(lower), flat, precision=high)
     upper = lower.T

time: 162 us -> 121 us (0.75)
  blocking collectives: 73.7 us -> 0 us
  waiting for transfers between devices: 12.7 us -> 43.1 us
  starting transfers between devices: 14.4 us -> 18.2 us
    psum x1 -> x0, blocking collectives: 73.7 us -> none  [body(): lax.psum(jnp.einsum('pc,qc->pq', flat, flat, precision=high), ('lat', 'lo...]
    ppermute x0 -> x8, waiting for transfers between devices: none -> 30.4 us  [all_sum(): lax.ppermute(value, axis, [(i, i ^ stride) for i in range(count)])]
    ppermute x0 -> x8, starting transfers between devices: none -> 3.82 us  [all_sum(): lax.ppermute(value, axis, [(i, i ^ stride) for i in range(count)])]
  transfers between devices with their start and end apart: 4 -> 12, of which waited for: 4 -> 12; matrix products, arithmetic and copies ran while one was open for 2% -> 3% of each run, Pallas kernels for 0% -> 0%
where the time goes in v1:
time: 121 us
  waiting for transfers between devices  43.1 us (36%)
  Pallas kernels  29.1 us (24%)
  starting transfers between devices  18.2 us (15%)
  local copies, waits for them, and re-layouts  14.8 us (12%)
  matrix products  7.42 us (6%)
  other arithmetic  7.28 us (6%)
    ppermute x8, waiting for transfers between devices, all_sum(): lax.ppermute(value, axis, [(i, i ^ stride) for i in range(count)])  30.4 us
    pallas_call x1, Pallas kernels, transport(): pl.pallas_call(transport_kernel, grid=(levels,), in_specs=[pl.BlockSpec((...  29.1 us
    ppermute x2, starting transfers between devices, neighbours(): lax.ppermute(head, axis, [((i + 1) % count, i) for i in range(ends)])  11.4 us
    ppermute x2, waiting for transfers between devices, neighbours(): lax.ppermute(tail, axis, [(i, (i + 1) % count) for i in range(ends)])  7.38 us
    ppermute x2, waiting for transfers between devices, neighbours(): lax.ppermute(head, axis, [((i + 1) % count, i) for i in range(ends)])  5.28 us
    slice x2, local copies, waits for them, and re-layouts, neighbours(): head = lax.slice_in_dim(cells, 0, HALO, axis=dim)  4.93 us
    dot_general x1, matrix products, body(): jnp.einsum('pc,qc->pq', flat, flat, precision=high)  4.51 us
    unnamed x15, local copies, waits for them, and re-layouts  3.89 us
  transfers between devices with their start and end apart: 12, of which 12 were waited for; matrix products, arithmetic and copies ran while one was open for 3% of the time, Pallas kernels for 0%

profile of v1, /device:TPU:6, one launch (start us, length us, event | category | flops | bytes accessed | tf_op | source)
XLA Modules:
  0.0 120.6 jit_solution(1382651142416383935)
XLA Ops:
  0.7 1.4 %copy.45 = f32[8,4,64,128]{3,2,0,1:T(8,128)S(1)} copy(f32[8,4,64,128]{3,2,1,0:T(8,128)} %param.4) | data formatting | bytes 2097152 | tf_op args[0]
  2.1 6.4 %collective-permute-start = (f32[4,13,8,128]{3,2,1,0:T(8,128)S(1)}, f32[4,13,8,128]{3,2,1,0:T(8,128)S(1)}, u32[]{:S(2)}, u32[]{:S(2)}) collective-permute-start(f32[4,13,8,128]{3,2,1,0:T(8,128)S(1)} %get-tuple-element.8), channel_id=1, source_target_pairs={{1,0},{2,1},{3,2},{4,3},{5,4},{6,5},{7,6},{8,7},{9,8},{10,9},{11,1... | collective-permute-start | bytes 638984 | tf_op jit(solution)/shard_map/ppermute | solution.py:38
  8.5 3.4 %collective-permute-done = f32[4,13,8,128]{3,2,1,0:T(8,128)S(1)} collective-permute-done((f32[4,13,8,128]{3,2,1,0:T(8,128)S(1)}, f32[4,13,8,128]{3,2,1,0:T(8,128)S(1)}, u32[]{:S(2)}, u32[]{:S(2)}) %collective-permute-start) | collective-permute-done | bytes 213024 | tf_op jit(solution)/shard_map/ppermute | solution.py:38
  11.9 4.0 %collective-permute-done.1 = f32[4,13,8,128]{3,2,1,0:T(8,128)S(1)} collective-permute-done((f32[4,13,8,128]{3,2,1,0:T(8,128)S(1)}, f32[4,13,8,128]{3,2,1,0:T(8,128)S(1)}, u32[]{:S(2)}, u32[]{:S(2)}) %collective-permute-start.1) | collective-permute-done | bytes 213024 | tf_op jit(solution)/shard_map/ppermute | solution.py:39
  15.9 0.7 copy-done.3
  16.8 2.0 %fusion.6 = (f32[4,13,8,80]{2,3,1,0:T(8,128)}, f32[4,13,8,80]{2,3,1,0:T(8,128)S(1)}) fusion(f32[4,13,128,80]{2,3,1,0:T(8,128)S(1)} %maximum_bitcast_fusion), kind=kLoop, calls=%fused_computation.27 | loop fusion | bytes 532480 | tf_op jit(solution)/shard_map/slice | solution.py:36
  18.8 2.9 %copy.20 = f32[4,13,8,80]{3,2,1,0:T(8,128)} copy(f32[4,13,8,80]{2,3,1,0:T(8,128)} %get-tuple-element.6) | data formatting | bytes 266240 | tf_op jit(solution)/shard_map/slice | solution.py:36
  21.7 5.1 %collective-permute-start.2 = (f32[4,13,8,80]{3,2,1,0:T(8,128)}, f32[4,13,8,80]{3,2,1,0:T(8,128)}, u32[]{:S(2)}, u32[]{:S(2)}) collective-permute-start(f32[4,13,8,80]{3,2,1,0:T(8,128)} %copy.20), channel_id=1, source_target_pairs={{32,0},{64,32},{96,64},{128,96},{160,128},{192,160},{224,192},{33,... | collective-permute-start | bytes 399368 | tf_op jit(solution)/shard_map/ppermute | solution.py:38
  26.8 1.3 %copy.22 = f32[4,13,8,80]{3,2,1,0:T(8,128)} copy(f32[4,13,8,80]{2,3,1,0:T(8,128)S(1)} %get-tuple-element.7) | data formatting | bytes 266240 | tf_op jit(solution)/shard_map/slice | solution.py:37
  28.1 2.9 %collective-permute-start.3 = (f32[4,13,8,80]{3,2,1,0:T(8,128)}, f32[4,13,8,80]{3,2,1,0:T(8,128)}, u32[]{:S(2)}, u32[]{:S(2)}) collective-permute-start(f32[4,13,8,80]{3,2,1,0:T(8,128)} %copy.22), channel_id=1, source_target_pairs={{0,32},{32,64},{64,96},{96,128},{128,160},{160,192},{192,224},{1,3... | collective-permute-start | bytes 399368 | tf_op jit(solution)/shard_map/ppermute | solution.py:39
  31.7 1.9 %collective-permute-done.2 = f32[4,13,8,80]{3,2,1,0:T(8,128)} collective-permute-done((f32[4,13,8,80]{3,2,1,0:T(8,128)}, f32[4,13,8,80]{3,2,1,0:T(8,128)}, u32[]{:S(2)}, u32[]{:S(2)}) %collective-permute-start.2) | collective-permute-done | bytes 133152 | tf_op jit(solution)/shard_map/ppermute | solution.py:38
  33.5 1.6 %copy.21 = f32[4,13,8,80]{2,3,1,0:T(8,128)S(1)} copy(f32[4,13,8,80]{3,2,1,0:T(8,128)} %collective-permute-done.2) | data formatting | bytes 266240 | tf_op jit(solution)/shard_map/ppermute | solution.py:38
  35.1 3.4 %collective-permute-done.3 = f32[4,13,8,80]{3,2,1,0:T(8,128)} collective-permute-done((f32[4,13,8,80]{3,2,1,0:T(8,128)}, f32[4,13,8,80]{3,2,1,0:T(8,128)}, u32[]{:S(2)}, u32[]{:S(2)}) %collective-permute-start.3) | collective-permute-done | bytes 133152 | tf_op jit(solution)/shard_map/ppermute | solution.py:39
  38.5 2.9 %copy.23 = f32[4,13,8,80]{2,3,1,0:T(8,128)} copy(f32[4,13,8,80]{3,2,1,0:T(8,128)} %collective-permute-done.3) | data formatting | bytes 266240 | tf_op jit(solution)/shard_map/ppermute | solution.py:39
  41.4 3.8 %pad_maximum_fusion.x_ref = f32[4,13,80,256]{3,2,1,0:T(8,128)} fusion(f32[4,13,80,8]{3,2,1,0:T(8,128)} %bitcast.40, f32[4,13,80,8]{3,2,1,0:T(8,128)S(1)} %bitcast.39, f32[4,13,8,128]{3,2,1,0:T(8,128)} %copy-done.3, f32[4,13,8,128]{3,2,1,0:T(8,128)} %copy-done.2, f32[4,1,64,128]{3,2,1,0:T(8,128)} %bitcast.42, f32[4,2,64,128]{3,2,1,0:T(8,128)S(1)} %get-tuple-element.12, ...), kind=kLoop, calls=%fused_computation.1 | loop fusion | flops 8519680 | bytes 6657024 | tf_op jit(solution)/shard_map/concatenate | solution.py:129
  45.2 29.1 %shard_map.59 = f32[8,4,64,128]{3,2,1,0:T(8,128)} custom-call(f32[1,256]{1,0:T(1,128)} %and_convert_fusion.mask_ref, f32[4,13,80,256]{3,2,1,0:T(8,128)} %pad_maximum_fusion.x_ref), custom_call_target="tpu_custom_call" | custom-call | tf_op jit(solution)/shard_map/pallas_call | solution.py:99
  74.3 4.5 %convolution_bitcast_fusion = f32[8,8]{0,1:T(8,128)S(1)} fusion(f32[8,4,64,128]{3,2,1,0:T(8,128)} %shard_map.59), kind=kOutput, calls=%fused_computation.3 | convolution fusion | flops 25165824 | bytes 1048832 | tf_op jit(solution)/shard_map/pc,qc->pq/dot_general | solution.py:143
  78.8 1.2 collective-permute-done.4
  80.0 3.6 %collective-permute-done.5 = f32[8,8]{0,1:T(8,128)S(1)} collective-permute-done((f32[8,8]{0,1:T(8,128)S(1)}, f32[8,8]{0,1:T(8,128)S(1)}, u32[]{:S(2)}, u32[]{:S(2)}) %collective-permute-start.5) | collective-permute-done | bytes 288 | tf_op jit(solution)/shard_map/ppermute | solution.py:27
  83.6 3.6 %collective-permute-done.6 = f32[8,8]{0,1:T(8,128)S(1)} collective-permute-done((f32[8,8]{0,1:T(8,128)S(1)}, f32[8,8]{0,1:T(8,128)S(1)}, u32[]{:S(2)}, u32[]{:S(2)}) %collective-permute-start.6) | collective-permute-done | bytes 288 | tf_op jit(solution)/shard_map/ppermute | solution.py:27
  87.2 4.5 %collective-permute-done.7 = f32[8,8]{0,1:T(8,128)S(1)} collective-permute-done((f32[8,8]{0,1:T(8,128)S(1)}, f32[8,8]{0,1:T(8,128)S(1)}, u32[]{:S(2)}, u32[]{:S(2)}) %collective-permute-start.7) | collective-permute-done | bytes 288 | tf_op jit(solution)/shard_map/ppermute | solution.py:27
  91.8 2.0 %collective-permute-start.8 = (f32[8,8]{0,1:T(8,128)S(1)}, f32[8,8]{0,1:T(8,128)S(1)}, u32[]{:S(2)}, u32[]{:S(2)}) collective-permute-start(f32[8,8]{0,1:T(8,128)S(1)} %add.65), channel_id=1, source_target_pairs={{0,16},{1,17},{2,18},{3,19},{4,20},{5,21},{6,22},{7,23},{8,24},{9,... | collective-permute-start | bytes 776 | tf_op jit(solution)/shard_map/ppermute | solution.py:27
  93.8 5.5 %collective-permute-done.8 = f32[8,8]{0,1:T(8,128)S(1)} collective-permute-done((f32[8,8]{0,1:T(8,128)S(1)}, f32[8,8]{0,1:T(8,128)S(1)}, u32[]{:S(2)}, u32[]{:S(2)}) %collective-permute-start.8) | collective-permute-done | bytes 288 | tf_op jit(solution)/shard_map/ppermute | solution.py:27
  99.4 5.0 %collective-permute-done.9 = f32[8,8]{0,1:T(8,128)S(1)} collective-permute-done((f32[8,8]{0,1:T(8,128)S(1)}, f32[8,8]{0,1:T(8,128)S(1)}, u32[]{:S(2)}, u32[]{:S(2)}) %collective-permute-start.9) | collective-permute-done | bytes 288 | tf_op jit(solution)/shard_map/ppermute | solution.py:27
  104.9 3.1 %collective-permute-done.10 = f32[8,8]{0,1:T(8,128)S(1)} collective-permute-done((f32[8,8]{0,1:T(8,128)S(1)}, f32[8,8]{0,1:T(8,128)S(1)}, u32[]{:S(2)}, u32[]{:S(2)}) %collective-permute-start.10) | collective-permute-done | bytes 288 | tf_op jit(solution)/shard_map/ppermute | solution.py:27
  108.0 1.1 collective-permute-start.11
  109.1 4.0 %collective-permute-done.11 = f32[8,8]{0,1:T(8,128)S(1)} collective-permute-done((f32[8,8]{0,1:T(8,128)S(1)}, f32[8,8]{0,1:T(8,128)S(1)}, u32[]{:S(2)}, u32[]{:S(2)}) %collective-permute-start.11) | collective-permute-done | bytes 288 | tf_op jit(solution)/shard_map/ppermute | solution.py:27
  113.2 0.7 cholesky.17
  114.6 0.6 multiply_bitcast_fusion
  116.1 2.7 %convolution_multiply_fusion = f32[8,32768]{1,0:T(8,128)S(1)} fusion(f32[8,8]{1,0:T(8,128)S(1)} %fusion.3, f32[1,8,256,128]{3,2,1,0:T(8,128)} %bitcast.38), kind=kOutput, calls=%fused_computation | convolution fusion | flops 25427968 | bytes 2097408 | tf_op jit(solution)/shard_map/dot_general | solution.py:145
  118.8 1.2 copy.30
  120.0 0.7 copy.31
  (38 shorter events, 3.2 us)
Async XLA Ops:
  0.6 1.4 %copy-start.5 = (f32[2,4,64,128]{3,2,1,0:T(8,128)S(1)}, f32[2,4,64,128]{3,2,1,0:T(8,128)}, u32[]{:S(2)}) copy-start(f32[2,4,64,128]{3,2,1,0:T(8,128)} %param.5) | copy-start | bytes 786436
  0.6 1.4 %copy-start.4 = (f32[2,4,64,128]{3,2,1,0:T(8,128)S(1)}, f32[2,4,64,128]{3,2,1,0:T(8,128)}, u32[]{:S(2)}) copy-start(f32[2,4,64,128]{3,2,1,0:T(8,128)} %param.6) | copy-start | bytes 786436
  0.6 1.4 %copy-start.1 = (f32[4,64,128]{2,1,0:T(8,128)S(1)}, f32[4,64,128]{2,1,0:T(8,128)}, u32[]{:S(2)}) copy-start(f32[4,64,128]{2,1,0:T(8,128)} %param.7) | copy-start | bytes 393220
  2.1 13.8 %copy-start = (f32[4,2,64,128]{3,2,1,0:T(8,128)}, f32[4,2,64,128]{3,2,1,0:T(8,128)S(1)}, u32[]{:S(2)}) copy-start(f32[4,2,64,128]{3,2,1,0:T(8,128)S(1)} %get-tuple-element.13) | copy-start | bytes 786436
  2.1 9.8 %collective-permute-start = (f32[4,13,8,128]{3,2,1,0:T(8,128)S(1)}, f32[4,13,8,128]{3,2,1,0:T(8,128)S(1)}, u32[]{:S(2)}, u32[]{:S(2)}) collective-permute-start(f32[4,13,8,128]{3,2,1,0:T(8,128)S(1)} %get-tuple-element.8), channel_id=1, source_target_pairs={{1,0},{2,1},{3,2},{4,3},{5,4},{6,5},{7,6},{8,7},{9,8},{10,9},{11,1... | collective-permute-start | bytes 638984 | tf_op jit(solution)/shard_map/ppermute | solution.py:38
  8.5 7.4 %collective-permute-start.1 = (f32[4,13,8,128]{3,2,1,0:T(8,128)S(1)}, f32[4,13,8,128]{3,2,1,0:T(8,128)S(1)}, u32[]{:S(2)}, u32[]{:S(2)}) collective-permute-start(f32[4,13,8,128]{3,2,1,0:T(8,128)S(1)} %get-tuple-element.9), channel_id=1, source_target_pairs={{0,1},{1,2},{2,3},{3,4},{4,5},{5,6},{6,7},{7,8},{8,9},{9,10},{10,1... | collective-permute-start | bytes 638984 | tf_op jit(solution)/shard_map/ppermute | solution.py:39
  11.9 4.0 %copy-start.2 = (f32[4,13,8,128]{3,2,1,0:T(8,128)}, f32[4,13,8,128]{3,2,1,0:T(8,128)S(1)}, u32[]{:S(2)}) copy-start(f32[4,13,8,128]{3,2,1,0:T(8,128)S(1)} %collective-permute-done) | copy-start | bytes 638980
  15.9 0.7 copy-start.3
  21.7 11.8 %collective-permute-start.2 = (f32[4,13,8,80]{3,2,1,0:T(8,128)}, f32[4,13,8,80]{3,2,1,0:T(8,128)}, u32[]{:S(2)}, u32[]{:S(2)}) collective-permute-start(f32[4,13,8,80]{3,2,1,0:T(8,128)} %copy.20), channel_id=1, source_target_pairs={{32,0},{64,32},{96,64},{128,96},{160,128},{192,160},{224,192},{33,... | collective-permute-start | bytes 399368 | tf_op jit(solution)/shard_map/ppermute | solution.py:38
  28.1 10.4 %collective-permute-start.3 = (f32[4,13,8,80]{3,2,1,0:T(8,128)}, f32[4,13,8,80]{3,2,1,0:T(8,128)}, u32[]{:S(2)}, u32[]{:S(2)}) collective-permute-start(f32[4,13,8,80]{3,2,1,0:T(8,128)} %copy.22), channel_id=1, source_target_pairs={{0,32},{32,64},{64,96},{96,128},{128,160},{160,192},{192,224},{1,3... | collective-permute-start | bytes 399368 | tf_op jit(solution)/shard_map/ppermute | solution.py:39
  78.8 1.2 collective-permute-start.4
  80.0 3.6 %collective-permute-start.5 = (f32[8,8]{0,1:T(8,128)S(1)}, f32[8,8]{0,1:T(8,128)S(1)}, u32[]{:S(2)}, u32[]{:S(2)}) collective-permute-start(f32[8,8]{0,1:T(8,128)S(1)} %add.62), channel_id=1, source_target_pairs={{0,2},{1,3},{2,0},{3,1},{4,6},{5,7},{6,4},{7,5},{8,10},{9,11},{10,... | collective-permute-start | bytes 776 | tf_op jit(solution)/shard_map/ppermute | solution.py:27
  83.6 3.6 %collective-permute-start.6 = (f32[8,8]{0,1:T(8,128)S(1)}, f32[8,8]{0,1:T(8,128)S(1)}, u32[]{:S(2)}, u32[]{:S(2)}) collective-permute-start(f32[8,8]{0,1:T(8,128)S(1)} %add.63), channel_id=1, source_target_pairs={{0,4},{1,5},{2,6},{3,7},{4,0},{5,1},{6,2},{7,3},{8,12},{9,13},{10,... | collective-permute-start | bytes 776 | tf_op jit(solution)/shard_map/ppermute | solution.py:27
  87.2 4.5 %collective-permute-start.7 = (f32[8,8]{0,1:T(8,128)S(1)}, f32[8,8]{0,1:T(8,128)S(1)}, u32[]{:S(2)}, u32[]{:S(2)}) collective-permute-start(f32[8,8]{0,1:T(8,128)S(1)} %add.64), channel_id=1, source_target_pairs={{0,8},{1,9},{2,10},{3,11},{4,12},{5,13},{6,14},{7,15},{8,0},{9,1},... | collective-permute-start | bytes 776 | tf_op jit(solution)/shard_map/ppermute | solution.py:27
  91.8 7.5 %collective-permute-start.8 = (f32[8,8]{0,1:T(8,128)S(1)}, f32[8,8]{0,1:T(8,128)S(1)}, u32[]{:S(2)}, u32[]{:S(2)}) collective-permute-start(f32[8,8]{0,1:T(8,128)S(1)} %add.65), channel_id=1, source_target_pairs={{0,16},{1,17},{2,18},{3,19},{4,20},{5,21},{6,22},{7,23},{8,24},{9,... | collective-permute-start | bytes 776 | tf_op jit(solution)/shard_map/ppermute | solution.py:27
  99.3 5.1 %collective-permute-start.9 = (f32[8,8]{0,1:T(8,128)S(1)}, f32[8,8]{0,1:T(8,128)S(1)}, u32[]{:S(2)}, u32[]{:S(2)}) collective-permute-start(f32[8,8]{0,1:T(8,128)S(1)} %add.66), channel_id=1, source_target_pairs={{0,32},{32,0},{64,96},{96,64},{128,160},{160,128},{192,224},{224,1... | collective-permute-start | bytes 776 | tf_op jit(solution)/shard_map/ppermute | solution.py:27
  104.4 3.6 %collective-permute-start.10 = (f32[8,8]{0,1:T(8,128)S(1)}, f32[8,8]{0,1:T(8,128)S(1)}, u32[]{:S(2)}, u32[]{:S(2)}) collective-permute-start(f32[8,8]{0,1:T(8,128)S(1)} %add.67), channel_id=1, source_target_pairs={{0,64},{32,96},{64,0},{96,32},{128,192},{160,224},{192,128},{224,1... | collective-permute-start | bytes 776 | tf_op jit(solution)/shard_map/ppermute | solution.py:27
  108.0 5.1 %collective-permute-start.11 = (f32[8,8]{0,1:T(8,128)S(1)}, f32[8,8]{0,1:T(8,128)S(1)}, u32[]{:S(2)}, u32[]{:S(2)}) collective-permute-start(f32[8,8]{0,1:T(8,128)S(1)} %add.68), channel_id=1, source_target_pairs={{0,128},{32,160},{64,192},{96,224},{128,0},{160,32},{192,64},{224,... | collective-permute-start | bytes 776 | tf_op jit(solution)/shard_map/ppermute | solution.py:27

commit v2 on v1

--- a/solution.py
+++ b/solution.py
@@ -45,7 +45,7 @@
     return pltpu.roll(x, (-offset) % n, axis)
 
 
-def transport_kernel(mask_ref, x_ref, o_ref, coef_ref):
+def transport_kernel(mask_ref, x_ref, o_ref, g_ref, coef_ref):
     k = diffuse
     c0 = 1.0 - 4.0 * diffuse
     probes = o_ref.shape[0]
@@ -90,6 +90,13 @@
         return carry
 
     lax.fori_loop(0, probes, one_probe, 0)
+    for p in range(probes):
+        for q in range(p, probes):
+            prod = (o_ref[p, 0] * o_ref[q, 0]).reshape(rows // 8, 8, lanes)
+            part = jnp.sum(jnp.sum(prod, axis=0), axis=0, keepdims=True)
+            g_ref[0, pl.ds(p * probes + q, 1), :] = part
+            if q != p:
+                g_ref[0, pl.ds(q * probes + p, 1), :] = part
 
 
 def transport(mask, stack, probes):
@@ -103,10 +110,42 @@
             pl.BlockSpec((1, lanes), lambda l: (0, 0)),
             pl.BlockSpec((1, planes, rows, lanes), lambda l: (l, 0, 0, 0)),
         ],
-        out_specs=pl.BlockSpec((probes, 1, out_rows, out_lanes), lambda l: (0, l, 0, 0)),
-        out_shape=jax.ShapeDtypeStruct((probes, levels, out_rows, out_lanes), jnp.float32),
+        out_specs=[
+            pl.BlockSpec((probes, 1, out_rows, out_lanes), lambda l: (0, l, 0, 0)),
+            pl.BlockSpec((1, probes * probes, out_lanes), lambda l: (l, 0, 0)),
+        ],
+        out_shape=[
+            jax.ShapeDtypeStruct((probes, levels, out_rows, out_lanes), jnp.float32),
+            jax.ShapeDtypeStruct((levels, probes * probes, out_lanes), jnp.float32),
+        ],
         scratch_shapes=[pltpu.VMEM((STEPS, 8, rows, lanes), jnp.float32)],
     )(mask, stack)
+
+
+def basis_kernel(inv_ref, scale_ref, z_ref, o_ref):
+    probes = z_ref.shape[0]
+    z = [z_ref[q, 0] for q in range(probes)]
+    for p in range(probes):
+        acc = inv_ref[p, 0] * z[0]
+        for q in range(1, probes):
+            acc = acc + inv_ref[p, q] * z[q]
+        o_ref[p, 0] = acc * scale_ref[0, 0]
+
+
+def basis(inverse, scale, field):
+    probes, levels, rows, lanes = field.shape
+    block = pl.BlockSpec((probes, 1, rows, lanes), lambda l: (0, l, 0, 0))
+    return pl.pallas_call(
+        basis_kernel,
+        grid=(levels,),
+        in_specs=[
+            pl.BlockSpec(memory_space=pltpu.SMEM),
+            pl.BlockSpec(memory_space=pltpu.SMEM),
+            block,
+        ],
+        out_specs=block,
+        out_shape=jax.ShapeDtypeStruct(field.shape, jnp.float32),
+    )(inverse, scale, field)
 
 
 def body(probes, wind, wind_tend, obs_weight):
@@ -136,17 +175,16 @@
     inside = inside & (cell < width_lat * lax.axis_size("lat"))
     mask = inside.astype(jnp.float32)
 
-    field = transport(mask, stack, n_probes)
-
-    high = lax.Precision.HIGHEST
-    flat = field.reshape(field.shape[0], -1)
-    gram = all_sum(jnp.einsum("pc,qc->pq", flat, flat, precision=high), ("lon", "lat"))
+    field, partial = transport(mask, stack, n_probes)
+
+    gram = jnp.sum(partial, axis=(0, 2)).reshape(n_probes, n_probes)
+    gram = all_sum(gram, ("lon", "lat"))
     lower = jnp.linalg.cholesky(gram)
-    result = jnp.dot(lower_inverse(lower), flat, precision=high)
     upper = lower.T
     cells = field.shape[1] * width_lon * width_lat * lax.axis_size("lat") * lax.axis_size("lon")
     scale = jnp.sqrt(jnp.float32(cells))
-    return ((result * scale).reshape(field.shape), upper / scale)
+    result = basis(lower_inverse(lower), scale.reshape(1, 1), field)
+    return (result, upper / scale)
 
 
 def solution(mesh):

time: 121 us -> 118 us (0.975)
  matrix products: 7.42 us -> 0.79 us
  Pallas kernels: 29.1 us -> 33.2 us
    dot_general x2 -> x0, matrix products: 7.24 us -> none  [the longest x1 4.51 us: body(): jnp.einsum('pc,qc->pq', flat, flat, precision=high)]
    pallas_call x0 -> x1, Pallas kernels: none -> 3.66 us  [basis(): pl.pallas_call(basis_kernel, grid=(levels,), in_specs=[pl.BlockSpec(memor...]
    unnamed x15 -> x14, local copies, waits for them, and re-layouts: 3.89 us -> 2.72 us
where the time goes in v2:
time: 118 us
  waiting for transfers between devices  43.1 us (37%)
  Pallas kernels  33.2 us (28%)
  starting transfers between devices  18.2 us (15%)
  local copies, waits for them, and re-layouts  13.7 us (12%)
  other arithmetic  8.3 us (7%)
    ppermute x8, waiting for transfers between devices, all_sum(): lax.ppermute(value, axis, [(i, i ^ stride) for i in range(count)])  30.4 us
    pallas_call x1, Pallas kernels, transport(): pl.pallas_call(transport_kernel, grid=(levels,), in_specs=[pl.BlockSpec((...  29.5 us
    ppermute x2, starting transfers between devices, neighbours(): lax.ppermute(head, axis, [((i + 1) % count, i) for i in range(ends)])  11.4 us
    ppermute x2, waiting for transfers between devices, neighbours(): lax.ppermute(tail, axis, [(i, (i + 1) % count) for i in range(ends)])  7.38 us
    ppermute x2, waiting for transfers between devices, neighbours(): lax.ppermute(head, axis, [((i + 1) % count, i) for i in range(ends)])  5.28 us
    slice x2, local copies, waits for them, and re-layouts, neighbours(): head = lax.slice_in_dim(cells, 0, HALO, axis=dim)  4.91 us
    concatenate x1, other arithmetic, body(): jnp.concatenate((stack, jnp.swapaxes(lat_next, 2, 3), gap, jnp.swapaxes(l...  3.81 us
    ppermute x8, starting transfers between devices, all_sum(): lax.ppermute(value, axis, [(i, i ^ stride) for i in range(count)])  3.8 us
  transfers between devices with their start and end apart: 12, of which 12 were waited for; matrix products, arithmetic and copies ran while one was open for 3% of the time, Pallas kernels for 0%

profile of v2, /device:TPU:6, one launch (start us, length us, event | category | flops | bytes accessed | tf_op | source)
XLA Modules:
  0.0 118.1 jit_solution(11478204811709605668)
XLA Ops:
  0.7 1.4 %copy.29 = f32[8,4,64,128]{3,2,0,1:T(8,128)S(1)} copy(f32[8,4,64,128]{3,2,1,0:T(8,128)} %param.4) | data formatting | bytes 2097152 | tf_op args[0]
  2.1 6.4 %collective-permute-start = (f32[4,13,8,128]{3,2,1,0:T(8,128)S(1)}, f32[4,13,8,128]{3,2,1,0:T(8,128)S(1)}, u32[]{:S(2)}, u32[]{:S(2)}) collective-permute-start(f32[4,13,8,128]{3,2,1,0:T(8,128)S(1)} %get-tuple-element.12), channel_id=1, source_target_pairs={{1,0},{2,1},{3,2},{4,3},{5,4},{6,5},{7,6},{8,7},{9,8},{10,9},{11,1... | collective-permute-start | bytes 638984 | tf_op jit(solution)/shard_map/ppermute | solution.py:38
  8.5 3.4 %collective-permute-done = f32[4,13,8,128]{3,2,1,0:T(8,128)S(1)} collective-permute-done((f32[4,13,8,128]{3,2,1,0:T(8,128)S(1)}, f32[4,13,8,128]{3,2,1,0:T(8,128)S(1)}, u32[]{:S(2)}, u32[]{:S(2)}) %collective-permute-start) | collective-permute-done | bytes 213024 | tf_op jit(solution)/shard_map/ppermute | solution.py:38
  11.9 4.0 %collective-permute-done.1 = f32[4,13,8,128]{3,2,1,0:T(8,128)S(1)} collective-permute-done((f32[4,13,8,128]{3,2,1,0:T(8,128)S(1)}, f32[4,13,8,128]{3,2,1,0:T(8,128)S(1)}, u32[]{:S(2)}, u32[]{:S(2)}) %collective-permute-start.1) | collective-permute-done | bytes 213024 | tf_op jit(solution)/shard_map/ppermute | solution.py:39
  15.9 0.7 copy-done.3
  16.8 2.0 %fusion.3 = (f32[4,13,8,80]{2,3,1,0:T(8,128)}, f32[4,13,8,80]{2,3,1,0:T(8,128)S(1)}) fusion(f32[4,13,128,80]{2,3,1,0:T(8,128)S(1)} %maximum_bitcast_fusion), kind=kLoop, calls=%fused_computation.22 | loop fusion | bytes 532480 | tf_op jit(solution)/shard_map/slice | solution.py:36
  18.8 2.9 %copy.17 = f32[4,13,8,80]{3,2,1,0:T(8,128)} copy(f32[4,13,8,80]{2,3,1,0:T(8,128)} %get-tuple-element.10) | data formatting | bytes 266240 | tf_op jit(solution)/shard_map/slice | solution.py:36
  21.7 5.1 %collective-permute-start.2 = (f32[4,13,8,80]{3,2,1,0:T(8,128)}, f32[4,13,8,80]{3,2,1,0:T(8,128)}, u32[]{:S(2)}, u32[]{:S(2)}) collective-permute-start(f32[4,13,8,80]{3,2,1,0:T(8,128)} %copy.17), channel_id=1, source_target_pairs={{32,0},{64,32},{96,64},{128,96},{160,128},{192,160},{224,192},{33,... | collective-permute-start | bytes 399368 | tf_op jit(solution)/shard_map/ppermute | solution.py:38
  26.8 1.3 %copy.19 = f32[4,13,8,80]{3,2,1,0:T(8,128)} copy(f32[4,13,8,80]{2,3,1,0:T(8,128)S(1)} %get-tuple-element.11) | data formatting | bytes 266240 | tf_op jit(solution)/shard_map/slice | solution.py:37
  28.1 2.9 %collective-permute-start.3 = (f32[4,13,8,80]{3,2,1,0:T(8,128)}, f32[4,13,8,80]{3,2,1,0:T(8,128)}, u32[]{:S(2)}, u32[]{:S(2)}) collective-permute-start(f32[4,13,8,80]{3,2,1,0:T(8,128)} %copy.19), channel_id=1, source_target_pairs={{0,32},{32,64},{64,96},{96,128},{128,160},{160,192},{192,224},{1,3... | collective-permute-start | bytes 399368 | tf_op jit(solution)/shard_map/ppermute | solution.py:39
  31.7 1.9 %collective-permute-done.2 = f32[4,13,8,80]{3,2,1,0:T(8,128)} collective-permute-done((f32[4,13,8,80]{3,2,1,0:T(8,128)}, f32[4,13,8,80]{3,2,1,0:T(8,128)}, u32[]{:S(2)}, u32[]{:S(2)}) %collective-permute-start.2) | collective-permute-done | bytes 133152 | tf_op jit(solution)/shard_map/ppermute | solution.py:38
  33.5 1.6 %copy.18 = f32[4,13,8,80]{2,3,1,0:T(8,128)S(1)} copy(f32[4,13,8,80]{3,2,1,0:T(8,128)} %collective-permute-done.2) | data formatting | bytes 266240 | tf_op jit(solution)/shard_map/ppermute | solution.py:38
  35.1 3.4 %collective-permute-done.3 = f32[4,13,8,80]{3,2,1,0:T(8,128)} collective-permute-done((f32[4,13,8,80]{3,2,1,0:T(8,128)}, f32[4,13,8,80]{3,2,1,0:T(8,128)}, u32[]{:S(2)}, u32[]{:S(2)}) %collective-permute-start.3) | collective-permute-done | bytes 133152 | tf_op jit(solution)/shard_map/ppermute | solution.py:39
  38.5 2.9 %copy.20 = f32[4,13,8,80]{2,3,1,0:T(8,128)} copy(f32[4,13,8,80]{3,2,1,0:T(8,128)} %collective-permute-done.3) | data formatting | bytes 266240 | tf_op jit(solution)/shard_map/ppermute | solution.py:39
  41.4 3.8 %pad_maximum_fusion.x_ref = f32[4,13,80,256]{3,2,1,0:T(8,128)} fusion(f32[4,13,80,8]{3,2,1,0:T(8,128)} %bitcast.28, f32[4,13,80,8]{3,2,1,0:T(8,128)S(1)} %bitcast.27, f32[4,13,8,128]{3,2,1,0:T(8,128)} %copy-done.3, f32[4,13,8,128]{3,2,1,0:T(8,128)} %copy-done.2, f32[4,1,64,128]{3,2,1,0:T(8,128)} %bitcast.29, f32[4,2,64,128]{3,2,1,0:T(8,128)S(1)} %get-tuple-element.16, ...), kind=kLoop, calls=%fused_computation | loop fusion | flops 8519680 | bytes 6657024 | tf_op jit(solution)/shard_map/concatenate | solution.py:168
  45.2 29.5 %shard_map.59 = (f32[8,4,64,128]{3,2,1,0:T(8,128)}, f32[4,64,128]{2,1,0:T(8,128)}) custom-call(f32[1,256]{1,0:T(1,128)} %and_convert_fusion.mask_ref, f32[4,13,80,256]{3,2,1,0:T(8,128)} %pad_maximum_fusion.x_ref), custom_call_target="tpu_custom_call" | custom-call | tf_op jit(solution)/shard_map/pallas_call | solution.py:106
  74.8 1.0 reduce_sum.9
  75.9 1.2 collective-permute-done.4
  77.1 3.6 %collective-permute-done.5 = f32[8,8]{0,1:T(8,128)S(1)} collective-permute-done((f32[8,8]{0,1:T(8,128)S(1)}, f32[8,8]{0,1:T(8,128)S(1)}, u32[]{:S(2)}, u32[]{:S(2)}) %collective-permute-start.5) | collective-permute-done | bytes 288 | tf_op jit(solution)/shard_map/ppermute | solution.py:27
  80.7 3.6 %collective-permute-done.6 = f32[8,8]{0,1:T(8,128)S(1)} collective-permute-done((f32[8,8]{0,1:T(8,128)S(1)}, f32[8,8]{0,1:T(8,128)S(1)}, u32[]{:S(2)}, u32[]{:S(2)}) %collective-permute-start.6) | collective-permute-done | bytes 288 | tf_op jit(solution)/shard_map/ppermute | solution.py:27
  84.4 4.5 %collective-permute-done.7 = f32[8,8]{0,1:T(8,128)S(1)} collective-permute-done((f32[8,8]{0,1:T(8,128)S(1)}, f32[8,8]{0,1:T(8,128)S(1)}, u32[]{:S(2)}, u32[]{:S(2)}) %collective-permute-start.7) | collective-permute-done | bytes 288 | tf_op jit(solution)/shard_map/ppermute | solution.py:27
  88.9 2.0 %collective-permute-start.8 = (f32[8,8]{0,1:T(8,128)S(1)}, f32[8,8]{0,1:T(8,128)S(1)}, u32[]{:S(2)}, u32[]{:S(2)}) collective-permute-start(f32[8,8]{0,1:T(8,128)S(1)} %add.65), channel_id=1, source_target_pairs={{0,16},{1,17},{2,18},{3,19},{4,20},{5,21},{6,22},{7,23},{8,24},{9,... | collective-permute-start | bytes 776 | tf_op jit(solution)/shard_map/ppermute | solution.py:27
  90.9 5.5 %collective-permute-done.8 = f32[8,8]{0,1:T(8,128)S(1)} collective-permute-done((f32[8,8]{0,1:T(8,128)S(1)}, f32[8,8]{0,1:T(8,128)S(1)}, u32[]{:S(2)}, u32[]{:S(2)}) %collective-permute-start.8) | collective-permute-done | bytes 288 | tf_op jit(solution)/shard_map/ppermute | solution.py:27
  96.5 5.0 %collective-permute-done.9 = f32[8,8]{0,1:T(8,128)S(1)} collective-permute-done((f32[8,8]{0,1:T(8,128)S(1)}, f32[8,8]{0,1:T(8,128)S(1)}, u32[]{:S(2)}, u32[]{:S(2)}) %collective-permute-start.9) | collective-permute-done | bytes 288 | tf_op jit(solution)/shard_map/ppermute | solution.py:27
  102.0 3.1 %collective-permute-done.10 = f32[8,8]{0,1:T(8,128)S(1)} collective-permute-done((f32[8,8]{0,1:T(8,128)S(1)}, f32[8,8]{0,1:T(8,128)S(1)}, u32[]{:S(2)}, u32[]{:S(2)}) %collective-permute-start.10) | collective-permute-done | bytes 288 | tf_op jit(solution)/shard_map/ppermute | solution.py:27
  105.1 1.1 collective-permute-start.11
  106.2 4.0 %collective-permute-done.11 = f32[8,8]{0,1:T(8,128)S(1)} collective-permute-done((f32[8,8]{0,1:T(8,128)S(1)}, f32[8,8]{0,1:T(8,128)S(1)}, u32[]{:S(2)}, u32[]{:S(2)}) %collective-permute-start.11) | collective-permute-done | bytes 288 | tf_op jit(solution)/shard_map/ppermute | solution.py:27
  110.3 0.7 cholesky.17
  111.7 0.6 multiply_bitcast_fusion
  113.0 0.8 fusion.inv_ref
  113.8 0.7 copy.25
  114.4 3.7 %shard_map.60 = f32[8,4,64,128]{3,2,1,0:T(8,128)} custom-call(f32[8,8]{1,0:T(8,128)} %fusion.inv_ref, f32[1,1]{1,0:T(1,128)} %constant.65.clone.1.scale_ref, f32[8,4,64,128]{3,2,1,0:T(8,128)} %get-tuple-element.5.z_ref), custom_call_target="tpu_custom_call" | custom-call | tf_op jit(solution)/shard_map/pallas_call | solution.py:138
  (39 shorter events, 3.2 us)
Async XLA Ops:
  0.6 1.4 %copy-start.5 = (f32[2,4,64,128]{3,2,1,0:T(8,128)S(1)}, f32[2,4,64,128]{3,2,1,0:T(8,128)}, u32[]{:S(2)}) copy-start(f32[2,4,64,128]{3,2,1,0:T(8,128)} %param.5) | copy-start | bytes 786436
  0.6 1.4 %copy-start.4 = (f32[2,4,64,128]{3,2,1,0:T(8,128)S(1)}, f32[2,4,64,128]{3,2,1,0:T(8,128)}, u32[]{:S(2)}) copy-start(f32[2,4,64,128]{3,2,1,0:T(8,128)} %param.6) | copy-start | bytes 786436
  0.6 1.4 %copy-start.1 = (f32[4,64,128]{2,1,0:T(8,128)S(1)}, f32[4,64,128]{2,1,0:T(8,128)}, u32[]{:S(2)}) copy-start(f32[4,64,128]{2,1,0:T(8,128)} %param.7) | copy-start | bytes 393220
  2.1 13.8 %copy-start = (f32[4,2,64,128]{3,2,1,0:T(8,128)}, f32[4,2,64,128]{3,2,1,0:T(8,128)S(1)}, u32[]{:S(2)}) copy-start(f32[4,2,64,128]{3,2,1,0:T(8,128)S(1)} %get-tuple-element.17) | copy-start | bytes 786436
  2.1 9.8 %collective-permute-start = (f32[4,13,8,128]{3,2,1,0:T(8,128)S(1)}, f32[4,13,8,128]{3,2,1,0:T(8,128)S(1)}, u32[]{:S(2)}, u32[]{:S(2)}) collective-permute-start(f32[4,13,8,128]{3,2,1,0:T(8,128)S(1)} %get-tuple-element.12), channel_id=1, source_target_pairs={{1,0},{2,1},{3,2},{4,3},{5,4},{6,5},{7,6},{8,7},{9,8},{10,9},{11,1... | collective-permute-start | bytes 638984 | tf_op jit(solution)/shard_map/ppermute | solution.py:38
  8.5 7.4 %collective-permute-start.1 = (f32[4,13,8,128]{3,2,1,0:T(8,128)S(1)}, f32[4,13,8,128]{3,2,1,0:T(8,128)S(1)}, u32[]{:S(2)}, u32[]{:S(2)}) collective-permute-start(f32[4,13,8,128]{3,2,1,0:T(8,128)S(1)} %get-tuple-element.13), channel_id=1, source_target_pairs={{0,1},{1,2},{2,3},{3,4},{4,5},{5,6},{6,7},{7,8},{8,9},{9,10},{10,1... | collective-permute-start | bytes 638984 | tf_op jit(solution)/shard_map/ppermute | solution.py:39
  11.9 4.0 %copy-start.2 = (f32[4,13,8,128]{3,2,1,0:T(8,128)}, f32[4,13,8,128]{3,2,1,0:T(8,128)S(1)}, u32[]{:S(2)}) copy-start(f32[4,13,8,128]{3,2,1,0:T(8,128)S(1)} %collective-permute-done) | copy-start | bytes 638980
  15.9 0.7 copy-start.3
  21.7 11.8 %collective-permute-start.2 = (f32[4,13,8,80]{3,2,1,0:T(8,128)}, f32[4,13,8,80]{3,2,1,0:T(8,128)}, u32[]{:S(2)}, u32[]{:S(2)}) collective-permute-start(f32[4,13,8,80]{3,2,1,0:T(8,128)} %copy.17), channel_id=1, source_target_pairs={{32,0},{64,32},{96,64},{128,96},{160,128},{192,160},{224,192},{33,... | collective-permute-start | bytes 399368 | tf_op jit(solution)/shard_map/ppermute | solution.py:38
  28.1 10.4 %collective-permute-start.3 = (f32[4,13,8,80]{3,2,1,0:T(8,128)}, f32[4,13,8,80]{3,2,1,0:T(8,128)}, u32[]{:S(2)}, u32[]{:S(2)}) collective-permute-start(f32[4,13,8,80]{3,2,1,0:T(8,128)} %copy.19), channel_id=1, source_target_pairs={{0,32},{32,64},{64,96},{96,128},{128,160},{160,192},{192,224},{1,3... | collective-permute-start | bytes 399368 | tf_op jit(solution)/shard_map/ppermute | solution.py:39
  75.9 1.2 %collective-permute-start.4 = (f32[8,8]{0,1:T(8,128)S(1)}, f32[8,8]{0,1:T(8,128)S(1)}, u32[]{:S(2)}, u32[]{:S(2)}) collective-permute-start(f32[8,8]{0,1:T(8,128)S(1)} %copy.22), channel_id=1, source_target_pairs={{0,1},{1,0},{2,3},{3,2},{4,5},{5,4},{6,7},{7,6},{8,9},{9,8},{10,11... | collective-permute-start | bytes 776 | tf_op jit(solution)/shard_map/ppermute | solution.py:27
  77.1 3.6 %collective-permute-start.5 = (f32[8,8]{0,1:T(8,128)S(1)}, f32[8,8]{0,1:T(8,128)S(1)}, u32[]{:S(2)}, u32[]{:S(2)}) collective-permute-start(f32[8,8]{0,1:T(8,128)S(1)} %add.62), channel_id=1, source_target_pairs={{0,2},{1,3},{2,0},{3,1},{4,6},{5,7},{6,4},{7,5},{8,10},{9,11},{10,... | collective-permute-start | bytes 776 | tf_op jit(solution)/shard_map/ppermute | solution.py:27
  80.7 3.6 %collective-permute-start.6 = (f32[8,8]{0,1:T(8,128)S(1)}, f32[8,8]{0,1:T(8,128)S(1)}, u32[]{:S(2)}, u32[]{:S(2)}) collective-permute-start(f32[8,8]{0,1:T(8,128)S(1)} %add.63), channel_id=1, source_target_pairs={{0,4},{1,5},{2,6},{3,7},{4,0},{5,1},{6,2},{7,3},{8,12},{9,13},{10,... | collective-permute-start | bytes 776 | tf_op jit(solution)/shard_map/ppermute | solution.py:27
  84.4 4.5 %collective-permute-start.7 = (f32[8,8]{0,1:T(8,128)S(1)}, f32[8,8]{0,1:T(8,128)S(1)}, u32[]{:S(2)}, u32[]{:S(2)}) collective-permute-start(f32[8,8]{0,1:T(8,128)S(1)} %add.64), channel_id=1, source_target_pairs={{0,8},{1,9},{2,10},{3,11},{4,12},{5,13},{6,14},{7,15},{8,0},{9,1},... | collective-permute-start | bytes 776 | tf_op jit(solution)/shard_map/ppermute | solution.py:27
  88.9 7.5 %collective-permute-start.8 = (f32[8,8]{0,1:T(8,128)S(1)}, f32[8,8]{0,1:T(8,128)S(1)}, u32[]{:S(2)}, u32[]{:S(2)}) collective-permute-start(f32[8,8]{0,1:T(8,128)S(1)} %add.65), channel_id=1, source_target_pairs={{0,16},{1,17},{2,18},{3,19},{4,20},{5,21},{6,22},{7,23},{8,24},{9,... | collective-permute-start | bytes 776 | tf_op jit(solution)/shard_map/ppermute | solution.py:27
  96.4 5.1 %collective-permute-start.9 = (f32[8,8]{0,1:T(8,128)S(1)}, f32[8,8]{0,1:T(8,128)S(1)}, u32[]{:S(2)}, u32[]{:S(2)}) collective-permute-start(f32[8,8]{0,1:T(8,128)S(1)} %add.66), channel_id=1, source_target_pairs={{0,32},{32,0},{64,96},{96,64},{128,160},{160,128},{192,224},{224,1... | collective-permute-start | bytes 776 | tf_op jit(solution)/shard_map/ppermute | solution.py:27
  101.5 3.6 %collective-permute-start.10 = (f32[8,8]{0,1:T(8,128)S(1)}, f32[8,8]{0,1:T(8,128)S(1)}, u32[]{:S(2)}, u32[]{:S(2)}) collective-permute-start(f32[8,8]{0,1:T(8,128)S(1)} %add.67), channel_id=1, source_target_pairs={{0,64},{32,96},{64,0},{96,32},{128,192},{160,224},{192,128},{224,1... | collective-permute-start | bytes 776 | tf_op jit(solution)/shard_map/ppermute | solution.py:27
  105.1 5.1 %collective-permute-start.11 = (f32[8,8]{0,1:T(8,128)S(1)}, f32[8,8]{0,1:T(8,128)S(1)}, u32[]{:S(2)}, u32[]{:S(2)}) collective-permute-start(f32[8,8]{0,1:T(8,128)S(1)} %add.68), channel_id=1, source_target_pairs={{0,128},{32,160},{64,192},{96,224},{128,0},{160,32},{192,64},{224,... | collective-permute-start | bytes 776 | tf_op jit(solution)/shard_map/ppermute | solution.py:27

commit v3 on v2

--- a/solution.py
+++ b/solution.py
@@ -159,15 +159,47 @@
         ),
         axis=1,
     )
-    lon_next, lon_prev = neighbours(stack, "lon", 2, True)
-    stack = jnp.concatenate((stack, lon_next, lon_prev), axis=2)
-    lat_in = jnp.swapaxes(stack, 2, 3)
-    lat_next, lat_prev = neighbours(lat_in, "lat", 2, False)
+    n_lon = lax.axis_size("lon")
+    n_lat = lax.axis_size("lat")
+    head_rows = stack[:, :, :HALO]
+    tail_rows = stack[:, :, width_lon - HALO :]
+
+    def lat_edges(rows):
+        return jnp.swapaxes(rows[..., :HALO], 2, 3), jnp.swapaxes(rows[..., width_lat - HALO :], 2, 3)
+
+    def lon_send(x, up):
+        pairs = [((i + 1) % n_lon, i) if up else (i, (i + 1) % n_lon) for i in range(n_lon)]
+        return lax.ppermute(x, "lon", pairs)
+
+    def lat_send(x, up):
+        pairs = [(j + 1, j) if up else (j, j + 1) for j in range(n_lat - 1)]
+        return lax.ppermute(x, "lat", pairs)
+
+    def diagonal_send(x, lon_up, lat_up):
+        pairs = []
+        for i in range(n_lon):
+            for j in range(n_lat - 1):
+                ni = (i + 1) % n_lon
+                src_i, dst_i = (ni, i) if lon_up else (i, ni)
+                src_j, dst_j = (j + 1, j) if lat_up else (j, j + 1)
+                pairs.append((src_j * n_lon + src_i, dst_j * n_lon + dst_i))
+        return lax.ppermute(x, ("lat", "lon"), pairs)
+
+    own_head, own_tail = lat_edges(stack)
+    lon_next = lon_send(head_rows, True)
+    lon_prev = lon_send(tail_rows, False)
+    lat_next = lat_send(own_head, True)
+    lat_prev = lat_send(own_tail, False)
+    corner_nn = diagonal_send(head_rows[..., :HALO], True, True)
+    corner_np = diagonal_send(head_rows[..., width_lat - HALO :], True, False)
+    corner_pn = diagonal_send(tail_rows[..., :HALO], False, True)
+    corner_pp = diagonal_send(tail_rows[..., width_lat - HALO :], False, False)
     lanes = 256
-    gap = jnp.zeros(stack.shape[:3] + (lanes - width_lat - 2 * HALO,), stack.dtype)
-    stack = jnp.concatenate(
-        (stack, jnp.swapaxes(lat_next, 2, 3), gap, jnp.swapaxes(lat_prev, 2, 3)), axis=3
-    )
+    gap = jnp.zeros(stack.shape[:2] + (width_lon + 2 * HALO, lanes - width_lat - 2 * HALO), stack.dtype)
+    left = jnp.concatenate((stack, lon_next, lon_prev), axis=2)
+    right_next = jnp.concatenate((jnp.swapaxes(lat_next, 2, 3), corner_nn, corner_pn), axis=2)
+    right_prev = jnp.concatenate((jnp.swapaxes(lat_prev, 2, 3), corner_np, corner_pp), axis=2)
+    stack = jnp.concatenate((left, right_next, gap, right_prev), axis=3)
     lane = lax.broadcasted_iota(jnp.int32, (1, lanes), 1)
     start = lax.axis_index("lat") * width_lat
     cell = jnp.where(lane < width_lat + HALO, start + lane, start + lane - lanes)

time: 118 us -> 138 us (1.17)
  starting transfers between devices: 18.2 us -> 39.9 us
  waiting for transfers between devices: 43.1 us -> 36 us
  local copies, waits for them, and re-layouts: 13.7 us -> 16.8 us
  other arithmetic: 8.3 us -> 10.1 us
    ppermute x4 -> x8, starting transfers between devices: 14.4 us -> 33 us  [the longest x4 19.1 us: diagonal_send(): return lax.ppermute(x, ('lat', 'lon'), pairs)]
    transpose x0 -> x3, local copies, waits for them, and re-layouts: none -> 7.6 us  [the longest x2 4.96 us: lat_edges(): jnp.swapaxes(rows[..., :HALO], 2, 3)]
    slice x3 -> x2, local copies, waits for them, and re-layouts: 6.19 us -> 1.79 us  [the longest x1 1 us: body(): corner_nn = diagonal_send(head_rows[..., :HALO], True, True)]
    ppermute x4 -> x8, waiting for transfers between devices: 12.7 us -> 8.64 us  [the longest x4 8.63 us: diagonal_send(): return lax.ppermute(x, ('lat', 'lon'), pairs)]
    ppermute x8, starting transfers between devices: 3.8 us -> 6.84 us  [all_sum(): lax.ppermute(value, axis, [(i, i ^ stride) for i in range(count)])]
    ppermute x8, waiting for transfers between devices: 30.4 us -> 27.4 us  [all_sum(): lax.ppermute(value, axis, [(i, i ^ stride) for i in range(count)])]
    concatenate x1 -> x2, other arithmetic: 3.81 us -> 5.77 us  [the longest x1 4.67 us: body(): stack = jnp.concatenate((left, right_next, gap, right_prev), axis=3)]
  transfers between devices with their start and end apart: 12 -> 16, of which waited for: 12 -> 10; matrix products, arithmetic and copies ran while one was open for 3% -> 7% of each run, Pallas kernels for 0% -> 0%
where the time goes in v3:
time: 138 us
  starting transfers between devices  39.9 us (29%)
  waiting for transfers between devices  36 us (26%)
  Pallas kernels  33.2 us (24%)
  local copies, waits for them, and re-layouts  16.8 us (12%)
  other arithmetic  10.1 us (7%)
    pallas_call x1, Pallas kernels, transport(): pl.pallas_call(transport_kernel, grid=(levels,), in_specs=[pl.BlockSpec((...  29.6 us
    ppermute x8, waiting for transfers between devices, all_sum(): lax.ppermute(value, axis, [(i, i ^ stride) for i in range(count)])  27.4 us
    ppermute x4, starting transfers between devices, diagonal_send(): return lax.ppermute(x, ('lat', 'lon'), pairs)  19.1 us
    ppermute x4, waiting for transfers between devices, diagonal_send(): return lax.ppermute(x, ('lat', 'lon'), pairs)  8.63 us
    ppermute x2, starting transfers between devices, lat_send(): return lax.ppermute(x, 'lat', pairs)  8.13 us
    ppermute x8, starting transfers between devices, all_sum(): lax.ppermute(value, axis, [(i, i ^ stride) for i in range(count)])  6.84 us
    ppermute x2, starting transfers between devices, lon_send(): return lax.ppermute(x, 'lon', pairs)  5.75 us
    transpose x2, local copies, waits for them, and re-layouts, lat_edges(): jnp.swapaxes(rows[..., :HALO], 2, 3)  4.96 us
  transfers between devices with their start and end apart: 16, of which 10 were waited for; matrix products, arithmetic and copies ran while one was open for 7% of the time, Pallas kernels for 0%

profile of v3, /device:TPU:6, one launch (start us, length us, event | category | flops | bytes accessed | tf_op | source)
XLA Modules:
  0.0 137.6 jit_solution(11987008126560429302)
XLA Ops:
  0.6 1.3 copy.45
  1.9 1.1 copy_bitcast_fusion.1
  3.0 1.1 pad_maximum_fusion
  4.1 2.3 %slice_bitcast_fusion.1 = (f32[4,13,8,64]{2,3,1,0:T(8,128)}, f32[4,13,8,64]{2,3,1,0:T(8,128)}) fusion(f32[4,13,64,128]{3,2,1,0:T(8,128)S(1)} %pad_maximum_fusion), kind=kLoop, calls=%fused_computation.2 | loop fusion | bytes 425984 | tf_op jit(solution)/shard_map/transpose | solution.py:168
  6.4 2.6 %copy.33 = f32[4,13,8,64]{3,2,1,0:T(8,128)} copy(f32[4,13,8,64]{2,3,1,0:T(8,128)} %get-tuple-element.14) | data formatting | bytes 212992 | tf_op jit(solution)/shard_map/transpose | solution.py:168
  9.1 5.5 %collective-permute-start.2 = (f32[4,13,8,64]{3,2,1,0:T(8,128)}, f32[4,13,8,64]{3,2,1,0:T(8,128)}, u32[]{:S(2)}, u32[]{:S(2)}) collective-permute-start(f32[4,13,8,64]{3,2,1,0:T(8,128)} %copy.33), channel_id=1, source_target_pairs={{32,0},{64,32},{96,64},{128,96},{160,128},{192,160},{224,192},{33,... | collective-permute-start | bytes 319496 | tf_op jit(solution)/shard_map/ppermute | solution.py:176
  14.6 2.6 %copy.35 = f32[4,13,8,64]{3,2,1,0:T(8,128)} copy(f32[4,13,8,64]{2,3,1,0:T(8,128)} %get-tuple-element.15) | data formatting | bytes 212992 | tf_op jit(solution)/shard_map/transpose | solution.py:168
  17.2 2.6 %collective-permute-start.5 = (f32[4,13,8,64]{3,2,1,0:T(8,128)}, f32[4,13,8,64]{3,2,1,0:T(8,128)}, u32[]{:S(2)}, u32[]{:S(2)}) collective-permute-start(f32[4,13,8,64]{3,2,1,0:T(8,128)} %copy.35), channel_id=1, source_target_pairs={{0,32},{32,64},{64,96},{96,128},{128,160},{160,192},{192,224},{1,3... | collective-permute-start | bytes 319496 | tf_op jit(solution)/shard_map/ppermute | solution.py:176
  20.6 5.7 %collective-permute-start = (f32[4,13,8,128]{3,2,1,0:T(8,128)}, f32[4,13,8,128]{3,2,1,0:T(8,128)}, u32[]{:S(2)}, u32[]{:S(2)}) collective-permute-start(f32[4,13,8,128]{3,2,1,0:T(8,128)} %get-tuple-element.12), channel_id=1, source_target_pairs={{1,0},{2,1},{3,2},{4,3},{5,4},{6,5},{7,6},{8,7},{9,8},{10,9},{11,1... | collective-permute-start | bytes 638984 | tf_op jit(solution)/shard_map/ppermute | solution.py:172
  26.4 1.0 fusion.4
  27.4 7.7 %collective-permute-start.3 = (f32[4,13,8,8]{3,2,1,0:T(8,128)}, f32[4,13,8,8]{3,2,1,0:T(8,128)S(1)}, u32[]{:S(2)}, u32[]{:S(2)}) collective-permute-start(f32[4,13,8,8]{3,2,1,0:T(8,128)} %get-tuple-element.16), channel_id=1, source_target_pairs={{33,0},{65,32},{97,64},{129,96},{161,128},{193,160},{225,192},{34,... | collective-permute-start | bytes 39944 | tf_op jit(solution)/shard_map/ppermute | solution.py:186
  35.1 3.7 %collective-permute-done.3 = f32[4,13,8,8]{3,2,1,0:T(8,128)S(1)} collective-permute-done((f32[4,13,8,8]{3,2,1,0:T(8,128)}, f32[4,13,8,8]{3,2,1,0:T(8,128)S(1)}, u32[]{:S(2)}, u32[]{:S(2)}) %collective-permute-start.3) | collective-permute-done | bytes 13344 | tf_op jit(solution)/shard_map/ppermute | solution.py:186
  38.7 1.9 %collective-permute-start.4 = (f32[4,13,8,8]{3,2,1,0:T(8,128)}, f32[4,13,8,8]{3,2,1,0:T(8,128)}, u32[]{:S(2)}, u32[]{:S(2)}) collective-permute-start(f32[4,13,8,8]{3,2,1,0:T(8,128)} %get-tuple-element.18), channel_id=1, source_target_pairs={{32,1},{64,33},{96,65},{128,97},{160,129},{192,161},{224,193},{33,... | collective-permute-start | bytes 39944 | tf_op jit(solution)/shard_map/ppermute | solution.py:186
  40.7 7.6 %collective-permute-start.6 = (f32[4,13,8,8]{3,2,1,0:T(8,128)}, f32[4,13,8,8]{3,2,1,0:T(8,128)}, u32[]{:S(2)}, u32[]{:S(2)}) collective-permute-start(f32[4,13,8,8]{3,2,1,0:T(8,128)} %get-tuple-element.17), channel_id=1, source_target_pairs={{1,32},{33,64},{65,96},{97,128},{129,160},{161,192},{193,224},{2,3... | collective-permute-start | bytes 39944 | tf_op jit(solution)/shard_map/ppermute | solution.py:186
  48.3 1.9 %collective-permute-start.7 = (f32[4,13,8,8]{3,2,1,0:T(8,128)}, f32[4,13,8,8]{3,2,1,0:T(8,128)}, u32[]{:S(2)}, u32[]{:S(2)}) collective-permute-start(f32[4,13,8,8]{3,2,1,0:T(8,128)} %get-tuple-element.19), channel_id=1, source_target_pairs={{0,33},{32,65},{64,97},{96,129},{128,161},{160,193},{192,225},{1,3... | collective-permute-start | bytes 39944 | tf_op jit(solution)/shard_map/ppermute | solution.py:186
  50.9 1.4 %copy.34 = f32[4,13,8,64]{2,3,1,0:T(8,128)S(1)} copy(f32[4,13,8,64]{3,2,1,0:T(8,128)} %collective-permute-done.2) | data formatting | bytes 212992 | tf_op jit(solution)/shard_map/ppermute | solution.py:176
  52.4 2.7 %copy.36 = f32[4,13,8,64]{2,3,1,0:T(8,128)} copy(f32[4,13,8,64]{3,2,1,0:T(8,128)} %collective-permute-done.5) | data formatting | bytes 212992 | tf_op jit(solution)/shard_map/ppermute | solution.py:176
  55.0 5.0 %collective-permute-done.7 = f32[4,13,8,8]{3,2,1,0:T(8,128)} collective-permute-done((f32[4,13,8,8]{3,2,1,0:T(8,128)}, f32[4,13,8,8]{3,2,1,0:T(8,128)}, u32[]{:S(2)}, u32[]{:S(2)}) %collective-permute-start.7) | collective-permute-done | bytes 13344 | tf_op jit(solution)/shard_map/ppermute | solution.py:186
  60.0 4.7 %maximum_maximum_fusion.x_ref = f32[4,13,80,256]{3,2,1,0:T(8,128)} fusion(f32[4,13,8,8]{3,2,1,0:T(8,128)} %collective-permute-done.7, f32[4,13,8,8]{3,2,1,0:T(8,128)} %collective-permute-done.6, f32[4,13,64,8]{3,2,1,0:T(8,128)} %bitcast.29, f32[4,13,8,8]{3,2,1,0:T(8,128)} %collective-permute-done.4, f32[4,13,8,8]{3,2,1,0:T(8,128)} %copy-done.1, ...), kind=kLoop, calls=%fused_computation | loop fusion | flops 12779520 | bytes 6657024 | tf_op jit(solution)/shard_map/concatenate | solution.py:202
  64.7 29.6 %shard_map.59 = (f32[8,4,64,128]{3,2,1,0:T(8,128)}, f32[4,64,128]{2,1,0:T(8,128)}) custom-call(f32[1,256]{1,0:T(1,128)} %and_convert_fusion.mask_ref, f32[4,13,80,256]{3,2,1,0:T(8,128)} %maximum_maximum_fusion.x_ref), custom_call_target="tpu_custom_call" | custom-call | tf_op jit(solution)/shard_map/pallas_call | solution.py:106
  94.3 1.0 reduce_sum.9
  95.4 1.2 collective-permute-done.8
  96.6 3.6 %collective-permute-done.9 = f32[8,8]{0,1:T(8,128)S(1)} collective-permute-done((f32[8,8]{0,1:T(8,128)S(1)}, f32[8,8]{0,1:T(8,128)S(1)}, u32[]{:S(2)}, u32[]{:S(2)}) %collective-permute-start.9) | collective-permute-done | bytes 288 | tf_op jit(solution)/shard_map/ppermute | solution.py:27
  100.2 3.6 %collective-permute-done.10 = f32[8,8]{0,1:T(8,128)S(1)} collective-permute-done((f32[8,8]{0,1:T(8,128)S(1)}, f32[8,8]{0,1:T(8,128)S(1)}, u32[]{:S(2)}, u32[]{:S(2)}) %collective-permute-start.10) | collective-permute-done | bytes 288 | tf_op jit(solution)/shard_map/ppermute | solution.py:27
  103.8 4.5 %collective-permute-done.11 = f32[8,8]{0,1:T(8,128)S(1)} collective-permute-done((f32[8,8]{0,1:T(8,128)S(1)}, f32[8,8]{0,1:T(8,128)S(1)}, u32[]{:S(2)}, u32[]{:S(2)}) %collective-permute-start.11) | collective-permute-done | bytes 288 | tf_op jit(solution)/shard_map/ppermute | solution.py:27
  108.3 4.5 %collective-permute-start.12 = (f32[8,8]{0,1:T(8,128)S(1)}, f32[8,8]{0,1:T(8,128)S(1)}, u32[]{:S(2)}, u32[]{:S(2)}) collective-permute-start(f32[8,8]{0,1:T(8,128)S(1)} %add.65), channel_id=1, source_target_pairs={{0,16},{1,17},{2,18},{3,19},{4,20},{5,21},{6,22},{7,23},{8,24},{9,... | collective-permute-start | bytes 776 | tf_op jit(solution)/shard_map/ppermute | solution.py:27
  112.9 3.0 %collective-permute-done.12 = f32[8,8]{0,1:T(8,128)S(1)} collective-permute-done((f32[8,8]{0,1:T(8,128)S(1)}, f32[8,8]{0,1:T(8,128)S(1)}, u32[]{:S(2)}, u32[]{:S(2)}) %collective-permute-start.12) | collective-permute-done | bytes 288 | tf_op jit(solution)/shard_map/ppermute | solution.py:27
  115.9 5.1 %collective-permute-done.13 = f32[8,8]{0,1:T(8,128)S(1)} collective-permute-done((f32[8,8]{0,1:T(8,128)S(1)}, f32[8,8]{0,1:T(8,128)S(1)}, u32[]{:S(2)}, u32[]{:S(2)}) %collective-permute-start.13) | collective-permute-done | bytes 288 | tf_op jit(solution)/shard_map/ppermute | solution.py:27
  121.8 2.7 %collective-permute-done.14 = f32[8,8]{0,1:T(8,128)S(1)} collective-permute-done((f32[8,8]{0,1:T(8,128)S(1)}, f32[8,8]{0,1:T(8,128)S(1)}, u32[]{:S(2)}, u32[]{:S(2)}) %collective-permute-start.14) | collective-permute-done | bytes 288 | tf_op jit(solution)/shard_map/ppermute | solution.py:27
  124.6 1.4 %collective-permute-start.15 = (f32[8,8]{0,1:T(8,128)S(1)}, f32[8,8]{0,1:T(8,128)S(1)}, u32[]{:S(2)}, u32[]{:S(2)}) collective-permute-start(f32[8,8]{0,1:T(8,128)S(1)} %add.68), channel_id=1, source_target_pairs={{0,128},{32,160},{64,192},{96,224},{128,0},{160,32},{192,64},{224,... | collective-permute-start | bytes 776 | tf_op jit(solution)/shard_map/ppermute | solution.py:27
  126.0 3.7 %collective-permute-done.15 = f32[8,8]{0,1:T(8,128)S(1)} collective-permute-done((f32[8,8]{0,1:T(8,128)S(1)}, f32[8,8]{0,1:T(8,128)S(1)}, u32[]{:S(2)}, u32[]{:S(2)}) %collective-permute-start.15) | collective-permute-done | bytes 288 | tf_op jit(solution)/shard_map/ppermute | solution.py:27
  133.9 3.7 %shard_map.60 = f32[8,4,64,128]{3,2,1,0:T(8,128)} custom-call(f32[8,8]{1,0:T(8,128)} %fusion.inv_ref, f32[1,1]{1,0:T(1,128)} %constant.65.clone.1.scale_ref, f32[8,4,64,128]{3,2,1,0:T(8,128)} %get-tuple-element.5.z_ref), custom_call_target="tpu_custom_call" | custom-call | tf_op jit(solution)/shard_map/pallas_call | solution.py:138
  (40 shorter events, 6.7 us)
Async XLA Ops:
  9.1 51.0 %copy-start = (f32[4,64,128]{2,1,0:T(8,128)S(1)}, f32[4,64,128]{2,1,0:T(8,128)}, u32[]{:S(2)}) copy-start(f32[4,64,128]{2,1,0:T(8,128)} %param.7) | copy-start | bytes 393220
  9.1 31.6 %collective-permute-start.2 = (f32[4,13,8,64]{3,2,1,0:T(8,128)}, f32[4,13,8,64]{3,2,1,0:T(8,128)}, u32[]{:S(2)}, u32[]{:S(2)}) collective-permute-start(f32[4,13,8,64]{3,2,1,0:T(8,128)} %copy.33), channel_id=1, source_target_pairs={{32,0},{64,32},{96,64},{128,96},{160,128},{192,160},{224,192},{33,... | collective-permute-start | bytes 319496 | tf_op jit(solution)/shard_map/ppermute | solution.py:176
  17.2 31.1 %collective-permute-start.5 = (f32[4,13,8,64]{3,2,1,0:T(8,128)}, f32[4,13,8,64]{3,2,1,0:T(8,128)}, u32[]{:S(2)}, u32[]{:S(2)}) collective-permute-start(f32[4,13,8,64]{3,2,1,0:T(8,128)} %copy.35), channel_id=1, source_target_pairs={{0,32},{32,64},{64,96},{96,128},{128,160},{160,192},{192,224},{1,3... | collective-permute-start | bytes 319496 | tf_op jit(solution)/shard_map/ppermute | solution.py:176
  20.6 39.4 %collective-permute-start = (f32[4,13,8,128]{3,2,1,0:T(8,128)}, f32[4,13,8,128]{3,2,1,0:T(8,128)}, u32[]{:S(2)}, u32[]{:S(2)}) collective-permute-start(f32[4,13,8,128]{3,2,1,0:T(8,128)} %get-tuple-element.12), channel_id=1, source_target_pairs={{1,0},{2,1},{3,2},{4,3},{5,4},{6,5},{7,6},{8,7},{9,8},{10,9},{11,1... | collective-permute-start | bytes 638984 | tf_op jit(solution)/shard_map/ppermute | solution.py:172
  26.4 33.6 %collective-permute-start.1 = (f32[4,13,8,128]{3,2,1,0:T(8,128)}, f32[4,13,8,128]{3,2,1,0:T(8,128)}, u32[]{:S(2)}, u32[]{:S(2)}) collective-permute-start(f32[4,13,8,128]{3,2,1,0:T(8,128)} %get-tuple-element.13), channel_id=1, source_target_pairs={{0,1},{1,2},{2,3},{3,4},{4,5},{5,6},{6,7},{7,8},{8,9},{9,10},{10,1... | collective-permute-start | bytes 638984 | tf_op jit(solution)/shard_map/ppermute | solution.py:172
  27.4 11.3 %collective-permute-start.3 = (f32[4,13,8,8]{3,2,1,0:T(8,128)}, f32[4,13,8,8]{3,2,1,0:T(8,128)S(1)}, u32[]{:S(2)}, u32[]{:S(2)}) collective-permute-start(f32[4,13,8,8]{3,2,1,0:T(8,128)} %get-tuple-element.16), channel_id=1, source_target_pairs={{33,0},{65,32},{97,64},{129,96},{161,128},{193,160},{225,192},{34,... | collective-permute-start | bytes 39944 | tf_op jit(solution)/shard_map/ppermute | solution.py:186
  38.7 12.1 %copy-start.1 = (f32[4,13,8,8]{3,2,1,0:T(8,128)}, f32[4,13,8,8]{3,2,1,0:T(8,128)S(1)}, u32[]{:S(2)}) copy-start(f32[4,13,8,8]{3,2,1,0:T(8,128)S(1)} %collective-permute-done.3) | copy-start | bytes 39940
  38.7 16.3 %collective-permute-start.4 = (f32[4,13,8,8]{3,2,1,0:T(8,128)}, f32[4,13,8,8]{3,2,1,0:T(8,128)}, u32[]{:S(2)}, u32[]{:S(2)}) collective-permute-start(f32[4,13,8,8]{3,2,1,0:T(8,128)} %get-tuple-element.18), channel_id=1, source_target_pairs={{32,1},{64,33},{96,65},{128,97},{160,129},{192,161},{224,193},{33,... | collective-permute-start | bytes 39944 | tf_op jit(solution)/shard_map/ppermute | solution.py:186
  40.7 14.4 %collective-permute-start.6 = (f32[4,13,8,8]{3,2,1,0:T(8,128)}, f32[4,13,8,8]{3,2,1,0:T(8,128)}, u32[]{:S(2)}, u32[]{:S(2)}) collective-permute-start(f32[4,13,8,8]{3,2,1,0:T(8,128)} %get-tuple-element.17), channel_id=1, source_target_pairs={{1,32},{33,64},{65,96},{97,128},{129,160},{161,192},{193,224},{2,3... | collective-permute-start | bytes 39944 | tf_op jit(solution)/shard_map/ppermute | solution.py:186
  48.3 11.7 %collective-permute-start.7 = (f32[4,13,8,8]{3,2,1,0:T(8,128)}, f32[4,13,8,8]{3,2,1,0:T(8,128)}, u32[]{:S(2)}, u32[]{:S(2)}) collective-permute-start(f32[4,13,8,8]{3,2,1,0:T(8,128)} %get-tuple-element.19), channel_id=1, source_target_pairs={{0,33},{32,65},{64,97},{96,129},{128,161},{160,193},{192,225},{1,3... | collective-permute-start | bytes 39944 | tf_op jit(solution)/shard_map/ppermute | solution.py:186
  95.4 1.2 collective-permute-start.8
  96.6 3.6 %collective-permute-start.9 = (f32[8,8]{0,1:T(8,128)S(1)}, f32[8,8]{0,1:T(8,128)S(1)}, u32[]{:S(2)}, u32[]{:S(2)}) collective-permute-start(f32[8,8]{0,1:T(8,128)S(1)} %add.62), channel_id=1, source_target_pairs={{0,2},{1,3},{2,0},{3,1},{4,6},{5,7},{6,4},{7,5},{8,10},{9,11},{10,... | collective-permute-start | bytes 776 | tf_op jit(solution)/shard_map/ppermute | solution.py:27
  100.2 3.6 %collective-permute-start.10 = (f32[8,8]{0,1:T(8,128)S(1)}, f32[8,8]{0,1:T(8,128)S(1)}, u32[]{:S(2)}, u32[]{:S(2)}) collective-permute-start(f32[8,8]{0,1:T(8,128)S(1)} %add.63), channel_id=1, source_target_pairs={{0,4},{1,5},{2,6},{3,7},{4,0},{5,1},{6,2},{7,3},{8,12},{9,13},{10,... | collective-permute-start | bytes 776 | tf_op jit(solution)/shard_map/ppermute | solution.py:27
  103.8 4.5 %collective-permute-start.11 = (f32[8,8]{0,1:T(8,128)S(1)}, f32[8,8]{0,1:T(8,128)S(1)}, u32[]{:S(2)}, u32[]{:S(2)}) collective-permute-start(f32[8,8]{0,1:T(8,128)S(1)} %add.64), channel_id=1, source_target_pairs={{0,8},{1,9},{2,10},{3,11},{4,12},{5,13},{6,14},{7,15},{8,0},{9,1},... | collective-permute-start | bytes 776 | tf_op jit(solution)/shard_map/ppermute | solution.py:27
  108.3 7.5 %collective-permute-start.12 = (f32[8,8]{0,1:T(8,128)S(1)}, f32[8,8]{0,1:T(8,128)S(1)}, u32[]{:S(2)}, u32[]{:S(2)}) collective-permute-start(f32[8,8]{0,1:T(8,128)S(1)} %add.65), channel_id=1, source_target_pairs={{0,16},{1,17},{2,18},{3,19},{4,20},{5,21},{6,22},{7,23},{8,24},{9,... | collective-permute-start | bytes 776 | tf_op jit(solution)/shard_map/ppermute | solution.py:27
  115.9 5.1 %collective-permute-start.13 = (f32[8,8]{0,1:T(8,128)S(1)}, f32[8,8]{0,1:T(8,128)S(1)}, u32[]{:S(2)}, u32[]{:S(2)}) collective-permute-start(f32[8,8]{0,1:T(8,128)S(1)} %add.66), channel_id=1, source_target_pairs={{0,32},{32,0},{64,96},{96,64},{128,160},{160,128},{192,224},{224,1... | collective-permute-start | bytes 776 | tf_op jit(solution)/shard_map/ppermute | solution.py:27
  121.0 3.6 %collective-permute-start.14 = (f32[8,8]{0,1:T(8,128)S(1)}, f32[8,8]{0,1:T(8,128)S(1)}, u32[]{:S(2)}, u32[]{:S(2)}) collective-permute-start(f32[8,8]{0,1:T(8,128)S(1)} %add.67), channel_id=1, source_target_pairs={{0,64},{32,96},{64,0},{96,32},{128,192},{160,224},{192,128},{224,1... | collective-permute-start | bytes 776 | tf_op jit(solution)/shard_map/ppermute | solution.py:27
  124.6 5.1 %collective-permute-start.15 = (f32[8,8]{0,1:T(8,128)S(1)}, f32[8,8]{0,1:T(8,128)S(1)}, u32[]{:S(2)}, u32[]{:S(2)}) collective-permute-start(f32[8,8]{0,1:T(8,128)S(1)} %add.68), channel_id=1, source_target_pairs={{0,128},{32,160},{64,192},{96,224},{128,0},{160,32},{192,64},{224,... | collective-permute-start | bytes 776 | tf_op jit(solution)/shard_map/ppermute | solution.py:27

commit v4 on v2

v4 whole, which is shorter than its diff:
```python
import jax
import jax.numpy as jnp
from jax import lax
from jax.experimental import pallas as pl
from jax.experimental.pallas import tpu as pltpu
from jax.sharding import PartitionSpec as P

STEPS = 4
HALO = 2 * STEPS

diffuse = 0.24


def lower_inverse(lower):
    eye = jnp.eye(lower.shape[0], dtype=lower.dtype)
    return lax.linalg.triangular_solve(lower, eye, left_side=True, lower=True)


def all_sum(value, axes):
    for axis in axes:
        count = lax.axis_size(axis)
        if count & (count - 1):
            value = lax.psum(value, axis)
            continue
        stride = 1
        while stride < count:
            value = value + lax.ppermute(value, axis, [(i, i ^ stride) for i in range(count)])
            stride *= 2
    return value


def shifted(x, offset, axis):
    n = x.shape[axis]
    return pltpu.roll(x, (-offset) % n, axis)


def transport_kernel(
    mask_ref, pr_ref, wi_ref, te_ref, ob_ref, ln_ref, lp_ref, rt_ref, o_ref, g_ref, coef_ref, plane_ref
):
    k = diffuse
    c0 = 1.0 - 4.0 * diffuse
    probes = o_ref.shape[0]
    rows = o_ref.shape[2]
    lanes = o_ref.shape[3]
    full_rows, full_lanes = plane_ref.shape
    mask = mask_ref[...]

    def masked(f):
        return (f.reshape(full_rows // 8, 8, full_lanes) * mask[None]).reshape(full_rows, full_lanes)

    def assemble(own, plane):
        plane_ref[0:rows, 0:lanes] = own
        plane_ref[rows : rows + HALO, 0:lanes] = ln_ref[0, plane]
        plane_ref[rows + HALO : full_rows, 0:lanes] = lp_ref[0, plane]
        plane_ref[:, lanes:full_lanes] = rt_ref[0, plane]
        return plane_ref[...]

    w_east = assemble(wi_ref[0, 0], probes + 0)
    w_north = assemble(wi_ref[1, 0], probes + 1)
    t_east = assemble(te_ref[0, 0], probes + 2)
    t_north = assemble(te_ref[1, 0], probes + 3)
    for s in range(STEPS):
        east = 0.5 * (w_east + s * t_east)
        north = 0.5 * (w_north + s * t_north)
        coef_ref[s, 0] = k - east
        coef_ref[s, 1] = k + east
        coef_ref[s, 2] = k - north
        coef_ref[s, 3] = k + north
        coef_ref[s, 4] = shifted(k - east, -1, 0)
        coef_ref[s, 5] = shifted(k + east, 1, 0)
        coef_ref[s, 6] = shifted(k - north, -1, 1)
        coef_ref[s, 7] = shifted(k + north, 1, 1)
    coef_ref[STEPS, 0] = assemble(ob_ref[0], probes + 4)

    def one_probe(p, carry):
        f = assemble(pr_ref[p, 0], p)
        for s in range(STEPS):
            f = (
                c0 * f
                + coef_ref[s, 0] * shifted(f, 1, 0)
                + coef_ref[s, 1] * shifted(f, -1, 0)
                + coef_ref[s, 2] * shifted(f, 1, 1)
                + coef_ref[s, 3] * shifted(f, -1, 1)
            )
            f = masked(f)
        f = f * coef_ref[STEPS, 0]
        for s in reversed(range(STEPS)):
            f = (
                c0 * f
                + coef_ref[s, 4] * shifted(f, -1, 0)
                + coef_ref[s, 5] * shifted(f, 1, 0)
                + coef_ref[s, 6] * shifted(f, -1, 1)
                + coef_ref[s, 7] * shifted(f, 1, 1)
            )
            f = masked(f)
        o_ref[p, 0] = f[:rows, :lanes]
        return carry

    lax.fori_loop(0, probes, one_probe, 0)
    for p in range(probes):
        for q in range(p, probes):
            prod = (o_ref[p, 0] * o_ref[q, 0]).reshape(rows // 8, 8, lanes)
            part = jnp.sum(jnp.sum(prod, axis=0), axis=0, keepdims=True)
            g_ref[0, pl.ds(p * probes + q, 1), :] = part
            if q != p:
                g_ref[0, pl.ds(q * probes + p, 1), :] = part


def transport(mask, probes, wind, wind_tend, obs_weight, lon_next, lon_prev, lat_block):
    n_probes, levels, rows, lanes = probes.shape
    planes = lon_next.shape[1]
    full_rows = rows + 2 * HALO
    full_lanes = 2 * lanes

    def level_block(lead):
        return pl.BlockSpec((lead, 1, rows, lanes), lambda l: (0, l, 0, 0))

    def halo_block(height):
        return pl.BlockSpec((1, planes, height, lanes), lambda l: (l, 0, 0, 0))

    return pl.pallas_call(
        transport_kernel,
        grid=(levels,),
        in_specs=[
            pl.BlockSpec((8, full_lanes), lambda l: (0, 0)),
            level_block(n_probes),
            level_block(2),
            level_block(2),
            pl.BlockSpec((1, rows, lanes), lambda l: (l, 0, 0)),
            halo_block(HALO),
            halo_block(HALO),
            halo_block(full_rows),
        ],
        out_specs=[
            level_block(n_probes),
            pl.BlockSpec((1, n_probes * n_probes, lanes), lambda l: (l, 0, 0)),
        ],
        out_shape=[
            jax.ShapeDtypeStruct((n_probes, levels, rows, lanes), jnp.float32),
            jax.ShapeDtypeStruct((levels, n_probes * n_probes, lanes), jnp.float32),
        ],
        scratch_shapes=[
            pltpu.VMEM((STEPS + 1, 8, full_rows, full_lanes), jnp.float32),
            pltpu.VMEM((full_rows, full_lanes), jnp.float32),
        ],
    )(mask, probes, wind, wind_tend, obs_weight, lon_next, lon_prev, lat_block)

def basis_kernel(inv_ref, scale_ref, z_ref, o_ref):
    probes = z_ref.shape[0]
    z = [z_ref[q, 0] for q in range(probes)]
    for p in range(probes):
        acc = inv_ref[p, 0] * z[0]
        for q in range(1, probes):
            acc = acc + inv_ref[p, q] * z[q]
        o_ref[p, 0] = acc * scale_ref[0, 0]


def basis(inverse, scale, field):
    probes, levels, rows, lanes = field.shape
    block = pl.BlockSpec((probes, 1, rows, lanes), lambda l: (0, l, 0, 0))
    return pl.pallas_call(
        basis_kernel,
        grid=(levels,),
        in_specs=[
            pl.BlockSpec(memory_space=pltpu.SMEM),
            pl.BlockSpec(memory_space=pltpu.SMEM),
            block,
        ],
        out_specs=block,
        out_shape=jax.ShapeDtypeStruct(field.shape, jnp.float32),
    )(inverse, scale, field)


def body(probes, wind, wind_tend, obs_weight):
    n_probes, levels, width_lon, width_lat = probes.shape

    def planes_of(part):
        return jnp.concatenate(
            (
                jnp.swapaxes(part(probes), 0, 1),
                jnp.swapaxes(part(wind), 0, 1),
                jnp.swapaxes(part(wind_tend), 0, 1),
                part(obs_weight[None])[0][:, None],
            ),
            axis=1,
        )

    heads = planes_of(lambda a: a[..., :HALO, :])
    tails = planes_of(lambda a: a[..., width_lon - HALO :, :])
    n_lon = lax.axis_size("lon")
    lon_next = lax.ppermute(heads, "lon", [((i + 1) % n_lon, i) for i in range(n_lon)])
    lon_prev = lax.ppermute(tails, "lon", [(i, (i + 1) % n_lon) for i in range(n_lon)])
    own_lo = planes_of(lambda a: a[..., :HALO])
    own_hi = planes_of(lambda a: a[..., width_lat - HALO :])
    edge_lo = jnp.concatenate((own_lo, lon_next[..., :HALO], lon_prev[..., :HALO]), axis=2)
    edge_hi = jnp.concatenate(
        (own_hi, lon_next[..., width_lat - HALO :], lon_prev[..., width_lat - HALO :]), axis=2
    )
    n_lat = lax.axis_size("lat")
    lat_next = lax.ppermute(jnp.swapaxes(edge_lo, 2, 3), "lat", [(j + 1, j) for j in range(n_lat - 1)])
    lat_prev = lax.ppermute(jnp.swapaxes(edge_hi, 2, 3), "lat", [(j, j + 1) for j in range(n_lat - 1)])
    gap = jnp.zeros(edge_lo.shape[:3] + (width_lat - 2 * HALO,), jnp.float32)
    lat_block = jnp.concatenate(
        (jnp.swapaxes(lat_next, 2, 3), gap, jnp.swapaxes(lat_prev, 2, 3)), axis=3
    )
    lanes = 2 * width_lat
    lane = lax.broadcasted_iota(jnp.int32, (8, lanes), 1)
    start = lax.axis_index("lat") * width_lat
    cell = jnp.where(lane < width_lat + HALO, start + lane, start + lane - lanes)
    inside = ((lane < width_lat + HALO) | (lane >= lanes - HALO)) & (cell >= 0)
    inside = inside & (cell < width_lat * n_lat)
    mask = inside.astype(jnp.float32)

    field, partial = transport(
        mask, probes, wind, wind_tend, obs_weight, lon_next, lon_prev, lat_block
    )

    gram = jnp.sum(partial, axis=(0, 2)).reshape(n_probes, n_probes)
    gram = all_sum(gram, ("lon", "lat"))
    lower = jnp.linalg.cholesky(gram)
    upper = lower.T
    cells = field.shape[1] * width_lon * width_lat * lax.axis_size("lat") * lax.axis_size("lon")
    scale = jnp.sqrt(jnp.float32(cells))
    result = basis(lower_inverse(lower), scale.reshape(1, 1), field)
    return (result, upper / scale)


def solution(mesh):
    placed = (
        P(None, None, "lon", "lat"),
        P(None, None, "lon", "lat"),
        P(None, None, "lon", "lat"),
        P(None, "lon", "lat"),
    )
    return jax.shard_map(
        body,
        mesh=mesh,
        in_specs=placed,
        out_specs=(P(None, None, "lon", "lat"), P()),
        check_vma=False,
    )
```

time: 118 us -> 113 us (0.958)
  waiting for transfers between devices: 43.1 us -> 34.1 us
  starting transfers between devices: 18.2 us -> 20.4 us
  other arithmetic: 8.3 us -> 9.64 us
    ppermute x4, waiting for transfers between devices: 12.7 us -> 6.62 us  [the longest x1 5.77 us: body(): lax.ppermute(jnp.swapaxes(edge_hi, 2, 3), 'lat', [(j, j + 1) for j in ran...]
    ppermute x8, starting transfers between devices: 3.8 us -> 6.73 us  [all_sum(): lax.ppermute(value, axis, [(i, i ^ stride) for i in range(count)])]
    ppermute x8, waiting for transfers between devices: 30.4 us -> 27.5 us  [all_sum(): lax.ppermute(value, axis, [(i, i ^ stride) for i in range(count)])]
    another operation x0 -> x4, local copies, waits for them, and re-layouts: none -> 2.55 us  [planes_of(): part(obs_weight[None])[0][:, None]]
    ppermute x2, local copies, waits for them, and re-layouts: 4.48 us -> 2.56 us  [the longest x1 1.94 us: body(): lax.ppermute(jnp.swapaxes(edge_hi, 2, 3), 'lat', [(j, j + 1) for j in ran...]
    slice x3 -> x12, local copies, waits for them, and re-layouts: 6.19 us -> 4.56 us  [the longest x3 2.65 us: body(): tails = planes_of(lambda a: a[..., width_lon - HALO:, :])]
    concatenate x1 -> x3, other arithmetic: 3.81 us -> 4.95 us  [the longest x1 3.56 us: body(): jnp.concatenate((jnp.swapaxes(lat_next, 2, 3), gap, jnp.swapaxes(lat_prev...]
    unnamed x14 -> x21, local copies, waits for them, and re-layouts: 2.72 us -> 3.33 us
  transfers between devices with their start and end apart: 12 -> 12, of which waited for: 12 -> 10; matrix products, arithmetic and copies ran while one was open for 3% -> 7% of each run, Pallas kernels for 0% -> 0%
where the time goes in v4:
time: 113 us; the launch traced here: 112 us
  waiting for transfers between devices  34.1 us (30%)
  Pallas kernels  33.3 us (29%)
  starting transfers between devices  20.4 us (18%)
  local copies, waits for them, and re-layouts  13.3 us (12%)
  other arithmetic  9.64 us (9%)
    pallas_call x1, Pallas kernels, transport(): pl.pallas_call(transport_kernel, grid=(levels,), in_specs=[pl.BlockSpec((...  29.7 us
    ppermute x8, waiting for transfers between devices, all_sum(): lax.ppermute(value, axis, [(i, i ^ stride) for i in range(count)])  27.5 us
    ppermute x8, starting transfers between devices, all_sum(): lax.ppermute(value, axis, [(i, i ^ stride) for i in range(count)])  6.73 us
    ppermute x1, starting transfers between devices, body(): lax.ppermute(heads, 'lon', [((i + 1) % n_lon, i) for i in range(n_lon)])  6.31 us
    ppermute x1, waiting for transfers between devices, body(): lax.ppermute(jnp.swapaxes(edge_hi, 2, 3), 'lat', [(j, j + 1) for j in ran...  5.77 us
    ppermute x1, starting transfers between devices, body(): lax.ppermute(jnp.swapaxes(edge_lo, 2, 3), 'lat', [(j + 1, j) for j in ran...  5.07 us
    pallas_call x1, Pallas kernels, basis(): pl.pallas_call(basis_kernel, grid=(levels,), in_specs=[pl.BlockSpec(memor...  3.66 us
    concatenate x1, other arithmetic, body(): jnp.concatenate((jnp.swapaxes(lat_next, 2, 3), gap, jnp.swapaxes(lat_prev...  3.56 us
  transfers between devices with their start and end apart: 12, of which 10 were waited for; matrix products, arithmetic and copies ran while one was open for 7% of the time, Pallas kernels for 0%

profile of v4, /device:TPU:6, one launch (start us, length us, event | category | flops | bytes accessed | tf_op | source)
XLA Modules:
  0.0 112.5 jit_solution(2779921355532323351)
XLA Ops:
  0.7 0.9 fusion.10
  1.5 0.8 fusion.11
  2.3 0.7 slice_bitcast_fusion.2
  3.0 1.0 fusion.7
  4.1 0.7 pad_maximum_fusion.2
  4.8 0.7 pad_maximum_fusion.1
  5.5 6.3 %collective-permute-start = (f32[4,13,8,128]{3,2,1,0:T(8,128)}, f32[4,13,8,128]{3,2,1,0:T(8,128)S(1)}, u32[]{:S(2)}, u32[]{:S(2)}) collective-permute-start(f32[4,13,8,128]{3,2,1,0:T(8,128)} %pad_maximum_fusion.1), channel_id=1, source_target_pairs={{1,0},{2,1},{3,2},{4,3},{5,4},{6,5},{7,6},{8,7},{9,8},{10,9},{11,1... | collective-permute-start | bytes 638984 | tf_op jit(solution)/shard_map/ppermute | solution.py:191
  11.8 0.7 slice_bitcast_fusion.1
  13.7 0.7 fusion.9
  14.9 1.1 copy.60
  16.0 1.0 copy.43
  18.3 5.1 %collective-permute-start.2 = (f32[4,13,8,80]{3,2,1,0:T(8,128)S(1)}, f32[4,13,8,80]{3,2,1,0:T(8,128)S(1)}, u32[]{:S(2)}, u32[]{:S(2)}) collective-permute-start(f32[4,13,8,80]{3,2,1,0:T(8,128)S(1)} %maximum_bitcast_fusion), channel_id=1, source_target_pairs={{32,0},{64,32},{96,64},{128,96},{160,128},{192,160},{224,192},{33,... | collective-permute-start | bytes 399368 | tf_op jit(solution)/shard_map/ppermute | solution.py:200
  23.8 2.3 %collective-permute-start.3 = (f32[4,13,8,80]{3,2,1,0:T(8,128)S(1)}, f32[4,13,8,80]{3,2,1,0:T(8,128)S(1)}, u32[]{:S(2)}, u32[]{:S(2)}) collective-permute-start(f32[4,13,8,80]{3,2,1,0:T(8,128)S(1)} %maximum_bitcast_fusion.1), channel_id=1, source_target_pairs={{0,32},{32,64},{64,96},{96,128},{128,160},{160,192},{192,224},{1,3... | collective-permute-start | bytes 399368 | tf_op jit(solution)/shard_map/ppermute | solution.py:201
  26.7 0.8 collective-permute-done.2
  28.2 5.8 %collective-permute-done.3 = f32[4,13,8,80]{3,2,1,0:T(8,128)S(1)} collective-permute-done((f32[4,13,8,80]{3,2,1,0:T(8,128)S(1)}, f32[4,13,8,80]{3,2,1,0:T(8,128)S(1)}, u32[]{:S(2)}, u32[]{:S(2)}) %collective-permute-start.3) | collective-permute-done | bytes 133152 | tf_op jit(solution)/shard_map/ppermute | solution.py:201
  34.0 1.9 %copy.46 = f32[4,13,8,80]{2,3,1,0:T(8,128)} copy(f32[4,13,8,80]{3,2,1,0:T(8,128)S(1)} %collective-permute-done.3) | data formatting | bytes 266240 | tf_op jit(solution)/shard_map/ppermute | solution.py:201
  35.9 3.6 %pad_maximum_fusion.rt_ref = f32[4,13,80,128]{3,2,1,0:T(8,128)} fusion(f32[4,13,80,8]{3,2,1,0:T(8,128)} %bitcast.50, f32[4,13,80,8]{3,2,1,0:T(8,128)S(1)} %bitcast.49, f32[128]{0:T(128)S(1)} %pad.1.clone), kind=kLoop, calls=%fused_computation | loop fusion | flops 1064960 | bytes 2396672 | tf_op jit(solution)/shard_map/concatenate | solution.py:203
  39.5 29.7 %shard_map.59 = (f32[8,4,64,128]{3,2,1,0:T(8,128)}, f32[4,64,128]{2,1,0:T(8,128)}) custom-call(f32[8,256]{1,0:T(8,128)} %fusion.2.mask_ref, f32[8,4,64,128]{3,2,1,0:T(8,128)} %pr_ref.1, f32[2,4,64,128]{3,2,1,0:T(8,128)} %wi_ref.1, f32[2,4,64,128]{3,2,1,0:T(8,128)} %te_ref.1, f32[4,64,128]{2,1,0:T(8,128)} %ob_ref.1, f32[4,13,8,128]{3,2,1,0:T(8,128)} %copy-done.4, ...), custom_call_target="tpu_custom_call" | custom-call | tf_op jit(solution)/shard_map/pallas_call | solution.py:121
  69.1 1.0 reduce_sum.9
  70.3 1.2 %collective-permute-done.4 = f32[8,8]{0,1:T(8,128)S(1)} collective-permute-done((f32[8,8]{0,1:T(8,128)S(1)}, f32[8,8]{0,1:T(8,128)S(1)}, u32[]{:S(2)}, u32[]{:S(2)}) %collective-permute-start.4) | collective-permute-done | bytes 288 | tf_op jit(solution)/shard_map/ppermute | solution.py:27
  71.5 3.6 %collective-permute-done.5 = f32[8,8]{0,1:T(8,128)S(1)} collective-permute-done((f32[8,8]{0,1:T(8,128)S(1)}, f32[8,8]{0,1:T(8,128)S(1)}, u32[]{:S(2)}, u32[]{:S(2)}) %collective-permute-start.5) | collective-permute-done | bytes 288 | tf_op jit(solution)/shard_map/ppermute | solution.py:27
  75.1 3.6 %collective-permute-done.6 = f32[8,8]{0,1:T(8,128)S(1)} collective-permute-done((f32[8,8]{0,1:T(8,128)S(1)}, f32[8,8]{0,1:T(8,128)S(1)}, u32[]{:S(2)}, u32[]{:S(2)}) %collective-permute-start.6) | collective-permute-done | bytes 288 | tf_op jit(solution)/shard_map/ppermute | solution.py:27
  78.7 4.5 %collective-permute-done.7 = f32[8,8]{0,1:T(8,128)S(1)} collective-permute-done((f32[8,8]{0,1:T(8,128)S(1)}, f32[8,8]{0,1:T(8,128)S(1)}, u32[]{:S(2)}, u32[]{:S(2)}) %collective-permute-start.7) | collective-permute-done | bytes 288 | tf_op jit(solution)/shard_map/ppermute | solution.py:27
  83.2 5.1 %collective-permute-start.8 = (f32[8,8]{0,1:T(8,128)S(1)}, f32[8,8]{0,1:T(8,128)S(1)}, u32[]{:S(2)}, u32[]{:S(2)}) collective-permute-start(f32[8,8]{0,1:T(8,128)S(1)} %add.51), channel_id=1, source_target_pairs={{0,16},{1,17},{2,18},{3,19},{4,20},{5,21},{6,22},{7,23},{8,24},{9,... | collective-permute-start | bytes 776 | tf_op jit(solution)/shard_map/ppermute | solution.py:27
  88.3 2.4 %collective-permute-done.8 = f32[8,8]{0,1:T(8,128)S(1)} collective-permute-done((f32[8,8]{0,1:T(8,128)S(1)}, f32[8,8]{0,1:T(8,128)S(1)}, u32[]{:S(2)}, u32[]{:S(2)}) %collective-permute-start.8) | collective-permute-done | bytes 288 | tf_op jit(solution)/shard_map/ppermute | solution.py:27
  90.8 5.1 %collective-permute-done.9 = f32[8,8]{0,1:T(8,128)S(1)} collective-permute-done((f32[8,8]{0,1:T(8,128)S(1)}, f32[8,8]{0,1:T(8,128)S(1)}, u32[]{:S(2)}, u32[]{:S(2)}) %collective-permute-start.9) | collective-permute-done | bytes 288 | tf_op jit(solution)/shard_map/ppermute | solution.py:27
  96.4 3.1 %collective-permute-done.10 = f32[8,8]{0,1:T(8,128)S(1)} collective-permute-done((f32[8,8]{0,1:T(8,128)S(1)}, f32[8,8]{0,1:T(8,128)S(1)}, u32[]{:S(2)}, u32[]{:S(2)}) %collective-permute-start.10) | collective-permute-done | bytes 288 | tf_op jit(solution)/shard_map/ppermute | solution.py:27
  99.5 1.1 collective-permute-start.11
  100.6 4.0 %collective-permute-done.11 = f32[8,8]{0,1:T(8,128)S(1)} collective-permute-done((f32[8,8]{0,1:T(8,128)S(1)}, f32[8,8]{0,1:T(8,128)S(1)}, u32[]{:S(2)}, u32[]{:S(2)}) %collective-permute-start.11) | collective-permute-done | bytes 288 | tf_op jit(solution)/shard_map/ppermute | solution.py:27
  104.7 0.7 cholesky.17
  107.4 0.8 fusion.3.inv_ref
  108.8 3.7 %shard_map.60 = f32[8,4,64,128]{3,2,1,0:T(8,128)} custom-call(f32[8,8]{1,0:T(8,128)} %fusion.3.inv_ref, f32[1,1]{1,0:T(1,128)} %constant.65.clone.1.scale_ref, f32[8,4,64,128]{3,2,1,0:T(8,128)} %get-tuple-element.5.z_ref), custom_call_target="tpu_custom_call" | custom-call | tf_op jit(solution)/shard_map/pallas_call | solution.py:161
  (64 shorter events, 8.0 us)
Async XLA Ops:
  0.6 11.2 %copy-start.5 = (f32[4,64,128]{2,1,0:T(8,128)S(1)}, f32[4,64,128]{2,1,0:T(8,128)}, u32[]{:S(2)}) copy-start(f32[4,64,128]{2,1,0:T(8,128)} %ob_ref.1) | copy-start | bytes 393220
  0.6 11.9 %copy-start = (f32[8,4,64,128]{3,2,1,0:T(8,128)S(1)}, f32[8,4,64,128]{3,2,1,0:T(8,128)}, u32[]{:S(2)}) copy-start(f32[8,4,64,128]{3,2,1,0:T(8,128)} %pr_ref.1) | copy-start | bytes 3145732
  4.8 12.9 %collective-permute-start.1 = (f32[4,13,8,128]{3,2,1,0:T(8,128)}, f32[4,13,8,128]{3,2,1,0:T(8,128)S(1)}, u32[]{:S(2)}, u32[]{:S(2)}) collective-permute-start(f32[4,13,8,128]{3,2,1,0:T(8,128)} %pad_maximum_fusion.2), channel_id=1, source_target_pairs={{0,1},{1,2},{2,3},{3,4},{4,5},{5,6},{6,7},{7,8},{8,9},{9,10},{10,1... | collective-permute-start | bytes 638984 | tf_op jit(solution)/shard_map/ppermute | solution.py:192
  5.5 12.4 %collective-permute-start = (f32[4,13,8,128]{3,2,1,0:T(8,128)}, f32[4,13,8,128]{3,2,1,0:T(8,128)S(1)}, u32[]{:S(2)}, u32[]{:S(2)}) collective-permute-start(f32[4,13,8,128]{3,2,1,0:T(8,128)} %pad_maximum_fusion.1), channel_id=1, source_target_pairs={{1,0},{2,1},{3,2},{4,3},{5,4},{6,5},{7,6},{8,7},{9,8},{10,9},{11,1... | collective-permute-start | bytes 638984 | tf_op jit(solution)/shard_map/ppermute | solution.py:191
  12.6 1.0 copy-start.1
  12.6 1.1 copy-start.2
  17.6 6.0 %copy-start.3 = (f32[4,13,8,128]{3,2,1,0:T(8,128)}, f32[4,13,8,128]{3,2,1,0:T(8,128)S(1)}, u32[]{:S(2)}) copy-start(f32[4,13,8,128]{3,2,1,0:T(8,128)S(1)} %collective-permute-done.1.lp_ref) | copy-start | bytes 638980
  17.9 10.3 %copy-start.4 = (f32[4,13,8,128]{3,2,1,0:T(8,128)}, f32[4,13,8,128]{3,2,1,0:T(8,128)S(1)}, u32[]{:S(2)}) copy-start(f32[4,13,8,128]{3,2,1,0:T(8,128)S(1)} %collective-permute-done.ln_ref) | copy-start | bytes 638980
  18.3 9.3 %collective-permute-start.2 = (f32[4,13,8,80]{3,2,1,0:T(8,128)S(1)}, f32[4,13,8,80]{3,2,1,0:T(8,128)S(1)}, u32[]{:S(2)}, u32[]{:S(2)}) collective-permute-start(f32[4,13,8,80]{3,2,1,0:T(8,128)S(1)} %maximum_bitcast_fusion), channel_id=1, source_target_pairs={{32,0},{64,32},{96,64},{128,96},{160,128},{192,160},{224,192},{33,... | collective-permute-start | bytes 399368 | tf_op jit(solution)/shard_map/ppermute | solution.py:200
  23.8 10.1 %collective-permute-start.3 = (f32[4,13,8,80]{3,2,1,0:T(8,128)S(1)}, f32[4,13,8,80]{3,2,1,0:T(8,128)S(1)}, u32[]{:S(2)}, u32[]{:S(2)}) collective-permute-start(f32[4,13,8,80]{3,2,1,0:T(8,128)S(1)} %maximum_bitcast_fusion.1), channel_id=1, source_target_pairs={{0,32},{32,64},{64,96},{96,128},{128,160},{160,192},{192,224},{1,3... | collective-permute-start | bytes 399368 | tf_op jit(solution)/shard_map/ppermute | solution.py:201
  70.3 1.2 %collective-permute-start.4 = (f32[8,8]{0,1:T(8,128)S(1)}, f32[8,8]{0,1:T(8,128)S(1)}, u32[]{:S(2)}, u32[]{:S(2)}) collective-permute-start(f32[8,8]{0,1:T(8,128)S(1)} %copy.48), channel_id=1, source_target_pairs={{0,1},{1,0},{2,3},{3,2},{4,5},{5,4},{6,7},{7,6},{8,9},{9,8},{10,11... | collective-permute-start | bytes 776 | tf_op jit(solution)/shard_map/ppermute | solution.py:27
  71.5 3.6 %collective-permute-start.5 = (f32[8,8]{0,1:T(8,128)S(1)}, f32[8,8]{0,1:T(8,128)S(1)}, u32[]{:S(2)}, u32[]{:S(2)}) collective-permute-start(f32[8,8]{0,1:T(8,128)S(1)} %add.48), channel_id=1, source_target_pairs={{0,2},{1,3},{2,0},{3,1},{4,6},{5,7},{6,4},{7,5},{8,10},{9,11},{10,... | collective-permute-start | bytes 776 | tf_op jit(solution)/shard_map/ppermute | solution.py:27
  75.1 3.6 %collective-permute-start.6 = (f32[8,8]{0,1:T(8,128)S(1)}, f32[8,8]{0,1:T(8,128)S(1)}, u32[]{:S(2)}, u32[]{:S(2)}) collective-permute-start(f32[8,8]{0,1:T(8,128)S(1)} %add.49), channel_id=1, source_target_pairs={{0,4},{1,5},{2,6},{3,7},{4,0},{5,1},{6,2},{7,3},{8,12},{9,13},{10,... | collective-permute-start | bytes 776 | tf_op jit(solution)/shard_map/ppermute | solution.py:27
  78.7 4.5 %collective-permute-start.7 = (f32[8,8]{0,1:T(8,128)S(1)}, f32[8,8]{0,1:T(8,128)S(1)}, u32[]{:S(2)}, u32[]{:S(2)}) collective-permute-start(f32[8,8]{0,1:T(8,128)S(1)} %add.50), channel_id=1, source_target_pairs={{0,8},{1,9},{2,10},{3,11},{4,12},{5,13},{6,14},{7,15},{8,0},{9,1},... | collective-permute-start | bytes 776 | tf_op jit(solution)/shard_map/ppermute | solution.py:27
  83.2 7.5 %collective-permute-start.8 = (f32[8,8]{0,1:T(8,128)S(1)}, f32[8,8]{0,1:T(8,128)S(1)}, u32[]{:S(2)}, u32[]{:S(2)}) collective-permute-start(f32[8,8]{0,1:T(8,128)S(1)} %add.51), channel_id=1, source_target_pairs={{0,16},{1,17},{2,18},{3,19},{4,20},{5,21},{6,22},{7,23},{8,24},{9,... | collective-permute-start | bytes 776 | tf_op jit(solution)/shard_map/ppermute | solution.py:27
  90.8 5.1 %collective-permute-start.9 = (f32[8,8]{0,1:T(8,128)S(1)}, f32[8,8]{0,1:T(8,128)S(1)}, u32[]{:S(2)}, u32[]{:S(2)}) collective-permute-start(f32[8,8]{0,1:T(8,128)S(1)} %add.52), channel_id=1, source_target_pairs={{0,32},{32,0},{64,96},{96,64},{128,160},{160,128},{192,224},{224,1... | collective-permute-start | bytes 776 | tf_op jit(solution)/shard_map/ppermute | solution.py:27
  95.9 3.6 %collective-permute-start.10 = (f32[8,8]{0,1:T(8,128)S(1)}, f32[8,8]{0,1:T(8,128)S(1)}, u32[]{:S(2)}, u32[]{:S(2)}) collective-permute-start(f32[8,8]{0,1:T(8,128)S(1)} %add.53), channel_id=1, source_target_pairs={{0,64},{32,96},{64,0},{96,32},{128,192},{160,224},{192,128},{224,1... | collective-permute-start | bytes 776 | tf_op jit(solution)/shard_map/ppermute | solution.py:27
  99.5 5.1 %collective-permute-start.11 = (f32[8,8]{0,1:T(8,128)S(1)}, f32[8,8]{0,1:T(8,128)S(1)}, u32[]{:S(2)}, u32[]{:S(2)}) collective-permute-start(f32[8,8]{0,1:T(8,128)S(1)} %add.54), channel_id=1, source_target_pairs={{0,128},{32,160},{64,192},{96,224},{128,0},{160,32},{192,64},{224,... | collective-permute-start | bytes 776 | tf_op jit(solution)/shard_map/ppermute | solution.py:27

commit v5 on v4

--- a/solution.py
+++ b/solution.py
@@ -42,18 +42,18 @@
     probes = o_ref.shape[0]
     rows = o_ref.shape[2]
     lanes = o_ref.shape[3]
-    full_rows, full_lanes = plane_ref.shape
+    full_rows, full_lanes = plane_ref.shape[1:]
     mask = mask_ref[...]
 
     def masked(f):
         return (f.reshape(full_rows // 8, 8, full_lanes) * mask[None]).reshape(full_rows, full_lanes)
 
-    def assemble(own, plane):
-        plane_ref[0:rows, 0:lanes] = own
-        plane_ref[rows : rows + HALO, 0:lanes] = ln_ref[0, plane]
-        plane_ref[rows + HALO : full_rows, 0:lanes] = lp_ref[0, plane]
-        plane_ref[:, lanes:full_lanes] = rt_ref[0, plane]
-        return plane_ref[...]
+    def assemble(own, plane, slot=0):
+        plane_ref[slot, 0:rows, 0:lanes] = own
+        plane_ref[slot, rows : rows + HALO, 0:lanes] = ln_ref[0, plane]
+        plane_ref[slot, rows + HALO : full_rows, 0:lanes] = lp_ref[0, plane]
+        plane_ref[slot, :, lanes:full_lanes] = rt_ref[0, plane]
+        return plane_ref[slot]
 
     w_east = assemble(wi_ref[0, 0], probes + 0)
     w_north = assemble(wi_ref[1, 0], probes + 1)
@@ -72,31 +72,40 @@
         coef_ref[s, 7] = shifted(k + north, 1, 1)
     coef_ref[STEPS, 0] = assemble(ob_ref[0], probes + 4)
 
-    def one_probe(p, carry):
-        f = assemble(pr_ref[p, 0], p)
+    def probe_pair(i, carry):
+        p = 2 * i
+        fs = [assemble(pr_ref[p + j, 0], p + j, j) for j in range(2)]
         for s in range(STEPS):
-            f = (
-                c0 * f
-                + coef_ref[s, 0] * shifted(f, 1, 0)
-                + coef_ref[s, 1] * shifted(f, -1, 0)
-                + coef_ref[s, 2] * shifted(f, 1, 1)
-                + coef_ref[s, 3] * shifted(f, -1, 1)
-            )
-            f = masked(f)
-        f = f * coef_ref[STEPS, 0]
+            ce_m, ce_p, cn_m, cn_p = (coef_ref[s, c] for c in range(4))
+            fs = [
+                masked(
+                    c0 * f
+                    + ce_m * shifted(f, 1, 0)
+                    + ce_p * shifted(f, -1, 0)
+                    + cn_m * shifted(f, 1, 1)
+                    + cn_p * shifted(f, -1, 1)
+                )
+                for f in fs
+            ]
+        weight = coef_ref[STEPS, 0]
+        fs = [f * weight for f in fs]
         for s in reversed(range(STEPS)):
-            f = (
-                c0 * f
-                + coef_ref[s, 4] * shifted(f, -1, 0)
-                + coef_ref[s, 5] * shifted(f, 1, 0)
-                + coef_ref[s, 6] * shifted(f, -1, 1)
-                + coef_ref[s, 7] * shifted(f, 1, 1)
-            )
-            f = masked(f)
-        o_ref[p, 0] = f[:rows, :lanes]
+            aw, ae, as_, an = (coef_ref[s, c] for c in range(4, 8))
+            fs = [
+                masked(
+                    c0 * f
+                    + aw * shifted(f, -1, 0)
+                    + ae * shifted(f, 1, 0)
+                    + as_ * shifted(f, -1, 1)
+                    + an * shifted(f, 1, 1)
+                )
+                for f in fs
+            ]
+        for j in range(2):
+            o_ref[p + j, 0] = fs[j][:rows, :lanes]
         return carry
 
-    lax.fori_loop(0, probes, one_probe, 0)
+    lax.fori_loop(0, probes // 2, probe_pair, 0)
     for p in range(probes):
         for q in range(p, probes):
             prod = (o_ref[p, 0] * o_ref[q, 0]).reshape(rows // 8, 8, lanes)
@@ -141,7 +150,7 @@
         ],
         scratch_shapes=[
             pltpu.VMEM((STEPS + 1, 8, full_rows, full_lanes), jnp.float32),
-            pltpu.VMEM((full_rows, full_lanes), jnp.float32),
+            pltpu.VMEM((2, full_rows, full_lanes), jnp.float32),
         ],
     )(mask, probes, wind, wind_tend, obs_weight, lon_next, lon_prev, lat_block)
 

time: 113 us -> 102 us (0.903)
  Pallas kernels: 33.3 us -> 22.1 us
    pallas_call x1, Pallas kernels: 29.7 us -> 18.4 us  [transport(): pl.pallas_call(transport_kernel, grid=(levels,), in_specs=[pl.BlockSpec((...]
  transfers between devices with their start and end apart: 12 -> 12, of which waited for: 10 -> 10; matrix products, arithmetic and copies ran while one was open for 7% -> 8% of each run, Pallas kernels for 0% -> 0%
where the time goes in v5:
time: 102 us; the launch traced here: 101 us
  waiting for transfers between devices  34.1 us (33%)
  Pallas kernels  22.1 us (22%)
  starting transfers between devices  20.4 us (20%)
  local copies, waits for them, and re-layouts  13.3 us (13%)
  other arithmetic  9.64 us (9%)
    ppermute x8, waiting for transfers between devices, all_sum(): lax.ppermute(value, axis, [(i, i ^ stride) for i in range(count)])  27.5 us
    pallas_call x1, Pallas kernels, transport(): pl.pallas_call(transport_kernel, grid=(levels,), in_specs=[pl.BlockSpec((...  18.4 us
    ppermute x8, starting transfers between devices, all_sum(): lax.ppermute(value, axis, [(i, i ^ stride) for i in range(count)])  6.73 us
    ppermute x1, starting transfers between devices, body(): lax.ppermute(heads, 'lon', [((i + 1) % n_lon, i) for i in range(n_lon)])  6.31 us
    ppermute x1, waiting for transfers between devices, body(): lax.ppermute(jnp.swapaxes(edge_hi, 2, 3), 'lat', [(j, j + 1) for j in ran...  5.77 us
    ppermute x1, starting transfers between devices, body(): lax.ppermute(jnp.swapaxes(edge_lo, 2, 3), 'lat', [(j + 1, j) for j in ran...  5.07 us
    pallas_call x1, Pallas kernels, basis(): pl.pallas_call(basis_kernel, grid=(levels,), in_specs=[pl.BlockSpec(memor...  3.66 us
    concatenate x1, other arithmetic, body(): jnp.concatenate((jnp.swapaxes(lat_next, 2, 3), gap, jnp.swapaxes(lat_prev...  3.56 us
  transfers between devices with their start and end apart: 12, of which 10 were waited for; matrix products, arithmetic and copies ran while one was open for 8% of the time, Pallas kernels for 0%

profile of v5, /device:TPU:6, one launch (start us, length us, event | category | flops | bytes accessed | tf_op | source)
XLA Modules:
  0.0 101.3 jit_solution(1041768273395379406)
XLA Ops:
  0.7 0.9 fusion.10
  1.5 0.8 fusion.11
  2.3 0.7 slice_bitcast_fusion.2
  3.0 1.0 fusion.7
  4.1 0.7 pad_maximum_fusion.2
  4.8 0.7 pad_maximum_fusion.1
  5.5 6.3 %collective-permute-start = (f32[4,13,8,128]{3,2,1,0:T(8,128)}, f32[4,13,8,128]{3,2,1,0:T(8,128)S(1)}, u32[]{:S(2)}, u32[]{:S(2)}) collective-permute-start(f32[4,13,8,128]{3,2,1,0:T(8,128)} %pad_maximum_fusion.1), channel_id=1, source_target_pairs={{1,0},{2,1},{3,2},{4,3},{5,4},{6,5},{7,6},{8,7},{9,8},{10,9},{11,1... | collective-permute-start | bytes 638984 | tf_op jit(solution)/shard_map/ppermute | solution.py:200
  11.8 0.7 slice_bitcast_fusion.1
  13.7 0.7 fusion.9
  14.9 1.1 %copy.60 = f32[2,4,64,8]{2,3,0,1:T(8,128)S(1)} copy(f32[2,4,64,8]{3,2,1,0:T(8,128)} %get-tuple-element.16) | data formatting | bytes 32768
  16.0 1.0 copy.43
  18.3 5.1 %collective-permute-start.2 = (f32[4,13,8,80]{3,2,1,0:T(8,128)S(1)}, f32[4,13,8,80]{3,2,1,0:T(8,128)S(1)}, u32[]{:S(2)}, u32[]{:S(2)}) collective-permute-start(f32[4,13,8,80]{3,2,1,0:T(8,128)S(1)} %maximum_bitcast_fusion), channel_id=1, source_target_pairs={{32,0},{64,32},{96,64},{128,96},{160,128},{192,160},{224,192},{33,... | collective-permute-start | bytes 399368 | tf_op jit(solution)/shard_map/ppermute | solution.py:209
  23.8 2.3 %collective-permute-start.3 = (f32[4,13,8,80]{3,2,1,0:T(8,128)S(1)}, f32[4,13,8,80]{3,2,1,0:T(8,128)S(1)}, u32[]{:S(2)}, u32[]{:S(2)}) collective-permute-start(f32[4,13,8,80]{3,2,1,0:T(8,128)S(1)} %maximum_bitcast_fusion.1), channel_id=1, source_target_pairs={{0,32},{32,64},{64,96},{96,128},{128,160},{160,192},{192,224},{1,3... | collective-permute-start | bytes 399368 | tf_op jit(solution)/shard_map/ppermute | solution.py:210
  26.7 0.8 collective-permute-done.2
  28.2 5.8 %collective-permute-done.3 = f32[4,13,8,80]{3,2,1,0:T(8,128)S(1)} collective-permute-done((f32[4,13,8,80]{3,2,1,0:T(8,128)S(1)}, f32[4,13,8,80]{3,2,1,0:T(8,128)S(1)}, u32[]{:S(2)}, u32[]{:S(2)}) %collective-permute-start.3) | collective-permute-done | bytes 133152 | tf_op jit(solution)/shard_map/ppermute | solution.py:210
  34.0 1.9 %copy.46 = f32[4,13,8,80]{2,3,1,0:T(8,128)} copy(f32[4,13,8,80]{3,2,1,0:T(8,128)S(1)} %collective-permute-done.3) | data formatting | bytes 266240 | tf_op jit(solution)/shard_map/ppermute | solution.py:210
  35.9 3.6 %pad_maximum_fusion.rt_ref = f32[4,13,80,128]{3,2,1,0:T(8,128)} fusion(f32[4,13,80,8]{3,2,1,0:T(8,128)} %bitcast.50, f32[4,13,80,8]{3,2,1,0:T(8,128)S(1)} %bitcast.49, f32[128]{0:T(128)S(1)} %pad.1.clone), kind=kLoop, calls=%fused_computation | loop fusion | flops 1064960 | bytes 2396672 | tf_op jit(solution)/shard_map/concatenate | solution.py:212
  39.5 18.4 %shard_map.59 = (f32[8,4,64,128]{3,2,1,0:T(8,128)}, f32[4,64,128]{2,1,0:T(8,128)}) custom-call(f32[8,256]{1,0:T(8,128)} %fusion.2.mask_ref, f32[8,4,64,128]{3,2,1,0:T(8,128)} %pr_ref.1, f32[2,4,64,128]{3,2,1,0:T(8,128)} %wi_ref.1, f32[2,4,64,128]{3,2,1,0:T(8,128)} %te_ref.1, f32[4,64,128]{2,1,0:T(8,128)} %ob_ref.1, f32[4,13,8,128]{3,2,1,0:T(8,128)} %copy-done.4, ...), custom_call_target="tpu_custom_call" | custom-call | tf_op jit(solution)/shard_map/pallas_call | solution.py:130
  57.9 1.0 %reduce_sum.9 = f32[64]{0:T(128)S(1)} reduce(f32[4,64,128]{2,1,0:T(8,128)} %get-tuple-element.4, f32[]{:T(128)} %constant.61.clone.1), dimensions={0,2}, to_apply=%region_0.1 | reduce | flops 32704 | bytes 131332 | tf_op jit(solution)/shard_map/reduce_sum | solution.py:227
  59.1 1.2 %collective-permute-done.4 = f32[8,8]{0,1:T(8,128)S(1)} collective-permute-done((f32[8,8]{0,1:T(8,128)S(1)}, f32[8,8]{0,1:T(8,128)S(1)}, u32[]{:S(2)}, u32[]{:S(2)}) %collective-permute-start.4) | collective-permute-done | bytes 288 | tf_op jit(solution)/shard_map/ppermute | solution.py:27
  60.3 3.6 %collective-permute-done.5 = f32[8,8]{0,1:T(8,128)S(1)} collective-permute-done((f32[8,8]{0,1:T(8,128)S(1)}, f32[8,8]{0,1:T(8,128)S(1)}, u32[]{:S(2)}, u32[]{:S(2)}) %collective-permute-start.5) | collective-permute-done | bytes 288 | tf_op jit(solution)/shard_map/ppermute | solution.py:27
  63.9 3.6 %collective-permute-done.6 = f32[8,8]{0,1:T(8,128)S(1)} collective-permute-done((f32[8,8]{0,1:T(8,128)S(1)}, f32[8,8]{0,1:T(8,128)S(1)}, u32[]{:S(2)}, u32[]{:S(2)}) %collective-permute-start.6) | collective-permute-done | bytes 288 | tf_op jit(solution)/shard_map/ppermute | solution.py:27
  67.5 4.5 %collective-permute-done.7 = f32[8,8]{0,1:T(8,128)S(1)} collective-permute-done((f32[8,8]{0,1:T(8,128)S(1)}, f32[8,8]{0,1:T(8,128)S(1)}, u32[]{:S(2)}, u32[]{:S(2)}) %collective-permute-start.7) | collective-permute-done | bytes 288 | tf_op jit(solution)/shard_map/ppermute | solution.py:27
  72.0 5.1 %collective-permute-start.8 = (f32[8,8]{0,1:T(8,128)S(1)}, f32[8,8]{0,1:T(8,128)S(1)}, u32[]{:S(2)}, u32[]{:S(2)}) collective-permute-start(f32[8,8]{0,1:T(8,128)S(1)} %add.51), channel_id=1, source_target_pairs={{0,16},{1,17},{2,18},{3,19},{4,20},{5,21},{6,22},{7,23},{8,24},{9,... | collective-permute-start | bytes 776 | tf_op jit(solution)/shard_map/ppermute | solution.py:27
  77.1 2.4 %collective-permute-done.8 = f32[8,8]{0,1:T(8,128)S(1)} collective-permute-done((f32[8,8]{0,1:T(8,128)S(1)}, f32[8,8]{0,1:T(8,128)S(1)}, u32[]{:S(2)}, u32[]{:S(2)}) %collective-permute-start.8) | collective-permute-done | bytes 288 | tf_op jit(solution)/shard_map/ppermute | solution.py:27
  79.5 5.1 %collective-permute-done.9 = f32[8,8]{0,1:T(8,128)S(1)} collective-permute-done((f32[8,8]{0,1:T(8,128)S(1)}, f32[8,8]{0,1:T(8,128)S(1)}, u32[]{:S(2)}, u32[]{:S(2)}) %collective-permute-start.9) | collective-permute-done | bytes 288 | tf_op jit(solution)/shard_map/ppermute | solution.py:27
  85.2 3.1 %collective-permute-done.10 = f32[8,8]{0,1:T(8,128)S(1)} collective-permute-done((f32[8,8]{0,1:T(8,128)S(1)}, f32[8,8]{0,1:T(8,128)S(1)}, u32[]{:S(2)}, u32[]{:S(2)}) %collective-permute-start.10) | collective-permute-done | bytes 288 | tf_op jit(solution)/shard_map/ppermute | solution.py:27
  88.3 1.1 %collective-permute-start.11 = (f32[8,8]{0,1:T(8,128)S(1)}, f32[8,8]{0,1:T(8,128)S(1)}, u32[]{:S(2)}, u32[]{:S(2)}) collective-permute-start(f32[8,8]{0,1:T(8,128)S(1)} %add.54), channel_id=1, source_target_pairs={{0,128},{32,160},{64,192},{96,224},{128,0},{160,32},{192,64},{224,... | collective-permute-start | bytes 776 | tf_op jit(solution)/shard_map/ppermute | solution.py:27
  89.4 4.0 %collective-permute-done.11 = f32[8,8]{0,1:T(8,128)S(1)} collective-permute-done((f32[8,8]{0,1:T(8,128)S(1)}, f32[8,8]{0,1:T(8,128)S(1)}, u32[]{:S(2)}, u32[]{:S(2)}) %collective-permute-start.11) | collective-permute-done | bytes 288 | tf_op jit(solution)/shard_map/ppermute | solution.py:27
  93.5 0.7 cholesky.17
  96.1 0.8 fusion.3.inv_ref
  97.6 3.7 %shard_map.60 = f32[8,4,64,128]{3,2,1,0:T(8,128)} custom-call(f32[8,8]{1,0:T(8,128)} %fusion.3.inv_ref, f32[1,1]{1,0:T(1,128)} %constant.65.clone.1.scale_ref, f32[8,4,64,128]{3,2,1,0:T(8,128)} %get-tuple-element.5.z_ref), custom_call_target="tpu_custom_call" | custom-call | tf_op jit(solution)/shard_map/pallas_call | solution.py:170
  (64 shorter events, 8.0 us)
Async XLA Ops:
  0.6 11.2 %copy-start.5 = (f32[4,64,128]{2,1,0:T(8,128)S(1)}, f32[4,64,128]{2,1,0:T(8,128)}, u32[]{:S(2)}) copy-start(f32[4,64,128]{2,1,0:T(8,128)} %ob_ref.1) | copy-start | bytes 393220
  0.6 11.9 %copy-start = (f32[8,4,64,128]{3,2,1,0:T(8,128)S(1)}, f32[8,4,64,128]{3,2,1,0:T(8,128)}, u32[]{:S(2)}) copy-start(f32[8,4,64,128]{3,2,1,0:T(8,128)} %pr_ref.1) | copy-start | bytes 3145732
  4.8 12.9 %collective-permute-start.1 = (f32[4,13,8,128]{3,2,1,0:T(8,128)}, f32[4,13,8,128]{3,2,1,0:T(8,128)S(1)}, u32[]{:S(2)}, u32[]{:S(2)}) collective-permute-start(f32[4,13,8,128]{3,2,1,0:T(8,128)} %pad_maximum_fusion.2), channel_id=1, source_target_pairs={{0,1},{1,2},{2,3},{3,4},{4,5},{5,6},{6,7},{7,8},{8,9},{9,10},{10,1... | collective-permute-start | bytes 638984 | tf_op jit(solution)/shard_map/ppermute | solution.py:201
  5.5 12.4 %collective-permute-start = (f32[4,13,8,128]{3,2,1,0:T(8,128)}, f32[4,13,8,128]{3,2,1,0:T(8,128)S(1)}, u32[]{:S(2)}, u32[]{:S(2)}) collective-permute-start(f32[4,13,8,128]{3,2,1,0:T(8,128)} %pad_maximum_fusion.1), channel_id=1, source_target_pairs={{1,0},{2,1},{3,2},{4,3},{5,4},{6,5},{7,6},{8,7},{9,8},{10,9},{11,1... | collective-permute-start | bytes 638984 | tf_op jit(solution)/shard_map/ppermute | solution.py:200
  12.6 1.0 copy-start.1
  12.6 1.1 %copy-start.2 = (f32[2,4,64,128]{3,2,1,0:T(8,128)S(1)}, f32[2,4,64,128]{3,2,1,0:T(8,128)}, u32[]{:S(2)}) copy-start(f32[2,4,64,128]{3,2,1,0:T(8,128)} %te_ref.1) | copy-start | bytes 786436
  17.6 6.0 %copy-start.3 = (f32[4,13,8,128]{3,2,1,0:T(8,128)}, f32[4,13,8,128]{3,2,1,0:T(8,128)S(1)}, u32[]{:S(2)}) copy-start(f32[4,13,8,128]{3,2,1,0:T(8,128)S(1)} %collective-permute-done.1.lp_ref) | copy-start | bytes 638980
  17.9 10.3 %copy-start.4 = (f32[4,13,8,128]{3,2,1,0:T(8,128)}, f32[4,13,8,128]{3,2,1,0:T(8,128)S(1)}, u32[]{:S(2)}) copy-start(f32[4,13,8,128]{3,2,1,0:T(8,128)S(1)} %collective-permute-done.ln_ref) | copy-start | bytes 638980
  18.3 9.3 %collective-permute-start.2 = (f32[4,13,8,80]{3,2,1,0:T(8,128)S(1)}, f32[4,13,8,80]{3,2,1,0:T(8,128)S(1)}, u32[]{:S(2)}, u32[]{:S(2)}) collective-permute-start(f32[4,13,8,80]{3,2,1,0:T(8,128)S(1)} %maximum_bitcast_fusion), channel_id=1, source_target_pairs={{32,0},{64,32},{96,64},{128,96},{160,128},{192,160},{224,192},{33,... | collective-permute-start | bytes 399368 | tf_op jit(solution)/shard_map/ppermute | solution.py:209
  23.8 10.1 %collective-permute-start.3 = (f32[4,13,8,80]{3,2,1,0:T(8,128)S(1)}, f32[4,13,8,80]{3,2,1,0:T(8,128)S(1)}, u32[]{:S(2)}, u32[]{:S(2)}) collective-permute-start(f32[4,13,8,80]{3,2,1,0:T(8,128)S(1)} %maximum_bitcast_fusion.1), channel_id=1, source_target_pairs={{0,32},{32,64},{64,96},{96,128},{128,160},{160,192},{192,224},{1,3... | collective-permute-start | bytes 399368 | tf_op jit(solution)/shard_map/ppermute | solution.py:210
  59.1 1.2 %collective-permute-start.4 = (f32[8,8]{0,1:T(8,128)S(1)}, f32[8,8]{0,1:T(8,128)S(1)}, u32[]{:S(2)}, u32[]{:S(2)}) collective-permute-start(f32[8,8]{0,1:T(8,128)S(1)} %copy.48), channel_id=1, source_target_pairs={{0,1},{1,0},{2,3},{3,2},{4,5},{5,4},{6,7},{7,6},{8,9},{9,8},{10,11... | collective-permute-start | bytes 776 | tf_op jit(solution)/shard_map/ppermute | solution.py:27
  60.3 3.6 %collective-permute-start.5 = (f32[8,8]{0,1:T(8,128)S(1)}, f32[8,8]{0,1:T(8,128)S(1)}, u32[]{:S(2)}, u32[]{:S(2)}) collective-permute-start(f32[8,8]{0,1:T(8,128)S(1)} %add.48), channel_id=1, source_target_pairs={{0,2},{1,3},{2,0},{3,1},{4,6},{5,7},{6,4},{7,5},{8,10},{9,11},{10,... | collective-permute-start | bytes 776 | tf_op jit(solution)/shard_map/ppermute | solution.py:27
  63.9 3.6 %collective-permute-start.6 = (f32[8,8]{0,1:T(8,128)S(1)}, f32[8,8]{0,1:T(8,128)S(1)}, u32[]{:S(2)}, u32[]{:S(2)}) collective-permute-start(f32[8,8]{0,1:T(8,128)S(1)} %add.49), channel_id=1, source_target_pairs={{0,4},{1,5},{2,6},{3,7},{4,0},{5,1},{6,2},{7,3},{8,12},{9,13},{10,... | collective-permute-start | bytes 776 | tf_op jit(solution)/shard_map/ppermute | solution.py:27
  67.5 4.5 %collective-permute-start.7 = (f32[8,8]{0,1:T(8,128)S(1)}, f32[8,8]{0,1:T(8,128)S(1)}, u32[]{:S(2)}, u32[]{:S(2)}) collective-permute-start(f32[8,8]{0,1:T(8,128)S(1)} %add.50), channel_id=1, source_target_pairs={{0,8},{1,9},{2,10},{3,11},{4,12},{5,13},{6,14},{7,15},{8,0},{9,1},... | collective-permute-start | bytes 776 | tf_op jit(solution)/shard_map/ppermute | solution.py:27
  72.0 7.5 %collective-permute-start.8 = (f32[8,8]{0,1:T(8,128)S(1)}, f32[8,8]{0,1:T(8,128)S(1)}, u32[]{:S(2)}, u32[]{:S(2)}) collective-permute-start(f32[8,8]{0,1:T(8,128)S(1)} %add.51), channel_id=1, source_target_pairs={{0,16},{1,17},{2,18},{3,19},{4,20},{5,21},{6,22},{7,23},{8,24},{9,... | collective-permute-start | bytes 776 | tf_op jit(solution)/shard_map/ppermute | solution.py:27
  79.5 5.1 %collective-permute-start.9 = (f32[8,8]{0,1:T(8,128)S(1)}, f32[8,8]{0,1:T(8,128)S(1)}, u32[]{:S(2)}, u32[]{:S(2)}) collective-permute-start(f32[8,8]{0,1:T(8,128)S(1)} %add.52), channel_id=1, source_target_pairs={{0,32},{32,0},{64,96},{96,64},{128,160},{160,128},{192,224},{224,1... | collective-permute-start | bytes 776 | tf_op jit(solution)/shard_map/ppermute | solution.py:27
  84.7 3.6 %collective-permute-start.10 = (f32[8,8]{0,1:T(8,128)S(1)}, f32[8,8]{0,1:T(8,128)S(1)}, u32[]{:S(2)}, u32[]{:S(2)}) collective-permute-start(f32[8,8]{0,1:T(8,128)S(1)} %add.53), channel_id=1, source_target_pairs={{0,64},{32,96},{64,0},{96,32},{128,192},{160,224},{192,128},{224,1... | collective-permute-start | bytes 776 | tf_op jit(solution)/shard_map/ppermute | solution.py:27
  88.3 5.1 %collective-permute-start.11 = (f32[8,8]{0,1:T(8,128)S(1)}, f32[8,8]{0,1:T(8,128)S(1)}, u32[]{:S(2)}, u32[]{:S(2)}) collective-permute-start(f32[8,8]{0,1:T(8,128)S(1)} %add.54), channel_id=1, source_target_pairs={{0,128},{32,160},{64,192},{96,224},{128,0},{160,32},{192,64},{224,... | collective-permute-start | bytes 776 | tf_op jit(solution)/shard_map/ppermute | solution.py:27

commit v6 on v5

--- a/solution.py
+++ b/solution.py
@@ -7,6 +7,7 @@
 
 STEPS = 4
 HALO = 2 * STEPS
+GROUP = 4
 
 diffuse = 0.24
 
@@ -73,8 +74,8 @@
     coef_ref[STEPS, 0] = assemble(ob_ref[0], probes + 4)
 
     def probe_pair(i, carry):
-        p = 2 * i
-        fs = [assemble(pr_ref[p + j, 0], p + j, j) for j in range(2)]
+        p = GROUP * i
+        fs = [assemble(pr_ref[p + j, 0], p + j, j) for j in range(GROUP)]
         for s in range(STEPS):
             ce_m, ce_p, cn_m, cn_p = (coef_ref[s, c] for c in range(4))
             fs = [
@@ -101,11 +102,11 @@
                 )
                 for f in fs
             ]
-        for j in range(2):
+        for j in range(GROUP):
             o_ref[p + j, 0] = fs[j][:rows, :lanes]
         return carry
 
-    lax.fori_loop(0, probes // 2, probe_pair, 0)
+    lax.fori_loop(0, probes // GROUP, probe_pair, 0)
     for p in range(probes):
         for q in range(p, probes):
             prod = (o_ref[p, 0] * o_ref[q, 0]).reshape(rows // 8, 8, lanes)
@@ -150,7 +151,7 @@
         ],
         scratch_shapes=[
             pltpu.VMEM((STEPS + 1, 8, full_rows, full_lanes), jnp.float32),
-            pltpu.VMEM((2, full_rows, full_lanes), jnp.float32),
+            pltpu.VMEM((GROUP, full_rows, full_lanes), jnp.float32),
         ],
     )(mask, probes, wind, wind_tend, obs_weight, lon_next, lon_prev, lat_block)
 

time: 102 us -> 99.6 us (0.976)
  Pallas kernels: 22.1 us -> 19.9 us
    pallas_call x1, Pallas kernels: 18.4 us -> 16.3 us  [transport(): pl.pallas_call(transport_kernel, grid=(levels,), in_specs=[pl.BlockSpec((...]
where the time goes in v6:
time: 99.6 us; the launch traced here: 99.1 us
  waiting for transfers between devices  34.1 us (34%)
  starting transfers between devices  20.4 us (20%)
  Pallas kernels  19.9 us (20%)
  local copies, waits for them, and re-layouts  13.3 us (13%)
  other arithmetic  9.64 us (10%)
    ppermute x8, waiting for transfers between devices, all_sum(): lax.ppermute(value, axis, [(i, i ^ stride) for i in range(count)])  27.5 us
    pallas_call x1, Pallas kernels, transport(): pl.pallas_call(transport_kernel, grid=(levels,), in_specs=[pl.BlockSpec((...  16.3 us
    ppermute x8, starting transfers between devices, all_sum(): lax.ppermute(value, axis, [(i, i ^ stride) for i in range(count)])  6.73 us
    ppermute x1, starting transfers between devices, body(): lax.ppermute(heads, 'lon', [((i + 1) % n_lon, i) for i in range(n_lon)])  6.31 us
    ppermute x1, waiting for transfers between devices, body(): lax.ppermute(jnp.swapaxes(edge_hi, 2, 3), 'lat', [(j, j + 1) for j in ran...  5.77 us
    ppermute x1, starting transfers between devices, body(): lax.ppermute(jnp.swapaxes(edge_lo, 2, 3), 'lat', [(j + 1, j) for j in ran...  5.07 us
    pallas_call x1, Pallas kernels, basis(): pl.pallas_call(basis_kernel, grid=(levels,), in_specs=[pl.BlockSpec(memor...  3.66 us
    concatenate x1, other arithmetic, body(): jnp.concatenate((jnp.swapaxes(lat_next, 2, 3), gap, jnp.swapaxes(lat_prev...  3.56 us
  transfers between devices with their start and end apart: 12, of which 10 were waited for; matrix products, arithmetic and copies ran while one was open for 8% of the time, Pallas kernels for 0%

profile of v6, /device:TPU:6, one launch (start us, length us, event | category | flops | bytes accessed | tf_op | source)
XLA Modules:
  0.0 99.1 jit_solution(899303979219971343)
XLA Ops:
  0.7 0.9 fusion.10
  1.5 0.8 fusion.11
  2.3 0.7 slice_bitcast_fusion.2
  3.0 1.0 fusion.7
  4.1 0.7 pad_maximum_fusion.2
  4.8 0.7 pad_maximum_fusion.1
  5.5 6.3 %collective-permute-start = (f32[4,13,8,128]{3,2,1,0:T(8,128)}, f32[4,13,8,128]{3,2,1,0:T(8,128)S(1)}, u32[]{:S(2)}, u32[]{:S(2)}) collective-permute-start(f32[4,13,8,128]{3,2,1,0:T(8,128)} %pad_maximum_fusion.1), channel_id=1, source_target_pairs={{1,0},{2,1},{3,2},{4,3},{5,4},{6,5},{7,6},{8,7},{9,8},{10,9},{11,1... | collective-permute-start | bytes 638984 | tf_op jit(solution)/shard_map/ppermute | solution.py:201
  11.8 0.7 slice_bitcast_fusion.1
  13.7 0.7 fusion.9
  14.9 1.1 %copy.60 = f32[2,4,64,8]{2,3,0,1:T(8,128)S(1)} copy(f32[2,4,64,8]{3,2,1,0:T(8,128)} %get-tuple-element.16) | data formatting | bytes 32768
  16.0 1.0 copy.43
  18.3 5.1 %collective-permute-start.2 = (f32[4,13,8,80]{3,2,1,0:T(8,128)S(1)}, f32[4,13,8,80]{3,2,1,0:T(8,128)S(1)}, u32[]{:S(2)}, u32[]{:S(2)}) collective-permute-start(f32[4,13,8,80]{3,2,1,0:T(8,128)S(1)} %maximum_bitcast_fusion), channel_id=1, source_target_pairs={{32,0},{64,32},{96,64},{128,96},{160,128},{192,160},{224,192},{33,... | collective-permute-start | bytes 399368 | tf_op jit(solution)/shard_map/ppermute | solution.py:210
  23.8 2.3 %collective-permute-start.3 = (f32[4,13,8,80]{3,2,1,0:T(8,128)S(1)}, f32[4,13,8,80]{3,2,1,0:T(8,128)S(1)}, u32[]{:S(2)}, u32[]{:S(2)}) collective-permute-start(f32[4,13,8,80]{3,2,1,0:T(8,128)S(1)} %maximum_bitcast_fusion.1), channel_id=1, source_target_pairs={{0,32},{32,64},{64,96},{96,128},{128,160},{160,192},{192,224},{1,3... | collective-permute-start | bytes 399368 | tf_op jit(solution)/shard_map/ppermute | solution.py:211
  26.7 0.8 collective-permute-done.2
  28.2 5.8 %collective-permute-done.3 = f32[4,13,8,80]{3,2,1,0:T(8,128)S(1)} collective-permute-done((f32[4,13,8,80]{3,2,1,0:T(8,128)S(1)}, f32[4,13,8,80]{3,2,1,0:T(8,128)S(1)}, u32[]{:S(2)}, u32[]{:S(2)}) %collective-permute-start.3) | collective-permute-done | bytes 133152 | tf_op jit(solution)/shard_map/ppermute | solution.py:211
  34.0 1.9 %copy.46 = f32[4,13,8,80]{2,3,1,0:T(8,128)} copy(f32[4,13,8,80]{3,2,1,0:T(8,128)S(1)} %collective-permute-done.3) | data formatting | bytes 266240 | tf_op jit(solution)/shard_map/ppermute | solution.py:211
  35.9 3.6 %pad_maximum_fusion.rt_ref = f32[4,13,80,128]{3,2,1,0:T(8,128)} fusion(f32[4,13,80,8]{3,2,1,0:T(8,128)} %bitcast.50, f32[4,13,80,8]{3,2,1,0:T(8,128)S(1)} %bitcast.49, f32[128]{0:T(128)S(1)} %pad.1.clone), kind=kLoop, calls=%fused_computation | loop fusion | flops 1064960 | bytes 2396672 | tf_op jit(solution)/shard_map/concatenate | solution.py:213
  39.5 16.3 %shard_map.59 = (f32[8,4,64,128]{3,2,1,0:T(8,128)}, f32[4,64,128]{2,1,0:T(8,128)}) custom-call(f32[8,256]{1,0:T(8,128)} %fusion.2.mask_ref, f32[8,4,64,128]{3,2,1,0:T(8,128)} %pr_ref.1, f32[2,4,64,128]{3,2,1,0:T(8,128)} %wi_ref.1, f32[2,4,64,128]{3,2,1,0:T(8,128)} %te_ref.1, f32[4,64,128]{2,1,0:T(8,128)} %ob_ref.1, f32[4,13,8,128]{3,2,1,0:T(8,128)} %copy-done.4, ...), custom_call_target="tpu_custom_call" | custom-call | tf_op jit(solution)/shard_map/pallas_call | solution.py:131
  55.8 1.0 %reduce_sum.9 = f32[64]{0:T(128)S(1)} reduce(f32[4,64,128]{2,1,0:T(8,128)} %get-tuple-element.4, f32[]{:T(128)} %constant.61.clone.1), dimensions={0,2}, to_apply=%region_0.1 | reduce | flops 32704 | bytes 131332 | tf_op jit(solution)/shard_map/reduce_sum | solution.py:228
  57.0 1.2 %collective-permute-done.4 = f32[8,8]{0,1:T(8,128)S(1)} collective-permute-done((f32[8,8]{0,1:T(8,128)S(1)}, f32[8,8]{0,1:T(8,128)S(1)}, u32[]{:S(2)}, u32[]{:S(2)}) %collective-permute-start.4) | collective-permute-done | bytes 288 | tf_op jit(solution)/shard_map/ppermute | solution.py:28
  58.1 3.6 %collective-permute-done.5 = f32[8,8]{0,1:T(8,128)S(1)} collective-permute-done((f32[8,8]{0,1:T(8,128)S(1)}, f32[8,8]{0,1:T(8,128)S(1)}, u32[]{:S(2)}, u32[]{:S(2)}) %collective-permute-start.5) | collective-permute-done | bytes 288 | tf_op jit(solution)/shard_map/ppermute | solution.py:28
  61.8 3.6 %collective-permute-done.6 = f32[8,8]{0,1:T(8,128)S(1)} collective-permute-done((f32[8,8]{0,1:T(8,128)S(1)}, f32[8,8]{0,1:T(8,128)S(1)}, u32[]{:S(2)}, u32[]{:S(2)}) %collective-permute-start.6) | collective-permute-done | bytes 288 | tf_op jit(solution)/shard_map/ppermute | solution.py:28
  65.4 4.5 %collective-permute-done.7 = f32[8,8]{0,1:T(8,128)S(1)} collective-permute-done((f32[8,8]{0,1:T(8,128)S(1)}, f32[8,8]{0,1:T(8,128)S(1)}, u32[]{:S(2)}, u32[]{:S(2)}) %collective-permute-start.7) | collective-permute-done | bytes 288 | tf_op jit(solution)/shard_map/ppermute | solution.py:28
  69.9 5.1 %collective-permute-start.8 = (f32[8,8]{0,1:T(8,128)S(1)}, f32[8,8]{0,1:T(8,128)S(1)}, u32[]{:S(2)}, u32[]{:S(2)}) collective-permute-start(f32[8,8]{0,1:T(8,128)S(1)} %add.51), channel_id=1, source_target_pairs={{0,16},{1,17},{2,18},{3,19},{4,20},{5,21},{6,22},{7,23},{8,24},{9,... | collective-permute-start | bytes 776 | tf_op jit(solution)/shard_map/ppermute | solution.py:28
  74.9 2.4 %collective-permute-done.8 = f32[8,8]{0,1:T(8,128)S(1)} collective-permute-done((f32[8,8]{0,1:T(8,128)S(1)}, f32[8,8]{0,1:T(8,128)S(1)}, u32[]{:S(2)}, u32[]{:S(2)}) %collective-permute-start.8) | collective-permute-done | bytes 288 | tf_op jit(solution)/shard_map/ppermute | solution.py:28
  77.4 5.1 %collective-permute-done.9 = f32[8,8]{0,1:T(8,128)S(1)} collective-permute-done((f32[8,8]{0,1:T(8,128)S(1)}, f32[8,8]{0,1:T(8,128)S(1)}, u32[]{:S(2)}, u32[]{:S(2)}) %collective-permute-start.9) | collective-permute-done | bytes 288 | tf_op jit(solution)/shard_map/ppermute | solution.py:28
  83.0 3.1 %collective-permute-done.10 = f32[8,8]{0,1:T(8,128)S(1)} collective-permute-done((f32[8,8]{0,1:T(8,128)S(1)}, f32[8,8]{0,1:T(8,128)S(1)}, u32[]{:S(2)}, u32[]{:S(2)}) %collective-permute-start.10) | collective-permute-done | bytes 288 | tf_op jit(solution)/shard_map/ppermute | solution.py:28
  86.1 1.1 %collective-permute-start.11 = (f32[8,8]{0,1:T(8,128)S(1)}, f32[8,8]{0,1:T(8,128)S(1)}, u32[]{:S(2)}, u32[]{:S(2)}) collective-permute-start(f32[8,8]{0,1:T(8,128)S(1)} %add.54), channel_id=1, source_target_pairs={{0,128},{32,160},{64,192},{96,224},{128,0},{160,32},{192,64},{224,... | collective-permute-start | bytes 776 | tf_op jit(solution)/shard_map/ppermute | solution.py:28
  87.2 4.0 %collective-permute-done.11 = f32[8,8]{0,1:T(8,128)S(1)} collective-permute-done((f32[8,8]{0,1:T(8,128)S(1)}, f32[8,8]{0,1:T(8,128)S(1)}, u32[]{:S(2)}, u32[]{:S(2)}) %collective-permute-start.11) | collective-permute-done | bytes 288 | tf_op jit(solution)/shard_map/ppermute | solution.py:28
  91.3 0.7 cholesky.17
  94.0 0.8 fusion.3.inv_ref
  95.5 3.7 %shard_map.60 = f32[8,4,64,128]{3,2,1,0:T(8,128)} custom-call(f32[8,8]{1,0:T(8,128)} %fusion.3.inv_ref, f32[1,1]{1,0:T(1,128)} %constant.65.clone.1.scale_ref, f32[8,4,64,128]{3,2,1,0:T(8,128)} %get-tuple-element.5.z_ref), custom_call_target="tpu_custom_call" | custom-call | tf_op jit(solution)/shard_map/pallas_call | solution.py:171
  (64 shorter events, 8.0 us)
Async XLA Ops:
  0.6 11.2 %copy-start.5 = (f32[4,64,128]{2,1,0:T(8,128)S(1)}, f32[4,64,128]{2,1,0:T(8,128)}, u32[]{:S(2)}) copy-start(f32[4,64,128]{2,1,0:T(8,128)} %ob_ref.1) | copy-start | bytes 393220
  0.6 11.9 %copy-start = (f32[8,4,64,128]{3,2,1,0:T(8,128)S(1)}, f32[8,4,64,128]{3,2,1,0:T(8,128)}, u32[]{:S(2)}) copy-start(f32[8,4,64,128]{3,2,1,0:T(8,128)} %pr_ref.1) | copy-start | bytes 3145732
  4.8 12.9 %collective-permute-start.1 = (f32[4,13,8,128]{3,2,1,0:T(8,128)}, f32[4,13,8,128]{3,2,1,0:T(8,128)S(1)}, u32[]{:S(2)}, u32[]{:S(2)}) collective-permute-start(f32[4,13,8,128]{3,2,1,0:T(8,128)} %pad_maximum_fusion.2), channel_id=1, source_target_pairs={{0,1},{1,2},{2,3},{3,4},{4,5},{5,6},{6,7},{7,8},{8,9},{9,10},{10,1... | collective-permute-start | bytes 638984 | tf_op jit(solution)/shard_map/ppermute | solution.py:202
  5.5 12.4 %collective-permute-start = (f32[4,13,8,128]{3,2,1,0:T(8,128)}, f32[4,13,8,128]{3,2,1,0:T(8,128)S(1)}, u32[]{:S(2)}, u32[]{:S(2)}) collective-permute-start(f32[4,13,8,128]{3,2,1,0:T(8,128)} %pad_maximum_fusion.1), channel_id=1, source_target_pairs={{1,0},{2,1},{3,2},{4,3},{5,4},{6,5},{7,6},{8,7},{9,8},{10,9},{11,1... | collective-permute-start | bytes 638984 | tf_op jit(solution)/shard_map/ppermute | solution.py:201
  12.6 1.0 copy-start.1
  12.6 1.1 %copy-start.2 = (f32[2,4,64,128]{3,2,1,0:T(8,128)S(1)}, f32[2,4,64,128]{3,2,1,0:T(8,128)}, u32[]{:S(2)}) copy-start(f32[2,4,64,128]{3,2,1,0:T(8,128)} %te_ref.1) | copy-start | bytes 786436
  17.6 6.0 %copy-start.3 = (f32[4,13,8,128]{3,2,1,0:T(8,128)}, f32[4,13,8,128]{3,2,1,0:T(8,128)S(1)}, u32[]{:S(2)}) copy-start(f32[4,13,8,128]{3,2,1,0:T(8,128)S(1)} %collective-permute-done.1.lp_ref) | copy-start | bytes 638980
  17.9 10.3 %copy-start.4 = (f32[4,13,8,128]{3,2,1,0:T(8,128)}, f32[4,13,8,128]{3,2,1,0:T(8,128)S(1)}, u32[]{:S(2)}) copy-start(f32[4,13,8,128]{3,2,1,0:T(8,128)S(1)} %collective-permute-done.ln_ref) | copy-start | bytes 638980
  18.3 9.3 %collective-permute-start.2 = (f32[4,13,8,80]{3,2,1,0:T(8,128)S(1)}, f32[4,13,8,80]{3,2,1,0:T(8,128)S(1)}, u32[]{:S(2)}, u32[]{:S(2)}) collective-permute-start(f32[4,13,8,80]{3,2,1,0:T(8,128)S(1)} %maximum_bitcast_fusion), channel_id=1, source_target_pairs={{32,0},{64,32},{96,64},{128,96},{160,128},{192,160},{224,192},{33,... | collective-permute-start | bytes 399368 | tf_op jit(solution)/shard_map/ppermute | solution.py:210
  23.8 10.1 %collective-permute-start.3 = (f32[4,13,8,80]{3,2,1,0:T(8,128)S(1)}, f32[4,13,8,80]{3,2,1,0:T(8,128)S(1)}, u32[]{:S(2)}, u32[]{:S(2)}) collective-permute-start(f32[4,13,8,80]{3,2,1,0:T(8,128)S(1)} %maximum_bitcast_fusion.1), channel_id=1, source_target_pairs={{0,32},{32,64},{64,96},{96,128},{128,160},{160,192},{192,224},{1,3... | collective-permute-start | bytes 399368 | tf_op jit(solution)/shard_map/ppermute | solution.py:211
  57.0 1.2 %collective-permute-start.4 = (f32[8,8]{0,1:T(8,128)S(1)}, f32[8,8]{0,1:T(8,128)S(1)}, u32[]{:S(2)}, u32[]{:S(2)}) collective-permute-start(f32[8,8]{0,1:T(8,128)S(1)} %copy.48), channel_id=1, source_target_pairs={{0,1},{1,0},{2,3},{3,2},{4,5},{5,4},{6,7},{7,6},{8,9},{9,8},{10,11... | collective-permute-start | bytes 776 | tf_op jit(solution)/shard_map/ppermute | solution.py:28
  58.1 3.6 %collective-permute-start.5 = (f32[8,8]{0,1:T(8,128)S(1)}, f32[8,8]{0,1:T(8,128)S(1)}, u32[]{:S(2)}, u32[]{:S(2)}) collective-permute-start(f32[8,8]{0,1:T(8,128)S(1)} %add.48), channel_id=1, source_target_pairs={{0,2},{1,3},{2,0},{3,1},{4,6},{5,7},{6,4},{7,5},{8,10},{9,11},{10,... | collective-permute-start | bytes 776 | tf_op jit(solution)/shard_map/ppermute | solution.py:28
  61.8 3.6 %collective-permute-start.6 = (f32[8,8]{0,1:T(8,128)S(1)}, f32[8,8]{0,1:T(8,128)S(1)}, u32[]{:S(2)}, u32[]{:S(2)}) collective-permute-start(f32[8,8]{0,1:T(8,128)S(1)} %add.49), channel_id=1, source_target_pairs={{0,4},{1,5},{2,6},{3,7},{4,0},{5,1},{6,2},{7,3},{8,12},{9,13},{10,... | collective-permute-start | bytes 776 | tf_op jit(solution)/shard_map/ppermute | solution.py:28
  65.4 4.5 %collective-permute-start.7 = (f32[8,8]{0,1:T(8,128)S(1)}, f32[8,8]{0,1:T(8,128)S(1)}, u32[]{:S(2)}, u32[]{:S(2)}) collective-permute-start(f32[8,8]{0,1:T(8,128)S(1)} %add.50), channel_id=1, source_target_pairs={{0,8},{1,9},{2,10},{3,11},{4,12},{5,13},{6,14},{7,15},{8,0},{9,1},... | collective-permute-start | bytes 776 | tf_op jit(solution)/shard_map/ppermute | solution.py:28
  69.9 7.5 %collective-permute-start.8 = (f32[8,8]{0,1:T(8,128)S(1)}, f32[8,8]{0,1:T(8,128)S(1)}, u32[]{:S(2)}, u32[]{:S(2)}) collective-permute-start(f32[8,8]{0,1:T(8,128)S(1)} %add.51), channel_id=1, source_target_pairs={{0,16},{1,17},{2,18},{3,19},{4,20},{5,21},{6,22},{7,23},{8,24},{9,... | collective-permute-start | bytes 776 | tf_op jit(solution)/shard_map/ppermute | solution.py:28
  77.4 5.1 %collective-permute-start.9 = (f32[8,8]{0,1:T(8,128)S(1)}, f32[8,8]{0,1:T(8,128)S(1)}, u32[]{:S(2)}, u32[]{:S(2)}) collective-permute-start(f32[8,8]{0,1:T(8,128)S(1)} %add.52), channel_id=1, source_target_pairs={{0,32},{32,0},{64,96},{96,64},{128,160},{160,128},{192,224},{224,1... | collective-permute-start | bytes 776 | tf_op jit(solution)/shard_map/ppermute | solution.py:28
  82.5 3.6 %collective-permute-start.10 = (f32[8,8]{0,1:T(8,128)S(1)}, f32[8,8]{0,1:T(8,128)S(1)}, u32[]{:S(2)}, u32[]{:S(2)}) collective-permute-start(f32[8,8]{0,1:T(8,128)S(1)} %add.53), channel_id=1, source_target_pairs={{0,64},{32,96},{64,0},{96,32},{128,192},{160,224},{192,128},{224,1... | collective-permute-start | bytes 776 | tf_op jit(solution)/shard_map/ppermute | solution.py:28
  86.1 5.1 %collective-permute-start.11 = (f32[8,8]{0,1:T(8,128)S(1)}, f32[8,8]{0,1:T(8,128)S(1)}, u32[]{:S(2)}, u32[]{:S(2)}) collective-permute-start(f32[8,8]{0,1:T(8,128)S(1)} %add.54), channel_id=1, source_target_pairs={{0,128},{32,160},{64,192},{96,224},{128,0},{160,32},{192,64},{224,... | collective-permute-start | bytes 776 | tf_op jit(solution)/shard_map/ppermute | solution.py:28

commit v7 on v6

--- a/solution.py
+++ b/solution.py
@@ -36,7 +36,7 @@
 
 
 def transport_kernel(
-    mask_ref, pr_ref, wi_ref, te_ref, ob_ref, ln_ref, lp_ref, rt_ref, o_ref, g_ref, coef_ref, plane_ref
+    mask_ref, pr_ref, wi_ref, te_ref, ob_ref, ln_ref, lp_ref, un_ref, up_ref, o_ref, g_ref, coef_ref, plane_ref
 ):
     k = diffuse
     c0 = 1.0 - 4.0 * diffuse
@@ -53,7 +53,9 @@
         plane_ref[slot, 0:rows, 0:lanes] = own
         plane_ref[slot, rows : rows + HALO, 0:lanes] = ln_ref[0, plane]
         plane_ref[slot, rows + HALO : full_rows, 0:lanes] = lp_ref[0, plane]
-        plane_ref[slot, :, lanes:full_lanes] = rt_ref[0, plane]
+        gap = jnp.zeros((lanes - 2 * HALO, lanes), jnp.float32)
+        halo = jnp.concatenate((un_ref[0, plane], gap, up_ref[0, plane]), axis=0)
+        plane_ref[slot, :, lanes:full_lanes] = halo.T[:full_rows]
         return plane_ref[slot]
 
     w_east = assemble(wi_ref[0, 0], probes + 0)
@@ -116,7 +118,7 @@
                 g_ref[0, pl.ds(q * probes + p, 1), :] = part
 
 
-def transport(mask, probes, wind, wind_tend, obs_weight, lon_next, lon_prev, lat_block):
+def transport(mask, probes, wind, wind_tend, obs_weight, lon_next, lon_prev, lat_next, lat_prev):
     n_probes, levels, rows, lanes = probes.shape
     planes = lon_next.shape[1]
     full_rows = rows + 2 * HALO
@@ -139,7 +141,8 @@
             pl.BlockSpec((1, rows, lanes), lambda l: (l, 0, 0)),
             halo_block(HALO),
             halo_block(HALO),
-            halo_block(full_rows),
+            halo_block(HALO),
+            halo_block(HALO),
         ],
         out_specs=[
             level_block(n_probes),
@@ -153,16 +156,23 @@
             pltpu.VMEM((STEPS + 1, 8, full_rows, full_lanes), jnp.float32),
             pltpu.VMEM((GROUP, full_rows, full_lanes), jnp.float32),
         ],
-    )(mask, probes, wind, wind_tend, obs_weight, lon_next, lon_prev, lat_block)
+    )(mask, probes, wind, wind_tend, obs_weight, lon_next, lon_prev, lat_next, lat_prev)
 
 def basis_kernel(inv_ref, scale_ref, z_ref, o_ref):
     probes = z_ref.shape[0]
-    z = [z_ref[q, 0] for q in range(probes)]
-    for p in range(probes):
-        acc = inv_ref[p, 0] * z[0]
-        for q in range(1, probes):
-            acc = acc + inv_ref[p, q] * z[q]
-        o_ref[p, 0] = acc * scale_ref[0, 0]
+    scale = scale_ref[0, 0]
+
+    def chunk(c, carry):
+        rows = pl.ds(c * 8, 8)
+        z = [z_ref[q, 0, rows, :] for q in range(probes)]
+        for p in range(probes):
+            acc = inv_ref[p, 0] * z[0]
+            for q in range(1, probes):
+                acc = acc + inv_ref[p, q] * z[q]
+            o_ref[p, 0, rows, :] = acc * scale
+        return carry
+
+    lax.fori_loop(0, z_ref.shape[2] // 8, chunk, 0)
 
 
 def basis(inverse, scale, field):
@@ -202,17 +212,14 @@
     lon_prev = lax.ppermute(tails, "lon", [(i, (i + 1) % n_lon) for i in range(n_lon)])
     own_lo = planes_of(lambda a: a[..., :HALO])
     own_hi = planes_of(lambda a: a[..., width_lat - HALO :])
-    edge_lo = jnp.concatenate((own_lo, lon_next[..., :HALO], lon_prev[..., :HALO]), axis=2)
+    fill = jnp.zeros(own_lo.shape[:2] + (width_lat - width_lon - 2 * HALO, HALO), jnp.float32)
+    edge_lo = jnp.concatenate((own_lo, lon_next[..., :HALO], lon_prev[..., :HALO], fill), axis=2)
     edge_hi = jnp.concatenate(
-        (own_hi, lon_next[..., width_lat - HALO :], lon_prev[..., width_lat - HALO :]), axis=2
+        (own_hi, lon_next[..., width_lat - HALO :], lon_prev[..., width_lat - HALO :], fill), axis=2
     )
     n_lat = lax.axis_size("lat")
     lat_next = lax.ppermute(jnp.swapaxes(edge_lo, 2, 3), "lat", [(j + 1, j) for j in range(n_lat - 1)])
     lat_prev = lax.ppermute(jnp.swapaxes(edge_hi, 2, 3), "lat", [(j, j + 1) for j in range(n_lat - 1)])
-    gap = jnp.zeros(edge_lo.shape[:3] + (width_lat - 2 * HALO,), jnp.float32)
-    lat_block = jnp.concatenate(
-        (jnp.swapaxes(lat_next, 2, 3), gap, jnp.swapaxes(lat_prev, 2, 3)), axis=3
-    )
     lanes = 2 * width_lat
     lane = lax.broadcasted_iota(jnp.int32, (8, lanes), 1)
     start = lax.axis_index("lat") * width_lat
@@ -222,7 +229,7 @@
     mask = inside.astype(jnp.float32)
 
     field, partial = transport(
-        mask, probes, wind, wind_tend, obs_weight, lon_next, lon_prev, lat_block
+        mask, probes, wind, wind_tend, obs_weight, lon_next, lon_prev, lat_next, lat_prev
     )
 
     gram = jnp.sum(partial, axis=(0, 2)).reshape(n_probes, n_probes)

time: 99.6 us -> 95.2 us (0.956)
  other arithmetic: 9.64 us -> 6.03 us
  local copies, waits for them, and re-layouts: 13.3 us -> 11 us
  starting transfers between devices: 20.4 us -> 21.7 us
  Pallas kernels: 19.9 us -> 20.9 us
    concatenate x1 -> x0, other arithmetic: 3.56 us -> none  [body(): jnp.concatenate((jnp.swapaxes(lat_next, 2, 3), gap, jnp.swapaxes(lat_prev...]
    ppermute x2 -> x0, local copies, waits for them, and re-layouts: 2.56 us -> none  [the longest x1 1.94 us: body(): lax.ppermute(jnp.swapaxes(edge_hi, 2, 3), 'lat', [(j, j + 1) for j in ran...]
    unnamed x21 -> x28, local copies, waits for them, and re-layouts: 3.33 us -> 5.02 us
    another operation x4, local copies, waits for them, and re-layouts: 2.55 us -> 1.06 us  [planes_of(): part(obs_weight[None])[0][:, None]]
    ppermute x8, waiting for transfers between devices: 27.5 us -> 26.2 us  [all_sum(): lax.ppermute(value, axis, [(i, i ^ stride) for i in range(count)])]
    ppermute x8, starting transfers between devices: 6.73 us -> 8.05 us  [all_sum(): lax.ppermute(value, axis, [(i, i ^ stride) for i in range(count)])]
    slice x7 -> x3, local copies, waits for them, and re-layouts: 1.69 us -> 0.63 us  [body(): own_hi = planes_of(lambda a: a[..., width_lat - HALO:])]
    slice x1, local copies, waits for them, and re-layouts: 0.11 us -> 1.15 us  [body(): lon_prev[..., width_lat - HALO:]]
  transfers between devices with their start and end apart: 12 -> 12, of which waited for: 10 -> 10; matrix products, arithmetic and copies ran while one was open for 8% -> 6% of each run, Pallas kernels for 0% -> 0%
where the time goes in v7:
time: 95.2 us; the launch traced here: 94.7 us
  waiting for transfers between devices  33.4 us (35%)
  starting transfers between devices  21.7 us (23%)
  Pallas kernels  20.9 us (22%)
  local copies, waits for them, and re-layouts  11 us (12%)
  other arithmetic  6.03 us (6%)
    ppermute x8, waiting for transfers between devices, all_sum(): lax.ppermute(value, axis, [(i, i ^ stride) for i in range(count)])  26.2 us
    pallas_call x1, Pallas kernels, transport(): pl.pallas_call(transport_kernel, grid=(levels,), in_specs=[pl.BlockSpec((...  17 us
    ppermute x8, starting transfers between devices, all_sum(): lax.ppermute(value, axis, [(i, i ^ stride) for i in range(count)])  8.05 us
    ppermute x1, starting transfers between devices, body(): lax.ppermute(heads, 'lon', [((i + 1) % n_lon, i) for i in range(n_lon)])  6.31 us
    ppermute x1, waiting for transfers between devices, body(): lax.ppermute(jnp.swapaxes(edge_hi, 2, 3), 'lat', [(j, j + 1) for j in ran...  5.98 us
    ppermute x1, starting transfers between devices, body(): lax.ppermute(jnp.swapaxes(edge_lo, 2, 3), 'lat', [(j + 1, j) for j in ran...  5.07 us
    unnamed x28, local copies, waits for them, and re-layouts  5.02 us
    pallas_call x1, Pallas kernels, basis(): pl.pallas_call(basis_kernel, grid=(levels,), in_specs=[pl.BlockSpec(memor...  3.9 us
  transfers between devices with their start and end apart: 12, of which 10 were waited for; matrix products, arithmetic and copies ran while one was open for 6% of the time, Pallas kernels for 0%

profile of v7, /device:TPU:6, one launch (start us, length us, event | category | flops | bytes accessed | tf_op | source)
XLA Modules:
  0.0 94.7 jit_solution(856288685402461475)
XLA Ops:
  0.7 0.9 fusion.10
  1.5 0.8 fusion.11
  3.3 0.7 pad_maximum_fusion.1
  4.2 0.7 pad_maximum_fusion
  4.9 6.3 %collective-permute-start = (f32[4,13,8,128]{3,2,1,0:T(8,128)}, f32[4,13,8,128]{3,2,1,0:T(8,128)}, u32[]{:S(2)}, u32[]{:S(2)}) collective-permute-start(f32[4,13,8,128]{3,2,1,0:T(8,128)} %pad_maximum_fusion), channel_id=1, source_target_pairs={{1,0},{2,1},{3,2},{4,3},{5,4},{6,5},{7,6},{8,7},{9,8},{10,9},{11,1... | collective-permute-start | bytes 638984 | tf_op jit(solution)/shard_map/ppermute | solution.py:211
  12.2 0.8 copy-done.2
  14.4 0.7 slice_bitcast_fusion.2
  15.2 1.1 %fusion.13 = (f32[4,13,8,8]{3,2,1,0:T(8,128)S(1)}, f32[4,13,8,8]{3,2,1,0:T(8,128)S(1)}) fusion(f32[4,13,8,128]{3,2,1,0:T(8,128)} %collective-permute-done.1.lp_ref), kind=kLoop, calls=%fused_computation.41 | loop fusion | bytes 53248 | tf_op jit(solution)/shard_map/slice | solution.py:218
  16.6 1.1 %fusion.12 = (f32[4,13,8,8]{3,2,1,0:T(8,128)S(1)}, f32[4,13,8,8]{3,2,1,0:T(8,128)S(1)}) fusion(f32[4,13,8,128]{3,2,1,0:T(8,128)} %collective-permute-done.ln_ref), kind=kLoop, calls=%fused_computation.40 | loop fusion | bytes 53248 | tf_op jit(solution)/shard_map/slice | solution.py:218
  18.3 5.1 %collective-permute-start.2 = (f32[4,13,8,128]{3,2,1,0:T(8,128)S(1)}, f32[4,13,8,128]{3,2,1,0:T(8,128)S(1)}, u32[]{:S(2)}, u32[]{:S(2)}) collective-permute-start(f32[4,13,8,128]{3,2,1,0:T(8,128)S(1)} %get-tuple-element.33), channel_id=1, source_target_pairs={{32,0},{64,32},{96,64},{128,96},{160,128},{192,160},{224,192},{33,... | collective-permute-start | bytes 638984 | tf_op jit(solution)/shard_map/ppermute | solution.py:221
  23.4 2.3 %collective-permute-start.3 = (f32[4,13,8,128]{3,2,1,0:T(8,128)S(1)}, f32[4,13,8,128]{3,2,1,0:T(8,128)S(1)}, u32[]{:S(2)}, u32[]{:S(2)}) collective-permute-start(f32[4,13,8,128]{3,2,1,0:T(8,128)S(1)} %get-tuple-element.32), channel_id=1, source_target_pairs={{0,32},{32,64},{64,96},{96,128},{128,160},{160,192},{192,224},{1,3... | collective-permute-start | bytes 638984 | tf_op jit(solution)/shard_map/ppermute | solution.py:222
  26.3 1.3 %collective-permute-done.2.un_ref = f32[4,13,8,128]{3,2,1,0:T(8,128)S(1)} collective-permute-done((f32[4,13,8,128]{3,2,1,0:T(8,128)S(1)}, f32[4,13,8,128]{3,2,1,0:T(8,128)S(1)}, u32[]{:S(2)}, u32[]{:S(2)}) %collective-permute-start.2) | collective-permute-done | bytes 213024 | tf_op jit(solution)/shard_map/ppermute | solution.py:221
  27.5 6.0 %collective-permute-done.3.up_ref = f32[4,13,8,128]{3,2,1,0:T(8,128)S(1)} collective-permute-done((f32[4,13,8,128]{3,2,1,0:T(8,128)S(1)}, f32[4,13,8,128]{3,2,1,0:T(8,128)S(1)}, u32[]{:S(2)}, u32[]{:S(2)}) %collective-permute-start.3) | collective-permute-done | bytes 213024 | tf_op jit(solution)/shard_map/ppermute | solution.py:222
  33.5 0.7 copy-done.6
  34.2 17.0 %shard_map.59 = (f32[8,4,64,128]{3,2,1,0:T(8,128)}, f32[4,64,128]{2,1,0:T(8,128)}) custom-call(f32[8,256]{1,0:T(8,128)} %fusion.2.mask_ref, f32[8,4,64,128]{3,2,1,0:T(8,128)} %pr_ref.1, f32[2,4,64,128]{3,2,1,0:T(8,128)} %wi_ref.1, f32[2,4,64,128]{3,2,1,0:T(8,128)} %te_ref.1, f32[4,64,128]{2,1,0:T(8,128)} %ob_ref.1, ...), custom_call_target="tpu_custom_call" | custom-call | tf_op jit(solution)/shard_map/pallas_call | solution.py:133
  51.1 1.0 %reduce_sum.9 = f32[64]{0:T(128)S(1)} reduce(f32[4,64,128]{2,1,0:T(8,128)} %get-tuple-element.4, f32[]{:T(128)} %constant.61.clone.1), dimensions={0,2}, to_apply=%region_0.1 | reduce | flops 32704 | bytes 131332 | tf_op jit(solution)/shard_map/reduce_sum | solution.py:235
  52.3 1.2 %collective-permute-done.4 = f32[8,8]{0,1:T(8,128)S(1)} collective-permute-done((f32[8,8]{0,1:T(8,128)S(1)}, f32[8,8]{0,1:T(8,128)S(1)}, u32[]{:S(2)}, u32[]{:S(2)}) %collective-permute-start.4) | collective-permute-done | bytes 288 | tf_op jit(solution)/shard_map/ppermute | solution.py:28
  53.5 3.6 %collective-permute-done.5 = f32[8,8]{0,1:T(8,128)S(1)} collective-permute-done((f32[8,8]{0,1:T(8,128)S(1)}, f32[8,8]{0,1:T(8,128)S(1)}, u32[]{:S(2)}, u32[]{:S(2)}) %collective-permute-start.5) | collective-permute-done | bytes 288 | tf_op jit(solution)/shard_map/ppermute | solution.py:28
  57.1 3.6 %collective-permute-done.6 = f32[8,8]{0,1:T(8,128)S(1)} collective-permute-done((f32[8,8]{0,1:T(8,128)S(1)}, f32[8,8]{0,1:T(8,128)S(1)}, u32[]{:S(2)}, u32[]{:S(2)}) %collective-permute-start.6) | collective-permute-done | bytes 288 | tf_op jit(solution)/shard_map/ppermute | solution.py:28
  61.4 3.9 %collective-permute-done.7 = f32[8,8]{0,1:T(8,128)S(1)} collective-permute-done((f32[8,8]{0,1:T(8,128)S(1)}, f32[8,8]{0,1:T(8,128)S(1)}, u32[]{:S(2)}, u32[]{:S(2)}) %collective-permute-start.7) | collective-permute-done | bytes 288 | tf_op jit(solution)/shard_map/ppermute | solution.py:28
  65.2 5.8 %collective-permute-start.8 = (f32[8,8]{0,1:T(8,128)S(1)}, f32[8,8]{0,1:T(8,128)S(1)}, u32[]{:S(2)}, u32[]{:S(2)}) collective-permute-start(f32[8,8]{0,1:T(8,128)S(1)} %add.51), channel_id=1, source_target_pairs={{0,16},{1,17},{2,18},{3,19},{4,20},{5,21},{6,22},{7,23},{8,24},{9,... | collective-permute-start | bytes 776 | tf_op jit(solution)/shard_map/ppermute | solution.py:28
  71.0 1.8 %collective-permute-done.8 = f32[8,8]{0,1:T(8,128)S(1)} collective-permute-done((f32[8,8]{0,1:T(8,128)S(1)}, f32[8,8]{0,1:T(8,128)S(1)}, u32[]{:S(2)}, u32[]{:S(2)}) %collective-permute-start.8) | collective-permute-done | bytes 288 | tf_op jit(solution)/shard_map/ppermute | solution.py:28
  72.8 5.1 %collective-permute-done.9 = f32[8,8]{0,1:T(8,128)S(1)} collective-permute-done((f32[8,8]{0,1:T(8,128)S(1)}, f32[8,8]{0,1:T(8,128)S(1)}, u32[]{:S(2)}, u32[]{:S(2)}) %collective-permute-start.9) | collective-permute-done | bytes 288 | tf_op jit(solution)/shard_map/ppermute | solution.py:28
  78.4 3.1 %collective-permute-done.10 = f32[8,8]{0,1:T(8,128)S(1)} collective-permute-done((f32[8,8]{0,1:T(8,128)S(1)}, f32[8,8]{0,1:T(8,128)S(1)}, u32[]{:S(2)}, u32[]{:S(2)}) %collective-permute-start.10) | collective-permute-done | bytes 288 | tf_op jit(solution)/shard_map/ppermute | solution.py:28
  81.5 1.1 %collective-permute-start.11 = (f32[8,8]{0,1:T(8,128)S(1)}, f32[8,8]{0,1:T(8,128)S(1)}, u32[]{:S(2)}, u32[]{:S(2)}) collective-permute-start(f32[8,8]{0,1:T(8,128)S(1)} %add.54), channel_id=1, source_target_pairs={{0,128},{32,160},{64,192},{96,224},{128,0},{160,32},{192,64},{224,... | collective-permute-start | bytes 776 | tf_op jit(solution)/shard_map/ppermute | solution.py:28
  82.6 4.0 %collective-permute-done.11 = f32[8,8]{0,1:T(8,128)S(1)} collective-permute-done((f32[8,8]{0,1:T(8,128)S(1)}, f32[8,8]{0,1:T(8,128)S(1)}, u32[]{:S(2)}, u32[]{:S(2)}) %collective-permute-start.11) | collective-permute-done | bytes 288 | tf_op jit(solution)/shard_map/ppermute | solution.py:28
  86.7 0.7 cholesky.17
  87.4 0.6 compare_reduce_fusion
  88.1 0.6 multiply_bitcast_fusion
  89.4 0.8 fusion.3.inv_ref
  90.1 0.7 copy.53
  90.8 3.9 %shard_map.60 = f32[8,4,64,128]{3,2,1,0:T(8,128)} custom-call(f32[8,8]{1,0:T(8,128)} %fusion.3.inv_ref, f32[1,1]{1,0:T(1,128)} %constant.65.clone.1.scale_ref, f32[8,4,64,128]{3,2,1,0:T(8,128)} %get-tuple-element.5.z_ref), custom_call_target="tpu_custom_call" | custom-call | tf_op jit(solution)/shard_map/pallas_call | solution.py:181
  (63 shorter events, 7.0 us)
Async XLA Ops:
  0.6 1.7 %copy-start.4 = (f32[4,64,128]{2,1,0:T(8,128)S(1)}, f32[4,64,128]{2,1,0:T(8,128)}, u32[]{:S(2)}) copy-start(f32[4,64,128]{2,1,0:T(8,128)} %ob_ref.1) | copy-start | bytes 393220
  0.6 2.6 %copy-start = (f32[8,4,64,128]{3,2,1,0:T(8,128)S(1)}, f32[8,4,64,128]{3,2,1,0:T(8,128)}, u32[]{:S(2)}) copy-start(f32[8,4,64,128]{3,2,1,0:T(8,128)} %pr_ref.1) | copy-start | bytes 3145732
  2.4 0.7 copy-start.3
  4.0 11.1 %collective-permute-start.1 = (f32[4,13,8,128]{3,2,1,0:T(8,128)}, f32[4,13,8,128]{3,2,1,0:T(8,128)}, u32[]{:S(2)}, u32[]{:S(2)}) collective-permute-start(f32[4,13,8,128]{3,2,1,0:T(8,128)} %pad_maximum_fusion.1), channel_id=1, source_target_pairs={{0,1},{1,2},{2,3},{3,4},{4,5},{5,6},{6,7},{7,8},{8,9},{9,10},{10,1... | collective-permute-start | bytes 638984 | tf_op jit(solution)/shard_map/ppermute | solution.py:212
  4.9 11.7 %collective-permute-start = (f32[4,13,8,128]{3,2,1,0:T(8,128)}, f32[4,13,8,128]{3,2,1,0:T(8,128)}, u32[]{:S(2)}, u32[]{:S(2)}) collective-permute-start(f32[4,13,8,128]{3,2,1,0:T(8,128)} %pad_maximum_fusion), channel_id=1, source_target_pairs={{1,0},{2,1},{3,2},{4,3},{5,4},{6,5},{7,6},{8,7},{9,8},{10,9},{11,1... | collective-permute-start | bytes 638984 | tf_op jit(solution)/shard_map/ppermute | solution.py:211
  11.2 0.9 %copy-start.1 = (f32[2,4,64,128]{3,2,1,0:T(8,128)S(1)}, f32[2,4,64,128]{3,2,1,0:T(8,128)}, u32[]{:S(2)}) copy-start(f32[2,4,64,128]{3,2,1,0:T(8,128)} %wi_ref.1) | copy-start | bytes 786436
  12.1 0.9 %copy-start.2 = (f32[2,4,64,128]{3,2,1,0:T(8,128)S(1)}, f32[2,4,64,128]{3,2,1,0:T(8,128)}, u32[]{:S(2)}) copy-start(f32[2,4,64,128]{3,2,1,0:T(8,128)} %te_ref.1) | copy-start | bytes 786436
  18.3 9.2 %collective-permute-start.2 = (f32[4,13,8,128]{3,2,1,0:T(8,128)S(1)}, f32[4,13,8,128]{3,2,1,0:T(8,128)S(1)}, u32[]{:S(2)}, u32[]{:S(2)}) collective-permute-start(f32[4,13,8,128]{3,2,1,0:T(8,128)S(1)} %get-tuple-element.33), channel_id=1, source_target_pairs={{32,0},{64,32},{96,64},{128,96},{160,128},{192,160},{224,192},{33,... | collective-permute-start | bytes 638984 | tf_op jit(solution)/shard_map/ppermute | solution.py:221
  23.4 10.1 %collective-permute-start.3 = (f32[4,13,8,128]{3,2,1,0:T(8,128)S(1)}, f32[4,13,8,128]{3,2,1,0:T(8,128)S(1)}, u32[]{:S(2)}, u32[]{:S(2)}) collective-permute-start(f32[4,13,8,128]{3,2,1,0:T(8,128)S(1)} %get-tuple-element.32), channel_id=1, source_target_pairs={{0,32},{32,64},{64,96},{96,128},{128,160},{160,192},{192,224},{1,3... | collective-permute-start | bytes 638984 | tf_op jit(solution)/shard_map/ppermute | solution.py:222
  27.5 6.0 %copy-start.5 = (f32[4,13,8,128]{3,2,1,0:T(8,128)}, f32[4,13,8,128]{3,2,1,0:T(8,128)S(1)}, u32[]{:S(2)}) copy-start(f32[4,13,8,128]{3,2,1,0:T(8,128)S(1)} %collective-permute-done.2.un_ref) | copy-start | bytes 638980
  33.5 0.7 copy-start.6
  52.3 1.2 %collective-permute-start.4 = (f32[8,8]{0,1:T(8,128)S(1)}, f32[8,8]{0,1:T(8,128)S(1)}, u32[]{:S(2)}, u32[]{:S(2)}) collective-permute-start(f32[8,8]{0,1:T(8,128)S(1)} %copy.50), channel_id=1, source_target_pairs={{0,1},{1,0},{2,3},{3,2},{4,5},{5,4},{6,7},{7,6},{8,9},{9,8},{10,11... | collective-permute-start | bytes 776 | tf_op jit(solution)/shard_map/ppermute | solution.py:28
  53.5 3.6 %collective-permute-start.5 = (f32[8,8]{0,1:T(8,128)S(1)}, f32[8,8]{0,1:T(8,128)S(1)}, u32[]{:S(2)}, u32[]{:S(2)}) collective-permute-start(f32[8,8]{0,1:T(8,128)S(1)} %add.48), channel_id=1, source_target_pairs={{0,2},{1,3},{2,0},{3,1},{4,6},{5,7},{6,4},{7,5},{8,10},{9,11},{10,... | collective-permute-start | bytes 776 | tf_op jit(solution)/shard_map/ppermute | solution.py:28
  57.1 3.6 %collective-permute-start.6 = (f32[8,8]{0,1:T(8,128)S(1)}, f32[8,8]{0,1:T(8,128)S(1)}, u32[]{:S(2)}, u32[]{:S(2)}) collective-permute-start(f32[8,8]{0,1:T(8,128)S(1)} %add.49), channel_id=1, source_target_pairs={{0,4},{1,5},{2,6},{3,7},{4,0},{5,1},{6,2},{7,3},{8,12},{9,13},{10,... | collective-permute-start | bytes 776 | tf_op jit(solution)/shard_map/ppermute | solution.py:28
  60.7 4.5 %collective-permute-start.7 = (f32[8,8]{0,1:T(8,128)S(1)}, f32[8,8]{0,1:T(8,128)S(1)}, u32[]{:S(2)}, u32[]{:S(2)}) collective-permute-start(f32[8,8]{0,1:T(8,128)S(1)} %add.50), channel_id=1, source_target_pairs={{0,8},{1,9},{2,10},{3,11},{4,12},{5,13},{6,14},{7,15},{8,0},{9,1},... | collective-permute-start | bytes 776 | tf_op jit(solution)/shard_map/ppermute | solution.py:28
  65.2 7.5 %collective-permute-start.8 = (f32[8,8]{0,1:T(8,128)S(1)}, f32[8,8]{0,1:T(8,128)S(1)}, u32[]{:S(2)}, u32[]{:S(2)}) collective-permute-start(f32[8,8]{0,1:T(8,128)S(1)} %add.51), channel_id=1, source_target_pairs={{0,16},{1,17},{2,18},{3,19},{4,20},{5,21},{6,22},{7,23},{8,24},{9,... | collective-permute-start | bytes 776 | tf_op jit(solution)/shard_map/ppermute | solution.py:28
  72.8 5.1 %collective-permute-start.9 = (f32[8,8]{0,1:T(8,128)S(1)}, f32[8,8]{0,1:T(8,128)S(1)}, u32[]{:S(2)}, u32[]{:S(2)}) collective-permute-start(f32[8,8]{0,1:T(8,128)S(1)} %add.52), channel_id=1, source_target_pairs={{0,32},{32,0},{64,96},{96,64},{128,160},{160,128},{192,224},{224,1... | collective-permute-start | bytes 776 | tf_op jit(solution)/shard_map/ppermute | solution.py:28
  77.9 3.6 %collective-permute-start.10 = (f32[8,8]{0,1:T(8,128)S(1)}, f32[8,8]{0,1:T(8,128)S(1)}, u32[]{:S(2)}, u32[]{:S(2)}) collective-permute-start(f32[8,8]{0,1:T(8,128)S(1)} %add.53), channel_id=1, source_target_pairs={{0,64},{32,96},{64,0},{96,32},{128,192},{160,224},{192,128},{224,1... | collective-permute-start | bytes 776 | tf_op jit(solution)/shard_map/ppermute | solution.py:28
  81.5 5.1 %collective-permute-start.11 = (f32[8,8]{0,1:T(8,128)S(1)}, f32[8,8]{0,1:T(8,128)S(1)}, u32[]{:S(2)}, u32[]{:S(2)}) collective-permute-start(f32[8,8]{0,1:T(8,128)S(1)} %add.54), channel_id=1, source_target_pairs={{0,128},{32,160},{64,192},{96,224},{128,0},{160,32},{192,64},{224,... | collective-permute-start | bytes 776 | tf_op jit(solution)/shard_map/ppermute | solution.py:28

commit v8 on v7

--- a/solution.py
+++ b/solution.py
@@ -7,7 +7,7 @@
 
 STEPS = 4
 HALO = 2 * STEPS
-GROUP = 4
+GROUP = 8
 
 diffuse = 0.24
 

time: 95.2 us -> 94.1 us (0.988)
  Pallas kernels: 20.9 us -> 19.8 us
    pallas_call x1, Pallas kernels: 17 us -> 15.9 us  [transport(): pl.pallas_call(transport_kernel, grid=(levels,), in_specs=[pl.BlockSpec((...]
where the time goes in v8:
time: 94.1 us; the launch traced here: 93.7 us
  waiting for transfers between devices  33.4 us (35%)
  starting transfers between devices  21.7 us (23%)
  Pallas kernels  19.8 us (21%)
  local copies, waits for them, and re-layouts  11 us (12%)
  other arithmetic  6.03 us (6%)
    ppermute x8, waiting for transfers between devices, all_sum(): lax.ppermute(value, axis, [(i, i ^ stride) for i in range(count)])  26.2 us
    pallas_call x1, Pallas kernels, transport(): pl.pallas_call(transport_kernel, grid=(levels,), in_specs=[pl.BlockSpec((...  15.9 us
    ppermute x8, starting transfers between devices, all_sum(): lax.ppermute(value, axis, [(i, i ^ stride) for i in range(count)])  8.05 us
    ppermute x1, starting transfers between devices, body(): lax.ppermute(heads, 'lon', [((i + 1) % n_lon, i) for i in range(n_lon)])  6.31 us
    ppermute x1, waiting for transfers between devices, body(): lax.ppermute(jnp.swapaxes(edge_hi, 2, 3), 'lat', [(j, j + 1) for j in ran...  5.98 us
    ppermute x1, starting transfers between devices, body(): lax.ppermute(jnp.swapaxes(edge_lo, 2, 3), 'lat', [(j + 1, j) for j in ran...  5.07 us
    unnamed x28, local copies, waits for them, and re-layouts  5.02 us
    pallas_call x1, Pallas kernels, basis(): pl.pallas_call(basis_kernel, grid=(levels,), in_specs=[pl.BlockSpec(memor...  3.9 us
  transfers between devices with their start and end apart: 12, of which 10 were waited for; matrix products, arithmetic and copies ran while one was open for 6% of the time, Pallas kernels for 0%

profile of v8, /device:TPU:6, one launch (start us, length us, event | category | flops | bytes accessed | tf_op | source)
XLA Modules:
  0.0 93.7 jit_solution(15384710253437840515)
XLA Ops:
  0.7 0.9 fusion.10
  1.5 0.8 fusion.11
  3.3 0.7 pad_maximum_fusion.1
  4.2 0.7 pad_maximum_fusion
  4.9 6.3 %collective-permute-start = (f32[4,13,8,128]{3,2,1,0:T(8,128)}, f32[4,13,8,128]{3,2,1,0:T(8,128)}, u32[]{:S(2)}, u32[]{:S(2)}) collective-permute-start(f32[4,13,8,128]{3,2,1,0:T(8,128)} %pad_maximum_fusion), channel_id=1, source_target_pairs={{1,0},{2,1},{3,2},{4,3},{5,4},{6,5},{7,6},{8,7},{9,8},{10,9},{11,1... | collective-permute-start | bytes 638984 | tf_op jit(solution)/shard_map/ppermute | solution.py:211
  12.2 0.8 copy-done.2
  14.4 0.7 slice_bitcast_fusion.2
  15.2 1.1 %fusion.13 = (f32[4,13,8,8]{3,2,1,0:T(8,128)S(1)}, f32[4,13,8,8]{3,2,1,0:T(8,128)S(1)}) fusion(f32[4,13,8,128]{3,2,1,0:T(8,128)} %collective-permute-done.1.lp_ref), kind=kLoop, calls=%fused_computation.41 | loop fusion | bytes 53248 | tf_op jit(solution)/shard_map/slice | solution.py:218
  16.6 1.1 %fusion.12 = (f32[4,13,8,8]{3,2,1,0:T(8,128)S(1)}, f32[4,13,8,8]{3,2,1,0:T(8,128)S(1)}) fusion(f32[4,13,8,128]{3,2,1,0:T(8,128)} %collective-permute-done.ln_ref), kind=kLoop, calls=%fused_computation.40 | loop fusion | bytes 53248 | tf_op jit(solution)/shard_map/slice | solution.py:218
  18.3 5.1 %collective-permute-start.2 = (f32[4,13,8,128]{3,2,1,0:T(8,128)S(1)}, f32[4,13,8,128]{3,2,1,0:T(8,128)S(1)}, u32[]{:S(2)}, u32[]{:S(2)}) collective-permute-start(f32[4,13,8,128]{3,2,1,0:T(8,128)S(1)} %get-tuple-element.33), channel_id=1, source_target_pairs={{32,0},{64,32},{96,64},{128,96},{160,128},{192,160},{224,192},{33,... | collective-permute-start | bytes 638984 | tf_op jit(solution)/shard_map/ppermute | solution.py:221
  23.4 2.3 %collective-permute-start.3 = (f32[4,13,8,128]{3,2,1,0:T(8,128)S(1)}, f32[4,13,8,128]{3,2,1,0:T(8,128)S(1)}, u32[]{:S(2)}, u32[]{:S(2)}) collective-permute-start(f32[4,13,8,128]{3,2,1,0:T(8,128)S(1)} %get-tuple-element.32), channel_id=1, source_target_pairs={{0,32},{32,64},{64,96},{96,128},{128,160},{160,192},{192,224},{1,3... | collective-permute-start | bytes 638984 | tf_op jit(solution)/shard_map/ppermute | solution.py:222
  26.3 1.3 %collective-permute-done.2.un_ref = f32[4,13,8,128]{3,2,1,0:T(8,128)S(1)} collective-permute-done((f32[4,13,8,128]{3,2,1,0:T(8,128)S(1)}, f32[4,13,8,128]{3,2,1,0:T(8,128)S(1)}, u32[]{:S(2)}, u32[]{:S(2)}) %collective-permute-start.2) | collective-permute-done | bytes 213024 | tf_op jit(solution)/shard_map/ppermute | solution.py:221
  27.5 6.0 %collective-permute-done.3.up_ref = f32[4,13,8,128]{3,2,1,0:T(8,128)S(1)} collective-permute-done((f32[4,13,8,128]{3,2,1,0:T(8,128)S(1)}, f32[4,13,8,128]{3,2,1,0:T(8,128)S(1)}, u32[]{:S(2)}, u32[]{:S(2)}) %collective-permute-start.3) | collective-permute-done | bytes 213024 | tf_op jit(solution)/shard_map/ppermute | solution.py:222
  33.5 0.7 copy-done.6
  34.2 15.9 %shard_map.59 = (f32[8,4,64,128]{3,2,1,0:T(8,128)}, f32[4,64,128]{2,1,0:T(8,128)}) custom-call(f32[8,256]{1,0:T(8,128)} %fusion.2.mask_ref, f32[8,4,64,128]{3,2,1,0:T(8,128)} %pr_ref.1, f32[2,4,64,128]{3,2,1,0:T(8,128)} %wi_ref.1, f32[2,4,64,128]{3,2,1,0:T(8,128)} %te_ref.1, f32[4,64,128]{2,1,0:T(8,128)} %ob_ref.1, ...), custom_call_target="tpu_custom_call" | custom-call | tf_op jit(solution)/shard_map/pallas_call | solution.py:133
  50.1 1.0 %reduce_sum.9 = f32[64]{0:T(128)S(1)} reduce(f32[4,64,128]{2,1,0:T(8,128)} %get-tuple-element.4, f32[]{:T(128)} %constant.61.clone.1), dimensions={0,2}, to_apply=%region_0.1 | reduce | flops 32704 | bytes 131332 | tf_op jit(solution)/shard_map/reduce_sum | solution.py:235
  51.3 1.2 %collective-permute-done.4 = f32[8,8]{0,1:T(8,128)S(1)} collective-permute-done((f32[8,8]{0,1:T(8,128)S(1)}, f32[8,8]{0,1:T(8,128)S(1)}, u32[]{:S(2)}, u32[]{:S(2)}) %collective-permute-start.4) | collective-permute-done | bytes 288 | tf_op jit(solution)/shard_map/ppermute | solution.py:28
  52.5 3.6 %collective-permute-done.5 = f32[8,8]{0,1:T(8,128)S(1)} collective-permute-done((f32[8,8]{0,1:T(8,128)S(1)}, f32[8,8]{0,1:T(8,128)S(1)}, u32[]{:S(2)}, u32[]{:S(2)}) %collective-permute-start.5) | collective-permute-done | bytes 288 | tf_op jit(solution)/shard_map/ppermute | solution.py:28
  56.1 3.6 %collective-permute-done.6 = f32[8,8]{0,1:T(8,128)S(1)} collective-permute-done((f32[8,8]{0,1:T(8,128)S(1)}, f32[8,8]{0,1:T(8,128)S(1)}, u32[]{:S(2)}, u32[]{:S(2)}) %collective-permute-start.6) | collective-permute-done | bytes 288 | tf_op jit(solution)/shard_map/ppermute | solution.py:28
  60.3 3.9 %collective-permute-done.7 = f32[8,8]{0,1:T(8,128)S(1)} collective-permute-done((f32[8,8]{0,1:T(8,128)S(1)}, f32[8,8]{0,1:T(8,128)S(1)}, u32[]{:S(2)}, u32[]{:S(2)}) %collective-permute-start.7) | collective-permute-done | bytes 288 | tf_op jit(solution)/shard_map/ppermute | solution.py:28
  64.2 5.8 %collective-permute-start.8 = (f32[8,8]{0,1:T(8,128)S(1)}, f32[8,8]{0,1:T(8,128)S(1)}, u32[]{:S(2)}, u32[]{:S(2)}) collective-permute-start(f32[8,8]{0,1:T(8,128)S(1)} %add.51), channel_id=1, source_target_pairs={{0,16},{1,17},{2,18},{3,19},{4,20},{5,21},{6,22},{7,23},{8,24},{9,... | collective-permute-start | bytes 776 | tf_op jit(solution)/shard_map/ppermute | solution.py:28
  70.0 1.8 %collective-permute-done.8 = f32[8,8]{0,1:T(8,128)S(1)} collective-permute-done((f32[8,8]{0,1:T(8,128)S(1)}, f32[8,8]{0,1:T(8,128)S(1)}, u32[]{:S(2)}, u32[]{:S(2)}) %collective-permute-start.8) | collective-permute-done | bytes 288 | tf_op jit(solution)/shard_map/ppermute | solution.py:28
  71.7 5.1 %collective-permute-done.9 = f32[8,8]{0,1:T(8,128)S(1)} collective-permute-done((f32[8,8]{0,1:T(8,128)S(1)}, f32[8,8]{0,1:T(8,128)S(1)}, u32[]{:S(2)}, u32[]{:S(2)}) %collective-permute-start.9) | collective-permute-done | bytes 288 | tf_op jit(solution)/shard_map/ppermute | solution.py:28
  77.4 3.1 %collective-permute-done.10 = f32[8,8]{0,1:T(8,128)S(1)} collective-permute-done((f32[8,8]{0,1:T(8,128)S(1)}, f32[8,8]{0,1:T(8,128)S(1)}, u32[]{:S(2)}, u32[]{:S(2)}) %collective-permute-start.10) | collective-permute-done | bytes 288 | tf_op jit(solution)/shard_map/ppermute | solution.py:28
  80.5 1.1 %collective-permute-start.11 = (f32[8,8]{0,1:T(8,128)S(1)}, f32[8,8]{0,1:T(8,128)S(1)}, u32[]{:S(2)}, u32[]{:S(2)}) collective-permute-start(f32[8,8]{0,1:T(8,128)S(1)} %add.54), channel_id=1, source_target_pairs={{0,128},{32,160},{64,192},{96,224},{128,0},{160,32},{192,64},{224,... | collective-permute-start | bytes 776 | tf_op jit(solution)/shard_map/ppermute | solution.py:28
  81.6 4.0 %collective-permute-done.11 = f32[8,8]{0,1:T(8,128)S(1)} collective-permute-done((f32[8,8]{0,1:T(8,128)S(1)}, f32[8,8]{0,1:T(8,128)S(1)}, u32[]{:S(2)}, u32[]{:S(2)}) %collective-permute-start.11) | collective-permute-done | bytes 288 | tf_op jit(solution)/shard_map/ppermute | solution.py:28
  85.7 0.7 cholesky.17
  86.4 0.6 compare_reduce_fusion
  87.1 0.6 multiply_bitcast_fusion
  88.3 0.8 fusion.3.inv_ref
  89.1 0.7 copy.53
  89.8 3.9 %shard_map.60 = f32[8,4,64,128]{3,2,1,0:T(8,128)} custom-call(f32[8,8]{1,0:T(8,128)} %fusion.3.inv_ref, f32[1,1]{1,0:T(1,128)} %constant.65.clone.1.scale_ref, f32[8,4,64,128]{3,2,1,0:T(8,128)} %get-tuple-element.5.z_ref), custom_call_target="tpu_custom_call" | custom-call | tf_op jit(solution)/shard_map/pallas_call | solution.py:181
  (63 shorter events, 7.0 us)
Async XLA Ops:
  0.6 1.7 %copy-start.4 = (f32[4,64,128]{2,1,0:T(8,128)S(1)}, f32[4,64,128]{2,1,0:T(8,128)}, u32[]{:S(2)}) copy-start(f32[4,64,128]{2,1,0:T(8,128)} %ob_ref.1) | copy-start | bytes 393220
  0.6 2.6 %copy-start = (f32[8,4,64,128]{3,2,1,0:T(8,128)S(1)}, f32[8,4,64,128]{3,2,1,0:T(8,128)}, u32[]{:S(2)}) copy-start(f32[8,4,64,128]{3,2,1,0:T(8,128)} %pr_ref.1) | copy-start | bytes 3145732
  2.4 0.7 copy-start.3
  4.0 11.1 %collective-permute-start.1 = (f32[4,13,8,128]{3,2,1,0:T(8,128)}, f32[4,13,8,128]{3,2,1,0:T(8,128)}, u32[]{:S(2)}, u32[]{:S(2)}) collective-permute-start(f32[4,13,8,128]{3,2,1,0:T(8,128)} %pad_maximum_fusion.1), channel_id=1, source_target_pairs={{0,1},{1,2},{2,3},{3,4},{4,5},{5,6},{6,7},{7,8},{8,9},{9,10},{10,1... | collective-permute-start | bytes 638984 | tf_op jit(solution)/shard_map/ppermute | solution.py:212
  4.9 11.7 %collective-permute-start = (f32[4,13,8,128]{3,2,1,0:T(8,128)}, f32[4,13,8,128]{3,2,1,0:T(8,128)}, u32[]{:S(2)}, u32[]{:S(2)}) collective-permute-start(f32[4,13,8,128]{3,2,1,0:T(8,128)} %pad_maximum_fusion), channel_id=1, source_target_pairs={{1,0},{2,1},{3,2},{4,3},{5,4},{6,5},{7,6},{8,7},{9,8},{10,9},{11,1... | collective-permute-start | bytes 638984 | tf_op jit(solution)/shard_map/ppermute | solution.py:211
  11.2 0.9 %copy-start.1 = (f32[2,4,64,128]{3,2,1,0:T(8,128)S(1)}, f32[2,4,64,128]{3,2,1,0:T(8,128)}, u32[]{:S(2)}) copy-start(f32[2,4,64,128]{3,2,1,0:T(8,128)} %wi_ref.1) | copy-start | bytes 786436
  12.1 0.9 %copy-start.2 = (f32[2,4,64,128]{3,2,1,0:T(8,128)S(1)}, f32[2,4,64,128]{3,2,1,0:T(8,128)}, u32[]{:S(2)}) copy-start(f32[2,4,64,128]{3,2,1,0:T(8,128)} %te_ref.1) | copy-start | bytes 786436
  18.3 9.2 %collective-permute-start.2 = (f32[4,13,8,128]{3,2,1,0:T(8,128)S(1)}, f32[4,13,8,128]{3,2,1,0:T(8,128)S(1)}, u32[]{:S(2)}, u32[]{:S(2)}) collective-permute-start(f32[4,13,8,128]{3,2,1,0:T(8,128)S(1)} %get-tuple-element.33), channel_id=1, source_target_pairs={{32,0},{64,32},{96,64},{128,96},{160,128},{192,160},{224,192},{33,... | collective-permute-start | bytes 638984 | tf_op jit(solution)/shard_map/ppermute | solution.py:221
  23.4 10.1 %collective-permute-start.3 = (f32[4,13,8,128]{3,2,1,0:T(8,128)S(1)}, f32[4,13,8,128]{3,2,1,0:T(8,128)S(1)}, u32[]{:S(2)}, u32[]{:S(2)}) collective-permute-start(f32[4,13,8,128]{3,2,1,0:T(8,128)S(1)} %get-tuple-element.32), channel_id=1, source_target_pairs={{0,32},{32,64},{64,96},{96,128},{128,160},{160,192},{192,224},{1,3... | collective-permute-start | bytes 638984 | tf_op jit(solution)/shard_map/ppermute | solution.py:222
  27.5 6.0 %copy-start.5 = (f32[4,13,8,128]{3,2,1,0:T(8,128)}, f32[4,13,8,128]{3,2,1,0:T(8,128)S(1)}, u32[]{:S(2)}) copy-start(f32[4,13,8,128]{3,2,1,0:T(8,128)S(1)} %collective-permute-done.2.un_ref) | copy-start | bytes 638980
  33.5 0.7 copy-start.6
  51.3 1.2 %collective-permute-start.4 = (f32[8,8]{0,1:T(8,128)S(1)}, f32[8,8]{0,1:T(8,128)S(1)}, u32[]{:S(2)}, u32[]{:S(2)}) collective-permute-start(f32[8,8]{0,1:T(8,128)S(1)} %copy.50), channel_id=1, source_target_pairs={{0,1},{1,0},{2,3},{3,2},{4,5},{5,4},{6,7},{7,6},{8,9},{9,8},{10,11... | collective-permute-start | bytes 776 | tf_op jit(solution)/shard_map/ppermute | solution.py:28
  52.5 3.6 %collective-permute-start.5 = (f32[8,8]{0,1:T(8,128)S(1)}, f32[8,8]{0,1:T(8,128)S(1)}, u32[]{:S(2)}, u32[]{:S(2)}) collective-permute-start(f32[8,8]{0,1:T(8,128)S(1)} %add.48), channel_id=1, source_target_pairs={{0,2},{1,3},{2,0},{3,1},{4,6},{5,7},{6,4},{7,5},{8,10},{9,11},{10,... | collective-permute-start | bytes 776 | tf_op jit(solution)/shard_map/ppermute | solution.py:28
  56.1 3.6 %collective-permute-start.6 = (f32[8,8]{0,1:T(8,128)S(1)}, f32[8,8]{0,1:T(8,128)S(1)}, u32[]{:S(2)}, u32[]{:S(2)}) collective-permute-start(f32[8,8]{0,1:T(8,128)S(1)} %add.49), channel_id=1, source_target_pairs={{0,4},{1,5},{2,6},{3,7},{4,0},{5,1},{6,2},{7,3},{8,12},{9,13},{10,... | collective-permute-start | bytes 776 | tf_op jit(solution)/shard_map/ppermute | solution.py:28
  59.7 4.5 %collective-permute-start.7 = (f32[8,8]{0,1:T(8,128)S(1)}, f32[8,8]{0,1:T(8,128)S(1)}, u32[]{:S(2)}, u32[]{:S(2)}) collective-permute-start(f32[8,8]{0,1:T(8,128)S(1)} %add.50), channel_id=1, source_target_pairs={{0,8},{1,9},{2,10},{3,11},{4,12},{5,13},{6,14},{7,15},{8,0},{9,1},... | collective-permute-start | bytes 776 | tf_op jit(solution)/shard_map/ppermute | solution.py:28
  64.2 7.5 %collective-permute-start.8 = (f32[8,8]{0,1:T(8,128)S(1)}, f32[8,8]{0,1:T(8,128)S(1)}, u32[]{:S(2)}, u32[]{:S(2)}) collective-permute-start(f32[8,8]{0,1:T(8,128)S(1)} %add.51), channel_id=1, source_target_pairs={{0,16},{1,17},{2,18},{3,19},{4,20},{5,21},{6,22},{7,23},{8,24},{9,... | collective-permute-start | bytes 776 | tf_op jit(solution)/shard_map/ppermute | solution.py:28
  71.7 5.1 %collective-permute-start.9 = (f32[8,8]{0,1:T(8,128)S(1)}, f32[8,8]{0,1:T(8,128)S(1)}, u32[]{:S(2)}, u32[]{:S(2)}) collective-permute-start(f32[8,8]{0,1:T(8,128)S(1)} %add.52), channel_id=1, source_target_pairs={{0,32},{32,0},{64,96},{96,64},{128,160},{160,128},{192,224},{224,1... | collective-permute-start | bytes 776 | tf_op jit(solution)/shard_map/ppermute | solution.py:28
  76.8 3.6 %collective-permute-start.10 = (f32[8,8]{0,1:T(8,128)S(1)}, f32[8,8]{0,1:T(8,128)S(1)}, u32[]{:S(2)}, u32[]{:S(2)}) collective-permute-start(f32[8,8]{0,1:T(8,128)S(1)} %add.53), channel_id=1, source_target_pairs={{0,64},{32,96},{64,0},{96,32},{128,192},{160,224},{192,128},{224,1... | collective-permute-start | bytes 776 | tf_op jit(solution)/shard_map/ppermute | solution.py:28
  80.5 5.1 %collective-permute-start.11 = (f32[8,8]{0,1:T(8,128)S(1)}, f32[8,8]{0,1:T(8,128)S(1)}, u32[]{:S(2)}, u32[]{:S(2)}) collective-permute-start(f32[8,8]{0,1:T(8,128)S(1)} %add.54), channel_id=1, source_target_pairs={{0,128},{32,160},{64,192},{96,224},{128,0},{160,32},{192,64},{224,... | collective-permute-start | bytes 776 | tf_op jit(solution)/shard_map/ppermute | solution.py:28

commit v9 on v8

--- a/solution.py
+++ b/solution.py
@@ -51,10 +51,10 @@
 
     def assemble(own, plane, slot=0):
         plane_ref[slot, 0:rows, 0:lanes] = own
-        plane_ref[slot, rows : rows + HALO, 0:lanes] = ln_ref[0, plane]
-        plane_ref[slot, rows + HALO : full_rows, 0:lanes] = lp_ref[0, plane]
+        plane_ref[slot, rows : rows + HALO, 0:lanes] = ln_ref[plane, 0]
+        plane_ref[slot, rows + HALO : full_rows, 0:lanes] = lp_ref[plane, 0]
         gap = jnp.zeros((lanes - 2 * HALO, lanes), jnp.float32)
-        halo = jnp.concatenate((un_ref[0, plane], gap, up_ref[0, plane]), axis=0)
+        halo = jnp.concatenate((un_ref[plane, 0], gap, up_ref[plane, 0]), axis=0)
         plane_ref[slot, :, lanes:full_lanes] = halo.T[:full_rows]
         return plane_ref[slot]
 
@@ -120,7 +120,7 @@
 
 def transport(mask, probes, wind, wind_tend, obs_weight, lon_next, lon_prev, lat_next, lat_prev):
     n_probes, levels, rows, lanes = probes.shape
-    planes = lon_next.shape[1]
+    planes = lon_next.shape[0]
     full_rows = rows + 2 * HALO
     full_lanes = 2 * lanes
 
@@ -128,7 +128,7 @@
         return pl.BlockSpec((lead, 1, rows, lanes), lambda l: (0, l, 0, 0))
 
     def halo_block(height):
-        return pl.BlockSpec((1, planes, height, lanes), lambda l: (l, 0, 0, 0))
+        return pl.BlockSpec((planes, 1, height, lanes), lambda l: (0, l, 0, 0))
 
     return pl.pallas_call(
         transport_kernel,
@@ -196,13 +196,7 @@
 
     def planes_of(part):
         return jnp.concatenate(
-            (
-                jnp.swapaxes(part(probes), 0, 1),
-                jnp.swapaxes(part(wind), 0, 1),
-                jnp.swapaxes(part(wind_tend), 0, 1),
-                part(obs_weight[None])[0][:, None],
-            ),
-            axis=1,
+            (part(probes), part(wind), part(wind_tend), part(obs_weight[None])), axis=0
         )
 
     heads = planes_of(lambda a: a[..., :HALO, :])

time: 94.1 us -> 95 us (level)
  starting transfers between devices: 21.7 us -> 22.9 us
    unnamed x28 -> x24, local copies, waits for them, and re-layouts: 5.02 us -> 6.36 us
    ppermute x8, starting transfers between devices: 8.05 us -> 9.26 us  [all_sum(): lax.ppermute(value, axis, [(i, i ^ stride) for i in range(count)])]
    another operation x4 -> x0, local copies, waits for them, and re-layouts: 1.06 us -> none  [planes_of(): part(obs_weight[None])[0][:, None]]
where the time goes in v9:
time: 95 us; the launch traced here: 94.6 us
  waiting for transfers between devices  32.7 us (34%)
  starting transfers between devices  22.9 us (24%)
  Pallas kernels  19.9 us (21%)
  local copies, waits for them, and re-layouts  11.5 us (12%)
  other arithmetic  6.02 us (6%)
    ppermute x8, waiting for transfers between devices, all_sum(): lax.ppermute(value, axis, [(i, i ^ stride) for i in range(count)])  25.4 us
    pallas_call x1, Pallas kernels, transport(): pl.pallas_call(transport_kernel, grid=(levels,), in_specs=[pl.BlockSpec((...  16 us
    ppermute x8, starting transfers between devices, all_sum(): lax.ppermute(value, axis, [(i, i ^ stride) for i in range(count)])  9.26 us
    unnamed x24, local copies, waits for them, and re-layouts  6.36 us
    ppermute x1, starting transfers between devices, body(): lax.ppermute(heads, 'lon', [((i + 1) % n_lon, i) for i in range(n_lon)])  6.31 us
    ppermute x1, waiting for transfers between devices, body(): lax.ppermute(jnp.swapaxes(edge_hi, 2, 3), 'lat', [(j, j + 1) for j in ran...  5.98 us
    ppermute x1, starting transfers between devices, body(): lax.ppermute(jnp.swapaxes(edge_lo, 2, 3), 'lat', [(j + 1, j) for j in ran...  5.07 us
    pallas_call x1, Pallas kernels, basis(): pl.pallas_call(basis_kernel, grid=(levels,), in_specs=[pl.BlockSpec(memor...  3.9 us
  transfers between devices with their start and end apart: 12, of which 10 were waited for; matrix products, arithmetic and copies ran while one was open for 6% of the time, Pallas kernels for 0%

profile of v9, /device:TPU:6, one launch (start us, length us, event | category | flops | bytes accessed | tf_op | source)
XLA Modules:
  0.0 94.6 jit_solution(3996701138458933075)
XLA Ops:
  0.6 1.1 %copy.26 = f32[4,64,128]{1,2,0:T(8,128)S(1)} copy(f32[4,64,128]{2,1,0:T(8,128)} %ob_ref.1) | data formatting | bytes 262144 | tf_op args[3]
  2.6 0.9 copy-done.1
  3.5 0.8 fusion.11
  4.3 0.7 pad_maximum_fusion.1
  5.1 0.7 pad_maximum_fusion
  5.8 6.3 %collective-permute-start = (f32[13,4,8,128]{3,2,1,0:T(8,128)}, f32[13,4,8,128]{3,2,1,0:T(8,128)}, u32[]{:S(2)}, u32[]{:S(2)}) collective-permute-start(f32[13,4,8,128]{3,2,1,0:T(8,128)} %pad_maximum_fusion), channel_id=1, source_target_pairs={{1,0},{2,1},{3,2},{4,3},{5,4},{6,5},{7,6},{8,7},{9,8},{10,9},{11,1... | collective-permute-start | bytes 638984 | tf_op jit(solution)/shard_map/ppermute | solution.py:205
  12.7 0.8 copy-done.2
  14.8 0.7 fusion.10
  15.6 1.1 %fusion.15 = (f32[13,4,8,8]{3,2,1,0:T(8,128)S(1)}, f32[13,4,8,8]{3,2,1,0:T(8,128)S(1)}) fusion(f32[13,4,8,128]{3,2,1,0:T(8,128)} %collective-permute-done.1.lp_ref), kind=kLoop, calls=%fused_computation.33 | loop fusion | bytes 53248 | tf_op jit(solution)/shard_map/slice | solution.py:212
  17.0 1.1 %fusion.14 = (f32[13,4,8,8]{3,2,1,0:T(8,128)S(1)}, f32[13,4,8,8]{3,2,1,0:T(8,128)S(1)}) fusion(f32[13,4,8,128]{3,2,1,0:T(8,128)} %collective-permute-done.ln_ref), kind=kLoop, calls=%fused_computation.32 | loop fusion | bytes 53248 | tf_op jit(solution)/shard_map/slice | solution.py:212
  18.7 5.1 %collective-permute-start.2 = (f32[13,4,8,128]{3,2,1,0:T(8,128)S(1)}, f32[13,4,8,128]{3,2,1,0:T(8,128)S(1)}, u32[]{:S(2)}, u32[]{:S(2)}) collective-permute-start(f32[13,4,8,128]{3,2,1,0:T(8,128)S(1)} %get-tuple-element.33), channel_id=1, source_target_pairs={{32,0},{64,32},{96,64},{128,96},{160,128},{192,160},{224,192},{33,... | collective-permute-start | bytes 638984 | tf_op jit(solution)/shard_map/ppermute | solution.py:215
  23.8 2.3 %collective-permute-start.3 = (f32[13,4,8,128]{3,2,1,0:T(8,128)S(1)}, f32[13,4,8,128]{3,2,1,0:T(8,128)S(1)}, u32[]{:S(2)}, u32[]{:S(2)}) collective-permute-start(f32[13,4,8,128]{3,2,1,0:T(8,128)S(1)} %get-tuple-element.32), channel_id=1, source_target_pairs={{0,32},{32,64},{64,96},{96,128},{128,160},{160,192},{192,224},{1,3... | collective-permute-start | bytes 638984 | tf_op jit(solution)/shard_map/ppermute | solution.py:216
  26.6 1.3 %collective-permute-done.2.un_ref = f32[13,4,8,128]{3,2,1,0:T(8,128)S(1)} collective-permute-done((f32[13,4,8,128]{3,2,1,0:T(8,128)S(1)}, f32[13,4,8,128]{3,2,1,0:T(8,128)S(1)}, u32[]{:S(2)}, u32[]{:S(2)}) %collective-permute-start.2) | collective-permute-done | bytes 213024 | tf_op jit(solution)/shard_map/ppermute | solution.py:215
  27.9 6.0 %collective-permute-done.3.up_ref = f32[13,4,8,128]{3,2,1,0:T(8,128)S(1)} collective-permute-done((f32[13,4,8,128]{3,2,1,0:T(8,128)S(1)}, f32[13,4,8,128]{3,2,1,0:T(8,128)S(1)}, u32[]{:S(2)}, u32[]{:S(2)}) %collective-permute-start.3) | collective-permute-done | bytes 213024 | tf_op jit(solution)/shard_map/ppermute | solution.py:216
  33.9 0.7 copy-done.5
  34.6 16.0 %shard_map.59 = (f32[8,4,64,128]{3,2,1,0:T(8,128)}, f32[4,64,128]{2,1,0:T(8,128)}) custom-call(f32[8,256]{1,0:T(8,128)} %fusion.2.mask_ref, f32[8,4,64,128]{3,2,1,0:T(8,128)} %pr_ref.1, f32[2,4,64,128]{3,2,1,0:T(8,128)} %wi_ref.1, f32[2,4,64,128]{3,2,1,0:T(8,128)} %te_ref.1, f32[4,64,128]{2,1,0:T(8,128)} %ob_ref.1, ...), custom_call_target="tpu_custom_call" | custom-call | tf_op jit(solution)/shard_map/pallas_call | solution.py:133
  50.6 1.0 %reduce_sum.9 = f32[64]{0:T(128)S(1)} reduce(f32[4,64,128]{2,1,0:T(8,128)} %get-tuple-element.4, f32[]{:T(128)} %constant.61.clone.1), dimensions={0,2}, to_apply=%region_0.1 | reduce | flops 32704 | bytes 131332 | tf_op jit(solution)/shard_map/reduce_sum | solution.py:229
  51.7 1.2 %collective-permute-done.4 = f32[8,8]{0,1:T(8,128)S(1)} collective-permute-done((f32[8,8]{0,1:T(8,128)S(1)}, f32[8,8]{0,1:T(8,128)S(1)}, u32[]{:S(2)}, u32[]{:S(2)}) %collective-permute-start.4) | collective-permute-done | bytes 288 | tf_op jit(solution)/shard_map/ppermute | solution.py:28
  52.9 3.6 %collective-permute-done.5 = f32[8,8]{0,1:T(8,128)S(1)} collective-permute-done((f32[8,8]{0,1:T(8,128)S(1)}, f32[8,8]{0,1:T(8,128)S(1)}, u32[]{:S(2)}, u32[]{:S(2)}) %collective-permute-start.5) | collective-permute-done | bytes 288 | tf_op jit(solution)/shard_map/ppermute | solution.py:28
  56.5 3.6 %collective-permute-done.6 = f32[8,8]{0,1:T(8,128)S(1)} collective-permute-done((f32[8,8]{0,1:T(8,128)S(1)}, f32[8,8]{0,1:T(8,128)S(1)}, u32[]{:S(2)}, u32[]{:S(2)}) %collective-permute-start.6) | collective-permute-done | bytes 288 | tf_op jit(solution)/shard_map/ppermute | solution.py:28
  60.2 1.2 %collective-permute-start.7 = (f32[8,8]{0,1:T(8,128)S(1)}, f32[8,8]{0,1:T(8,128)S(1)}, u32[]{:S(2)}, u32[]{:S(2)}) collective-permute-start(f32[8,8]{0,1:T(8,128)S(1)} %add.50), channel_id=1, source_target_pairs={{0,8},{1,9},{2,10},{3,11},{4,12},{5,13},{6,14},{7,15},{8,0},{9,1},... | collective-permute-start | bytes 776 | tf_op jit(solution)/shard_map/ppermute | solution.py:28
  61.4 3.3 %collective-permute-done.7 = f32[8,8]{0,1:T(8,128)S(1)} collective-permute-done((f32[8,8]{0,1:T(8,128)S(1)}, f32[8,8]{0,1:T(8,128)S(1)}, u32[]{:S(2)}, u32[]{:S(2)}) %collective-permute-start.7) | collective-permute-done | bytes 288 | tf_op jit(solution)/shard_map/ppermute | solution.py:28
  64.7 6.4 %collective-permute-start.8 = (f32[8,8]{0,1:T(8,128)S(1)}, f32[8,8]{0,1:T(8,128)S(1)}, u32[]{:S(2)}, u32[]{:S(2)}) collective-permute-start(f32[8,8]{0,1:T(8,128)S(1)} %add.51), channel_id=1, source_target_pairs={{0,16},{1,17},{2,18},{3,19},{4,20},{5,21},{6,22},{7,23},{8,24},{9,... | collective-permute-start | bytes 776 | tf_op jit(solution)/shard_map/ppermute | solution.py:28
  71.0 1.6 %collective-permute-done.8 = f32[8,8]{0,1:T(8,128)S(1)} collective-permute-done((f32[8,8]{0,1:T(8,128)S(1)}, f32[8,8]{0,1:T(8,128)S(1)}, u32[]{:S(2)}, u32[]{:S(2)}) %collective-permute-start.8) | collective-permute-done | bytes 288 | tf_op jit(solution)/shard_map/ppermute | solution.py:28
  72.6 5.1 %collective-permute-done.9 = f32[8,8]{0,1:T(8,128)S(1)} collective-permute-done((f32[8,8]{0,1:T(8,128)S(1)}, f32[8,8]{0,1:T(8,128)S(1)}, u32[]{:S(2)}, u32[]{:S(2)}) %collective-permute-start.9) | collective-permute-done | bytes 288 | tf_op jit(solution)/shard_map/ppermute | solution.py:28
  78.3 3.1 %collective-permute-done.10 = f32[8,8]{0,1:T(8,128)S(1)} collective-permute-done((f32[8,8]{0,1:T(8,128)S(1)}, f32[8,8]{0,1:T(8,128)S(1)}, u32[]{:S(2)}, u32[]{:S(2)}) %collective-permute-start.10) | collective-permute-done | bytes 288 | tf_op jit(solution)/shard_map/ppermute | solution.py:28
  81.3 1.1 %collective-permute-start.11 = (f32[8,8]{0,1:T(8,128)S(1)}, f32[8,8]{0,1:T(8,128)S(1)}, u32[]{:S(2)}, u32[]{:S(2)}) collective-permute-start(f32[8,8]{0,1:T(8,128)S(1)} %add.54), channel_id=1, source_target_pairs={{0,128},{32,160},{64,192},{96,224},{128,0},{160,32},{192,64},{224,... | collective-permute-start | bytes 776 | tf_op jit(solution)/shard_map/ppermute | solution.py:28
  82.5 4.0 %collective-permute-done.11 = f32[8,8]{0,1:T(8,128)S(1)} collective-permute-done((f32[8,8]{0,1:T(8,128)S(1)}, f32[8,8]{0,1:T(8,128)S(1)}, u32[]{:S(2)}, u32[]{:S(2)}) %collective-permute-start.11) | collective-permute-done | bytes 288 | tf_op jit(solution)/shard_map/ppermute | solution.py:28
  86.5 0.7 cholesky.17
  89.2 0.8 fusion.3.inv_ref
  90.0 0.7 copy.43
  90.7 3.9 %shard_map.60 = f32[8,4,64,128]{3,2,1,0:T(8,128)} custom-call(f32[8,8]{1,0:T(8,128)} %fusion.3.inv_ref, f32[1,1]{1,0:T(1,128)} %constant.65.clone.1.scale_ref, f32[8,4,64,128]{3,2,1,0:T(8,128)} %get-tuple-element.5.z_ref), custom_call_target="tpu_custom_call" | custom-call | tf_op jit(solution)/shard_map/pallas_call | solution.py:181
  (56 shorter events, 6.9 us)
Async XLA Ops:
  0.6 1.9 %copy-start = (f32[8,4,64,128]{3,2,1,0:T(8,128)S(1)}, f32[8,4,64,128]{3,2,1,0:T(8,128)}, u32[]{:S(2)}) copy-start(f32[8,4,64,128]{3,2,1,0:T(8,128)} %pr_ref.1) | copy-start | bytes 3145732
  1.8 0.7 copy-start.3
  2.6 1.0 %copy-start.1 = (f32[2,4,64,128]{3,2,1,0:T(8,128)S(1)}, f32[2,4,64,128]{3,2,1,0:T(8,128)}, u32[]{:S(2)}) copy-start(f32[2,4,64,128]{3,2,1,0:T(8,128)} %wi_ref.1) | copy-start | bytes 786436
  5.0 10.5 %collective-permute-start.1 = (f32[13,4,8,128]{3,2,1,0:T(8,128)}, f32[13,4,8,128]{3,2,1,0:T(8,128)}, u32[]{:S(2)}, u32[]{:S(2)}) collective-permute-start(f32[13,4,8,128]{3,2,1,0:T(8,128)} %pad_maximum_fusion.1), channel_id=1, source_target_pairs={{0,1},{1,2},{2,3},{3,4},{4,5},{5,6},{6,7},{7,8},{8,9},{9,10},{10,1... | collective-permute-start | bytes 638984 | tf_op jit(solution)/shard_map/ppermute | solution.py:206
  5.8 11.1 %collective-permute-start = (f32[13,4,8,128]{3,2,1,0:T(8,128)}, f32[13,4,8,128]{3,2,1,0:T(8,128)}, u32[]{:S(2)}, u32[]{:S(2)}) collective-permute-start(f32[13,4,8,128]{3,2,1,0:T(8,128)} %pad_maximum_fusion), channel_id=1, source_target_pairs={{1,0},{2,1},{3,2},{4,3},{5,4},{6,5},{7,6},{8,7},{9,8},{10,9},{11,1... | collective-permute-start | bytes 638984 | tf_op jit(solution)/shard_map/ppermute | solution.py:205
  12.5 1.0 %copy-start.2 = (f32[2,4,64,128]{3,2,1,0:T(8,128)S(1)}, f32[2,4,64,128]{3,2,1,0:T(8,128)}, u32[]{:S(2)}) copy-start(f32[2,4,64,128]{3,2,1,0:T(8,128)} %te_ref.1) | copy-start | bytes 786436
  18.7 9.2 %collective-permute-start.2 = (f32[13,4,8,128]{3,2,1,0:T(8,128)S(1)}, f32[13,4,8,128]{3,2,1,0:T(8,128)S(1)}, u32[]{:S(2)}, u32[]{:S(2)}) collective-permute-start(f32[13,4,8,128]{3,2,1,0:T(8,128)S(1)} %get-tuple-element.33), channel_id=1, source_target_pairs={{32,0},{64,32},{96,64},{128,96},{160,128},{192,160},{224,192},{33,... | collective-permute-start | bytes 638984 | tf_op jit(solution)/shard_map/ppermute | solution.py:215
  23.8 10.1 %collective-permute-start.3 = (f32[13,4,8,128]{3,2,1,0:T(8,128)S(1)}, f32[13,4,8,128]{3,2,1,0:T(8,128)S(1)}, u32[]{:S(2)}, u32[]{:S(2)}) collective-permute-start(f32[13,4,8,128]{3,2,1,0:T(8,128)S(1)} %get-tuple-element.32), channel_id=1, source_target_pairs={{0,32},{32,64},{64,96},{96,128},{128,160},{160,192},{192,224},{1,3... | collective-permute-start | bytes 638984 | tf_op jit(solution)/shard_map/ppermute | solution.py:216
  27.9 6.0 %copy-start.4 = (f32[13,4,8,128]{3,2,1,0:T(8,128)}, f32[13,4,8,128]{3,2,1,0:T(8,128)S(1)}, u32[]{:S(2)}) copy-start(f32[13,4,8,128]{3,2,1,0:T(8,128)S(1)} %collective-permute-done.2.un_ref) | copy-start | bytes 638980
  33.9 0.7 copy-start.5
  51.7 1.2 %collective-permute-start.4 = (f32[8,8]{0,1:T(8,128)S(1)}, f32[8,8]{0,1:T(8,128)S(1)}, u32[]{:S(2)}, u32[]{:S(2)}) collective-permute-start(f32[8,8]{0,1:T(8,128)S(1)} %copy.40), channel_id=1, source_target_pairs={{0,1},{1,0},{2,3},{3,2},{4,5},{5,4},{6,7},{7,6},{8,9},{9,8},{10,11... | collective-permute-start | bytes 776 | tf_op jit(solution)/shard_map/ppermute | solution.py:28
  52.9 3.6 %collective-permute-start.5 = (f32[8,8]{0,1:T(8,128)S(1)}, f32[8,8]{0,1:T(8,128)S(1)}, u32[]{:S(2)}, u32[]{:S(2)}) collective-permute-start(f32[8,8]{0,1:T(8,128)S(1)} %add.48), channel_id=1, source_target_pairs={{0,2},{1,3},{2,0},{3,1},{4,6},{5,7},{6,4},{7,5},{8,10},{9,11},{10,... | collective-permute-start | bytes 776 | tf_op jit(solution)/shard_map/ppermute | solution.py:28
  56.5 3.6 %collective-permute-start.6 = (f32[8,8]{0,1:T(8,128)S(1)}, f32[8,8]{0,1:T(8,128)S(1)}, u32[]{:S(2)}, u32[]{:S(2)}) collective-permute-start(f32[8,8]{0,1:T(8,128)S(1)} %add.49), channel_id=1, source_target_pairs={{0,4},{1,5},{2,6},{3,7},{4,0},{5,1},{6,2},{7,3},{8,12},{9,13},{10,... | collective-permute-start | bytes 776 | tf_op jit(solution)/shard_map/ppermute | solution.py:28
  60.2 4.5 %collective-permute-start.7 = (f32[8,8]{0,1:T(8,128)S(1)}, f32[8,8]{0,1:T(8,128)S(1)}, u32[]{:S(2)}, u32[]{:S(2)}) collective-permute-start(f32[8,8]{0,1:T(8,128)S(1)} %add.50), channel_id=1, source_target_pairs={{0,8},{1,9},{2,10},{3,11},{4,12},{5,13},{6,14},{7,15},{8,0},{9,1},... | collective-permute-start | bytes 776 | tf_op jit(solution)/shard_map/ppermute | solution.py:28
  64.7 7.9 %collective-permute-start.8 = (f32[8,8]{0,1:T(8,128)S(1)}, f32[8,8]{0,1:T(8,128)S(1)}, u32[]{:S(2)}, u32[]{:S(2)}) collective-permute-start(f32[8,8]{0,1:T(8,128)S(1)} %add.51), channel_id=1, source_target_pairs={{0,16},{1,17},{2,18},{3,19},{4,20},{5,21},{6,22},{7,23},{8,24},{9,... | collective-permute-start | bytes 776 | tf_op jit(solution)/shard_map/ppermute | solution.py:28
  72.6 5.1 %collective-permute-start.9 = (f32[8,8]{0,1:T(8,128)S(1)}, f32[8,8]{0,1:T(8,128)S(1)}, u32[]{:S(2)}, u32[]{:S(2)}) collective-permute-start(f32[8,8]{0,1:T(8,128)S(1)} %add.52), channel_id=1, source_target_pairs={{0,32},{32,0},{64,96},{96,64},{128,160},{160,128},{192,224},{224,1... | collective-permute-start | bytes 776 | tf_op jit(solution)/shard_map/ppermute | solution.py:28
  77.7 3.6 %collective-permute-start.10 = (f32[8,8]{0,1:T(8,128)S(1)}, f32[8,8]{0,1:T(8,128)S(1)}, u32[]{:S(2)}, u32[]{:S(2)}) collective-permute-start(f32[8,8]{0,1:T(8,128)S(1)} %add.53), channel_id=1, source_target_pairs={{0,64},{32,96},{64,0},{96,32},{128,192},{160,224},{192,128},{224,1... | collective-permute-start | bytes 776 | tf_op jit(solution)/shard_map/ppermute | solution.py:28
  81.3 5.1 %collective-permute-start.11 = (f32[8,8]{0,1:T(8,128)S(1)}, f32[8,8]{0,1:T(8,128)S(1)}, u32[]{:S(2)}, u32[]{:S(2)}) collective-permute-start(f32[8,8]{0,1:T(8,128)S(1)} %add.54), channel_id=1, source_target_pairs={{0,128},{32,160},{64,192},{96,224},{128,0},{160,32},{192,64},{224,... | collective-permute-start | bytes 776 | tf_op jit(solution)/shard_map/ppermute | solution.py:28

commit v10 on v8

--- a/solution.py
+++ b/solution.py
@@ -233,7 +233,7 @@
     )
 
     gram = jnp.sum(partial, axis=(0, 2)).reshape(n_probes, n_probes)
-    gram = all_sum(gram, ("lon", "lat"))
+    gram = all_sum(gram, ("lat", "lon"))
     lower = jnp.linalg.cholesky(gram)
     upper = lower.T
     cells = field.shape[1] * width_lon * width_lat * lax.axis_size("lat") * lax.axis_size("lon")

time: 94.1 us -> 94.1 us (level)
  no operation moved by 1% of the time
where the time goes in v10:
time: 94.1 us; the launch traced here: 93.7 us
  waiting for transfers between devices  33.4 us (35%)
  starting transfers between devices  21.7 us (23%)
  Pallas kernels  19.8 us (21%)
  local copies, waits for them, and re-layouts  11 us (12%)
  other arithmetic  6.03 us (6%)
    ppermute x8, waiting for transfers between devices, all_sum(): lax.ppermute(value, axis, [(i, i ^ stride) for i in range(count)])  26.2 us
    pallas_call x1, Pallas kernels, transport(): pl.pallas_call(transport_kernel, grid=(levels,), in_specs=[pl.BlockSpec((...  15.9 us
    ppermute x8, starting transfers between devices, all_sum(): lax.ppermute(value, axis, [(i, i ^ stride) for i in range(count)])  8.05 us
    ppermute x1, starting transfers between devices, body(): lax.ppermute(heads, 'lon', [((i + 1) % n_lon, i) for i in range(n_lon)])  6.31 us
    ppermute x1, waiting for transfers between devices, body(): lax.ppermute(jnp.swapaxes(edge_hi, 2, 3), 'lat', [(j, j + 1) for j in ran...  5.98 us
    ppermute x1, starting transfers between devices, body(): lax.ppermute(jnp.swapaxes(edge_lo, 2, 3), 'lat', [(j + 1, j) for j in ran...  5.07 us
    unnamed x28, local copies, waits for them, and re-layouts  5.02 us
    pallas_call x1, Pallas kernels, basis(): pl.pallas_call(basis_kernel, grid=(levels,), in_specs=[pl.BlockSpec(memor...  3.9 us
  transfers between devices with their start and end apart: 12, of which 10 were waited for; matrix products, arithmetic and copies ran while one was open for 6% of the time, Pallas kernels for 0%

profile of v10, /device:TPU:6, one launch (start us, length us, event | category | flops | bytes accessed | tf_op | source)
XLA Modules:
  0.0 93.7 jit_solution(9245088195022639464)
XLA Ops:
  0.7 0.9 fusion.10
  1.5 0.8 fusion.11
  3.3 0.7 pad_maximum_fusion.1
  4.2 0.7 pad_maximum_fusion
  4.9 6.3 %collective-permute-start = (f32[4,13,8,128]{3,2,1,0:T(8,128)}, f32[4,13,8,128]{3,2,1,0:T(8,128)}, u32[]{:S(2)}, u32[]{:S(2)}) collective-permute-start(f32[4,13,8,128]{3,2,1,0:T(8,128)} %pad_maximum_fusion), channel_id=1, source_target_pairs={{1,0},{2,1},{3,2},{4,3},{5,4},{6,5},{7,6},{8,7},{9,8},{10,9},{11,1... | collective-permute-start | bytes 638984 | tf_op jit(solution)/shard_map/ppermute | solution.py:211
  12.2 0.8 copy-done.2
  14.4 0.7 slice_bitcast_fusion.2
  15.2 1.1 %fusion.13 = (f32[4,13,8,8]{3,2,1,0:T(8,128)S(1)}, f32[4,13,8,8]{3,2,1,0:T(8,128)S(1)}) fusion(f32[4,13,8,128]{3,2,1,0:T(8,128)} %collective-permute-done.1.lp_ref), kind=kLoop, calls=%fused_computation.41 | loop fusion | bytes 53248 | tf_op jit(solution)/shard_map/slice | solution.py:218
  16.6 1.1 %fusion.12 = (f32[4,13,8,8]{3,2,1,0:T(8,128)S(1)}, f32[4,13,8,8]{3,2,1,0:T(8,128)S(1)}) fusion(f32[4,13,8,128]{3,2,1,0:T(8,128)} %collective-permute-done.ln_ref), kind=kLoop, calls=%fused_computation.40 | loop fusion | bytes 53248 | tf_op jit(solution)/shard_map/slice | solution.py:218
  18.3 5.1 %collective-permute-start.2 = (f32[4,13,8,128]{3,2,1,0:T(8,128)S(1)}, f32[4,13,8,128]{3,2,1,0:T(8,128)S(1)}, u32[]{:S(2)}, u32[]{:S(2)}) collective-permute-start(f32[4,13,8,128]{3,2,1,0:T(8,128)S(1)} %get-tuple-element.33), channel_id=1, source_target_pairs={{32,0},{64,32},{96,64},{128,96},{160,128},{192,160},{224,192},{33,... | collective-permute-start | bytes 638984 | tf_op jit(solution)/shard_map/ppermute | solution.py:221
  23.4 2.3 %collective-permute-start.3 = (f32[4,13,8,128]{3,2,1,0:T(8,128)S(1)}, f32[4,13,8,128]{3,2,1,0:T(8,128)S(1)}, u32[]{:S(2)}, u32[]{:S(2)}) collective-permute-start(f32[4,13,8,128]{3,2,1,0:T(8,128)S(1)} %get-tuple-element.32), channel_id=1, source_target_pairs={{0,32},{32,64},{64,96},{96,128},{128,160},{160,192},{192,224},{1,3... | collective-permute-start | bytes 638984 | tf_op jit(solution)/shard_map/ppermute | solution.py:222
  26.3 1.3 %collective-permute-done.2.un_ref = f32[4,13,8,128]{3,2,1,0:T(8,128)S(1)} collective-permute-done((f32[4,13,8,128]{3,2,1,0:T(8,128)S(1)}, f32[4,13,8,128]{3,2,1,0:T(8,128)S(1)}, u32[]{:S(2)}, u32[]{:S(2)}) %collective-permute-start.2) | collective-permute-done | bytes 213024 | tf_op jit(solution)/shard_map/ppermute | solution.py:221
  27.5 6.0 %collective-permute-done.3.up_ref = f32[4,13,8,128]{3,2,1,0:T(8,128)S(1)} collective-permute-done((f32[4,13,8,128]{3,2,1,0:T(8,128)S(1)}, f32[4,13,8,128]{3,2,1,0:T(8,128)S(1)}, u32[]{:S(2)}, u32[]{:S(2)}) %collective-permute-start.3) | collective-permute-done | bytes 213024 | tf_op jit(solution)/shard_map/ppermute | solution.py:222
  33.5 0.7 copy-done.6
  34.2 15.9 %shard_map.59 = (f32[8,4,64,128]{3,2,1,0:T(8,128)}, f32[4,64,128]{2,1,0:T(8,128)}) custom-call(f32[8,256]{1,0:T(8,128)} %fusion.2.mask_ref, f32[8,4,64,128]{3,2,1,0:T(8,128)} %pr_ref.1, f32[2,4,64,128]{3,2,1,0:T(8,128)} %wi_ref.1, f32[2,4,64,128]{3,2,1,0:T(8,128)} %te_ref.1, f32[4,64,128]{2,1,0:T(8,128)} %ob_ref.1, ...), custom_call_target="tpu_custom_call" | custom-call | tf_op jit(solution)/shard_map/pallas_call | solution.py:133
  50.1 1.0 %reduce_sum.9 = f32[64]{0:T(128)S(1)} reduce(f32[4,64,128]{2,1,0:T(8,128)} %get-tuple-element.4, f32[]{:T(128)} %constant.61.clone.1), dimensions={0,2}, to_apply=%region_0.1 | reduce | flops 32704 | bytes 131332 | tf_op jit(solution)/shard_map/reduce_sum | solution.py:235
  51.3 5.1 %collective-permute-done.4 = f32[8,8]{0,1:T(8,128)S(1)} collective-permute-done((f32[8,8]{0,1:T(8,128)S(1)}, f32[8,8]{0,1:T(8,128)S(1)}, u32[]{:S(2)}, u32[]{:S(2)}) %collective-permute-start.4) | collective-permute-done | bytes 288 | tf_op jit(solution)/shard_map/ppermute | solution.py:28
  57.0 3.1 %collective-permute-done.5 = f32[8,8]{0,1:T(8,128)S(1)} collective-permute-done((f32[8,8]{0,1:T(8,128)S(1)}, f32[8,8]{0,1:T(8,128)S(1)}, u32[]{:S(2)}, u32[]{:S(2)}) %collective-permute-start.5) | collective-permute-done | bytes 288 | tf_op jit(solution)/shard_map/ppermute | solution.py:28
  60.0 1.1 %collective-permute-start.6 = (f32[8,8]{0,1:T(8,128)S(1)}, f32[8,8]{0,1:T(8,128)S(1)}, u32[]{:S(2)}, u32[]{:S(2)}) collective-permute-start(f32[8,8]{0,1:T(8,128)S(1)} %add.49), channel_id=1, source_target_pairs={{0,128},{32,160},{64,192},{96,224},{128,0},{160,32},{192,64},{224,... | collective-permute-start | bytes 776 | tf_op jit(solution)/shard_map/ppermute | solution.py:28
  61.1 4.0 %collective-permute-done.6 = f32[8,8]{0,1:T(8,128)S(1)} collective-permute-done((f32[8,8]{0,1:T(8,128)S(1)}, f32[8,8]{0,1:T(8,128)S(1)}, u32[]{:S(2)}, u32[]{:S(2)}) %collective-permute-start.6) | collective-permute-done | bytes 288 | tf_op jit(solution)/shard_map/ppermute | solution.py:28
  65.2 1.2 %collective-permute-done.7 = f32[8,8]{0,1:T(8,128)S(1)} collective-permute-done((f32[8,8]{0,1:T(8,128)S(1)}, f32[8,8]{0,1:T(8,128)S(1)}, u32[]{:S(2)}, u32[]{:S(2)}) %collective-permute-start.7) | collective-permute-done | bytes 288 | tf_op jit(solution)/shard_map/ppermute | solution.py:28
  66.3 3.6 %collective-permute-done.8 = f32[8,8]{0,1:T(8,128)S(1)} collective-permute-done((f32[8,8]{0,1:T(8,128)S(1)}, f32[8,8]{0,1:T(8,128)S(1)}, u32[]{:S(2)}, u32[]{:S(2)}) %collective-permute-start.8) | collective-permute-done | bytes 288 | tf_op jit(solution)/shard_map/ppermute | solution.py:28
  69.9 3.6 %collective-permute-done.9 = f32[8,8]{0,1:T(8,128)S(1)} collective-permute-done((f32[8,8]{0,1:T(8,128)S(1)}, f32[8,8]{0,1:T(8,128)S(1)}, u32[]{:S(2)}, u32[]{:S(2)}) %collective-permute-start.9) | collective-permute-done | bytes 288 | tf_op jit(solution)/shard_map/ppermute | solution.py:28
  74.2 3.9 %collective-permute-done.10 = f32[8,8]{0,1:T(8,128)S(1)} collective-permute-done((f32[8,8]{0,1:T(8,128)S(1)}, f32[8,8]{0,1:T(8,128)S(1)}, u32[]{:S(2)}, u32[]{:S(2)}) %collective-permute-start.10) | collective-permute-done | bytes 288 | tf_op jit(solution)/shard_map/ppermute | solution.py:28
  78.1 5.8 %collective-permute-start.11 = (f32[8,8]{0,1:T(8,128)S(1)}, f32[8,8]{0,1:T(8,128)S(1)}, u32[]{:S(2)}, u32[]{:S(2)}) collective-permute-start(f32[8,8]{0,1:T(8,128)S(1)} %add.54), channel_id=1, source_target_pairs={{0,16},{1,17},{2,18},{3,19},{4,20},{5,21},{6,22},{7,23},{8,24},{9,... | collective-permute-start | bytes 776 | tf_op jit(solution)/shard_map/ppermute | solution.py:28
  83.8 1.8 %collective-permute-done.11 = f32[8,8]{0,1:T(8,128)S(1)} collective-permute-done((f32[8,8]{0,1:T(8,128)S(1)}, f32[8,8]{0,1:T(8,128)S(1)}, u32[]{:S(2)}, u32[]{:S(2)}) %collective-permute-start.11) | collective-permute-done | bytes 288 | tf_op jit(solution)/shard_map/ppermute | solution.py:28
  85.7 0.7 cholesky.17
  86.4 0.6 compare_reduce_fusion
  87.1 0.6 multiply_bitcast_fusion
  88.3 0.8 fusion.3.inv_ref
  89.1 0.7 copy.53
  89.8 3.9 %shard_map.60 = f32[8,4,64,128]{3,2,1,0:T(8,128)} custom-call(f32[8,8]{1,0:T(8,128)} %fusion.3.inv_ref, f32[1,1]{1,0:T(1,128)} %constant.65.clone.1.scale_ref, f32[8,4,64,128]{3,2,1,0:T(8,128)} %get-tuple-element.5.z_ref), custom_call_target="tpu_custom_call" | custom-call | tf_op jit(solution)/shard_map/pallas_call | solution.py:181
  (63 shorter events, 7.0 us)
Async XLA Ops:
  0.6 1.7 %copy-start.4 = (f32[4,64,128]{2,1,0:T(8,128)S(1)}, f32[4,64,128]{2,1,0:T(8,128)}, u32[]{:S(2)}) copy-start(f32[4,64,128]{2,1,0:T(8,128)} %ob_ref.1) | copy-start | bytes 393220
  0.6 2.6 %copy-start = (f32[8,4,64,128]{3,2,1,0:T(8,128)S(1)}, f32[8,4,64,128]{3,2,1,0:T(8,128)}, u32[]{:S(2)}) copy-start(f32[8,4,64,128]{3,2,1,0:T(8,128)} %pr_ref.1) | copy-start | bytes 3145732
  2.4 0.7 copy-start.3
  4.0 11.1 %collective-permute-start.1 = (f32[4,13,8,128]{3,2,1,0:T(8,128)}, f32[4,13,8,128]{3,2,1,0:T(8,128)}, u32[]{:S(2)}, u32[]{:S(2)}) collective-permute-start(f32[4,13,8,128]{3,2,1,0:T(8,128)} %pad_maximum_fusion.1), channel_id=1, source_target_pairs={{0,1},{1,2},{2,3},{3,4},{4,5},{5,6},{6,7},{7,8},{8,9},{9,10},{10,1... | collective-permute-start | bytes 638984 | tf_op jit(solution)/shard_map/ppermute | solution.py:212
  4.9 11.7 %collective-permute-start = (f32[4,13,8,128]{3,2,1,0:T(8,128)}, f32[4,13,8,128]{3,2,1,0:T(8,128)}, u32[]{:S(2)}, u32[]{:S(2)}) collective-permute-start(f32[4,13,8,128]{3,2,1,0:T(8,128)} %pad_maximum_fusion), channel_id=1, source_target_pairs={{1,0},{2,1},{3,2},{4,3},{5,4},{6,5},{7,6},{8,7},{9,8},{10,9},{11,1... | collective-permute-start | bytes 638984 | tf_op jit(solution)/shard_map/ppermute | solution.py:211
  11.2 0.9 %copy-start.1 = (f32[2,4,64,128]{3,2,1,0:T(8,128)S(1)}, f32[2,4,64,128]{3,2,1,0:T(8,128)}, u32[]{:S(2)}) copy-start(f32[2,4,64,128]{3,2,1,0:T(8,128)} %wi_ref.1) | copy-start | bytes 786436
  12.1 0.9 %copy-start.2 = (f32[2,4,64,128]{3,2,1,0:T(8,128)S(1)}, f32[2,4,64,128]{3,2,1,0:T(8,128)}, u32[]{:S(2)}) copy-start(f32[2,4,64,128]{3,2,1,0:T(8,128)} %te_ref.1) | copy-start | bytes 786436
  18.3 9.2 %collective-permute-start.2 = (f32[4,13,8,128]{3,2,1,0:T(8,128)S(1)}, f32[4,13,8,128]{3,2,1,0:T(8,128)S(1)}, u32[]{:S(2)}, u32[]{:S(2)}) collective-permute-start(f32[4,13,8,128]{3,2,1,0:T(8,128)S(1)} %get-tuple-element.33), channel_id=1, source_target_pairs={{32,0},{64,32},{96,64},{128,96},{160,128},{192,160},{224,192},{33,... | collective-permute-start | bytes 638984 | tf_op jit(solution)/shard_map/ppermute | solution.py:221
  23.4 10.1 %collective-permute-start.3 = (f32[4,13,8,128]{3,2,1,0:T(8,128)S(1)}, f32[4,13,8,128]{3,2,1,0:T(8,128)S(1)}, u32[]{:S(2)}, u32[]{:S(2)}) collective-permute-start(f32[4,13,8,128]{3,2,1,0:T(8,128)S(1)} %get-tuple-element.32), channel_id=1, source_target_pairs={{0,32},{32,64},{64,96},{96,128},{128,160},{160,192},{192,224},{1,3... | collective-permute-start | bytes 638984 | tf_op jit(solution)/shard_map/ppermute | solution.py:222
  27.5 6.0 %copy-start.5 = (f32[4,13,8,128]{3,2,1,0:T(8,128)}, f32[4,13,8,128]{3,2,1,0:T(8,128)S(1)}, u32[]{:S(2)}) copy-start(f32[4,13,8,128]{3,2,1,0:T(8,128)S(1)} %collective-permute-done.2.un_ref) | copy-start | bytes 638980
  33.5 0.7 copy-start.6
  51.3 5.1 %collective-permute-start.4 = (f32[8,8]{0,1:T(8,128)S(1)}, f32[8,8]{0,1:T(8,128)S(1)}, u32[]{:S(2)}, u32[]{:S(2)}) collective-permute-start(f32[8,8]{0,1:T(8,128)S(1)} %copy.50), channel_id=1, source_target_pairs={{0,32},{32,0},{64,96},{96,64},{128,160},{160,128},{192,224},{224,1... | collective-permute-start | bytes 776 | tf_op jit(solution)/shard_map/ppermute | solution.py:28
  56.4 3.6 %collective-permute-start.5 = (f32[8,8]{0,1:T(8,128)S(1)}, f32[8,8]{0,1:T(8,128)S(1)}, u32[]{:S(2)}, u32[]{:S(2)}) collective-permute-start(f32[8,8]{0,1:T(8,128)S(1)} %add.48), channel_id=1, source_target_pairs={{0,64},{32,96},{64,0},{96,32},{128,192},{160,224},{192,128},{224,1... | collective-permute-start | bytes 776 | tf_op jit(solution)/shard_map/ppermute | solution.py:28
  60.0 5.1 %collective-permute-start.6 = (f32[8,8]{0,1:T(8,128)S(1)}, f32[8,8]{0,1:T(8,128)S(1)}, u32[]{:S(2)}, u32[]{:S(2)}) collective-permute-start(f32[8,8]{0,1:T(8,128)S(1)} %add.49), channel_id=1, source_target_pairs={{0,128},{32,160},{64,192},{96,224},{128,0},{160,32},{192,64},{224,... | collective-permute-start | bytes 776 | tf_op jit(solution)/shard_map/ppermute | solution.py:28
  65.2 1.2 %collective-permute-start.7 = (f32[8,8]{0,1:T(8,128)S(1)}, f32[8,8]{0,1:T(8,128)S(1)}, u32[]{:S(2)}, u32[]{:S(2)}) collective-permute-start(f32[8,8]{0,1:T(8,128)S(1)} %add.50), channel_id=1, source_target_pairs={{0,1},{1,0},{2,3},{3,2},{4,5},{5,4},{6,7},{7,6},{8,9},{9,8},{10,11... | collective-permute-start | bytes 776 | tf_op jit(solution)/shard_map/ppermute | solution.py:28
  66.3 3.6 %collective-permute-start.8 = (f32[8,8]{0,1:T(8,128)S(1)}, f32[8,8]{0,1:T(8,128)S(1)}, u32[]{:S(2)}, u32[]{:S(2)}) collective-permute-start(f32[8,8]{0,1:T(8,128)S(1)} %add.51), channel_id=1, source_target_pairs={{0,2},{1,3},{2,0},{3,1},{4,6},{5,7},{6,4},{7,5},{8,10},{9,11},{10,... | collective-permute-start | bytes 776 | tf_op jit(solution)/shard_map/ppermute | solution.py:28
  69.9 3.6 %collective-permute-start.9 = (f32[8,8]{0,1:T(8,128)S(1)}, f32[8,8]{0,1:T(8,128)S(1)}, u32[]{:S(2)}, u32[]{:S(2)}) collective-permute-start(f32[8,8]{0,1:T(8,128)S(1)} %add.52), channel_id=1, source_target_pairs={{0,4},{1,5},{2,6},{3,7},{4,0},{5,1},{6,2},{7,3},{8,12},{9,13},{10,... | collective-permute-start | bytes 776 | tf_op jit(solution)/shard_map/ppermute | solution.py:28
  73.5 4.5 %collective-permute-start.10 = (f32[8,8]{0,1:T(8,128)S(1)}, f32[8,8]{0,1:T(8,128)S(1)}, u32[]{:S(2)}, u32[]{:S(2)}) collective-permute-start(f32[8,8]{0,1:T(8,128)S(1)} %add.53), channel_id=1, source_target_pairs={{0,8},{1,9},{2,10},{3,11},{4,12},{5,13},{6,14},{7,15},{8,0},{9,1},... | collective-permute-start | bytes 776 | tf_op jit(solution)/shard_map/ppermute | solution.py:28
  78.1 7.5 %collective-permute-start.11 = (f32[8,8]{0,1:T(8,128)S(1)}, f32[8,8]{0,1:T(8,128)S(1)}, u32[]{:S(2)}, u32[]{:S(2)}) collective-permute-start(f32[8,8]{0,1:T(8,128)S(1)} %add.54), channel_id=1, source_target_pairs={{0,16},{1,17},{2,18},{3,19},{4,20},{5,21},{6,22},{7,23},{8,24},{9,... | collective-permute-start | bytes 776 | tf_op jit(solution)/shard_map/ppermute | solution.py:28

commit v11 on v8

--- a/solution.py
+++ b/solution.py
@@ -159,37 +159,37 @@
     )(mask, probes, wind, wind_tend, obs_weight, lon_next, lon_prev, lat_next, lat_prev)
 
 def basis_kernel(inv_ref, scale_ref, z_ref, o_ref):
-    probes = z_ref.shape[0]
+    probes, levels, rows = z_ref.shape[:3]
     scale = scale_ref[0, 0]
+    chunks = rows // 8
 
     def chunk(c, carry):
-        rows = pl.ds(c * 8, 8)
-        z = [z_ref[q, 0, rows, :] for q in range(probes)]
+        level = c // chunks
+        part = pl.ds((c % chunks) * 8, 8)
+        z = [z_ref[q, level, part, :] for q in range(probes)]
         for p in range(probes):
             acc = inv_ref[p, 0] * z[0]
             for q in range(1, probes):
                 acc = acc + inv_ref[p, q] * z[q]
-            o_ref[p, 0, rows, :] = acc * scale
+            o_ref[p, level, part, :] = acc * scale
         return carry
 
-    lax.fori_loop(0, z_ref.shape[2] // 8, chunk, 0)
+    lax.fori_loop(0, levels * chunks, chunk, 0)
 
 
 def basis(inverse, scale, field):
-    probes, levels, rows, lanes = field.shape
-    block = pl.BlockSpec((probes, 1, rows, lanes), lambda l: (0, l, 0, 0))
+    whole = pl.BlockSpec(field.shape, lambda i: (0, 0, 0, 0))
     return pl.pallas_call(
         basis_kernel,
-        grid=(levels,),
+        grid=(1,),
         in_specs=[
             pl.BlockSpec(memory_space=pltpu.SMEM),
             pl.BlockSpec(memory_space=pltpu.SMEM),
-            block,
-        ],
-        out_specs=block,
+            whole,
+        ],
+        out_specs=whole,
         out_shape=jax.ShapeDtypeStruct(field.shape, jnp.float32),
     )(inverse, scale, field)
-
 
 def body(probes, wind, wind_tend, obs_weight):
     n_probes, levels, width_lon, width_lat = probes.shape

time: 94.1 us -> 93.7 us (level)
  no operation moved by 1% of the time
where the time goes in v11:
time: 93.7 us; the launch traced here: 93.3 us
  waiting for transfers between devices  33.4 us (36%)
  starting transfers between devices  21.7 us (23%)
  Pallas kernels  19.4 us (21%)
  local copies, waits for them, and re-layouts  11 us (12%)
  other arithmetic  6.03 us (6%)
    ppermute x8, waiting for transfers between devices, all_sum(): lax.ppermute(value, axis, [(i, i ^ stride) for i in range(count)])  26.2 us
    pallas_call x1, Pallas kernels, transport(): pl.pallas_call(transport_kernel, grid=(levels,), in_specs=[pl.BlockSpec((...  15.9 us
    ppermute x8, starting transfers between devices, all_sum(): lax.ppermute(value, axis, [(i, i ^ stride) for i in range(count)])  8.05 us
    ppermute x1, starting transfers between devices, body(): lax.ppermute(heads, 'lon', [((i + 1) % n_lon, i) for i in range(n_lon)])  6.31 us
    ppermute x1, waiting for transfers between devices, body(): lax.ppermute(jnp.swapaxes(edge_hi, 2, 3), 'lat', [(j, j + 1) for j in ran...  5.98 us
    ppermute x1, starting transfers between devices, body(): lax.ppermute(jnp.swapaxes(edge_lo, 2, 3), 'lat', [(j + 1, j) for j in ran...  5.07 us
    unnamed x28, local copies, waits for them, and re-layouts  5.02 us
    pallas_call x1, Pallas kernels, basis(): pl.pallas_call(basis_kernel, grid=(1,), in_specs=[pl.BlockSpec(memory_spa...  3.48 us
  transfers between devices with their start and end apart: 12, of which 10 were waited for; matrix products, arithmetic and copies ran while one was open for 6% of the time, Pallas kernels for 0%

profile of v11, /device:TPU:6, one launch (start us, length us, event | category | flops | bytes accessed | tf_op | source)
XLA Modules:
  0.0 93.3 jit_solution(5822504611026993204)
XLA Ops:
  0.7 0.9 fusion.10
  1.5 0.8 fusion.11
  3.3 0.7 pad_maximum_fusion.1
  4.2 0.7 pad_maximum_fusion
  4.9 6.3 %collective-permute-start = (f32[4,13,8,128]{3,2,1,0:T(8,128)}, f32[4,13,8,128]{3,2,1,0:T(8,128)}, u32[]{:S(2)}, u32[]{:S(2)}) collective-permute-start(f32[4,13,8,128]{3,2,1,0:T(8,128)} %pad_maximum_fusion), channel_id=1, source_target_pairs={{1,0},{2,1},{3,2},{4,3},{5,4},{6,5},{7,6},{8,7},{9,8},{10,9},{11,1... | collective-permute-start | bytes 638984 | tf_op jit(solution)/shard_map/ppermute | solution.py:211
  12.2 0.8 copy-done.2
  14.4 0.7 slice_bitcast_fusion.2
  15.2 1.1 %fusion.13 = (f32[4,13,8,8]{3,2,1,0:T(8,128)S(1)}, f32[4,13,8,8]{3,2,1,0:T(8,128)S(1)}) fusion(f32[4,13,8,128]{3,2,1,0:T(8,128)} %collective-permute-done.1.lp_ref), kind=kLoop, calls=%fused_computation.41 | loop fusion | bytes 53248 | tf_op jit(solution)/shard_map/slice | solution.py:218
  16.6 1.1 %fusion.12 = (f32[4,13,8,8]{3,2,1,0:T(8,128)S(1)}, f32[4,13,8,8]{3,2,1,0:T(8,128)S(1)}) fusion(f32[4,13,8,128]{3,2,1,0:T(8,128)} %collective-permute-done.ln_ref), kind=kLoop, calls=%fused_computation.40 | loop fusion | bytes 53248 | tf_op jit(solution)/shard_map/slice | solution.py:218
  18.3 5.1 %collective-permute-start.2 = (f32[4,13,8,128]{3,2,1,0:T(8,128)S(1)}, f32[4,13,8,128]{3,2,1,0:T(8,128)S(1)}, u32[]{:S(2)}, u32[]{:S(2)}) collective-permute-start(f32[4,13,8,128]{3,2,1,0:T(8,128)S(1)} %get-tuple-element.33), channel_id=1, source_target_pairs={{32,0},{64,32},{96,64},{128,96},{160,128},{192,160},{224,192},{33,... | collective-permute-start | bytes 638984 | tf_op jit(solution)/shard_map/ppermute | solution.py:221
  23.4 2.3 %collective-permute-start.3 = (f32[4,13,8,128]{3,2,1,0:T(8,128)S(1)}, f32[4,13,8,128]{3,2,1,0:T(8,128)S(1)}, u32[]{:S(2)}, u32[]{:S(2)}) collective-permute-start(f32[4,13,8,128]{3,2,1,0:T(8,128)S(1)} %get-tuple-element.32), channel_id=1, source_target_pairs={{0,32},{32,64},{64,96},{96,128},{128,160},{160,192},{192,224},{1,3... | collective-permute-start | bytes 638984 | tf_op jit(solution)/shard_map/ppermute | solution.py:222
  26.3 1.3 %collective-permute-done.2.un_ref = f32[4,13,8,128]{3,2,1,0:T(8,128)S(1)} collective-permute-done((f32[4,13,8,128]{3,2,1,0:T(8,128)S(1)}, f32[4,13,8,128]{3,2,1,0:T(8,128)S(1)}, u32[]{:S(2)}, u32[]{:S(2)}) %collective-permute-start.2) | collective-permute-done | bytes 213024 | tf_op jit(solution)/shard_map/ppermute | solution.py:221
  27.5 6.0 %collective-permute-done.3.up_ref = f32[4,13,8,128]{3,2,1,0:T(8,128)S(1)} collective-permute-done((f32[4,13,8,128]{3,2,1,0:T(8,128)S(1)}, f32[4,13,8,128]{3,2,1,0:T(8,128)S(1)}, u32[]{:S(2)}, u32[]{:S(2)}) %collective-permute-start.3) | collective-permute-done | bytes 213024 | tf_op jit(solution)/shard_map/ppermute | solution.py:222
  33.5 0.7 copy-done.6
  34.2 15.9 %shard_map.59 = (f32[8,4,64,128]{3,2,1,0:T(8,128)}, f32[4,64,128]{2,1,0:T(8,128)}) custom-call(f32[8,256]{1,0:T(8,128)} %fusion.2.mask_ref, f32[8,4,64,128]{3,2,1,0:T(8,128)} %pr_ref.1, f32[2,4,64,128]{3,2,1,0:T(8,128)} %wi_ref.1, f32[2,4,64,128]{3,2,1,0:T(8,128)} %te_ref.1, f32[4,64,128]{2,1,0:T(8,128)} %ob_ref.1, ...), custom_call_target="tpu_custom_call" | custom-call | tf_op jit(solution)/shard_map/pallas_call | solution.py:133
  50.1 1.0 %reduce_sum.9 = f32[64]{0:T(128)S(1)} reduce(f32[4,64,128]{2,1,0:T(8,128)} %get-tuple-element.4, f32[]{:T(128)} %constant.61.clone.1), dimensions={0,2}, to_apply=%region_0.1 | reduce | flops 32704 | bytes 131332 | tf_op jit(solution)/shard_map/reduce_sum | solution.py:235
  51.3 1.2 %collective-permute-done.4 = f32[8,8]{0,1:T(8,128)S(1)} collective-permute-done((f32[8,8]{0,1:T(8,128)S(1)}, f32[8,8]{0,1:T(8,128)S(1)}, u32[]{:S(2)}, u32[]{:S(2)}) %collective-permute-start.4) | collective-permute-done | bytes 288 | tf_op jit(solution)/shard_map/ppermute | solution.py:28
  52.5 3.6 %collective-permute-done.5 = f32[8,8]{0,1:T(8,128)S(1)} collective-permute-done((f32[8,8]{0,1:T(8,128)S(1)}, f32[8,8]{0,1:T(8,128)S(1)}, u32[]{:S(2)}, u32[]{:S(2)}) %collective-permute-start.5) | collective-permute-done | bytes 288 | tf_op jit(solution)/shard_map/ppermute | solution.py:28
  56.1 3.6 %collective-permute-done.6 = f32[8,8]{0,1:T(8,128)S(1)} collective-permute-done((f32[8,8]{0,1:T(8,128)S(1)}, f32[8,8]{0,1:T(8,128)S(1)}, u32[]{:S(2)}, u32[]{:S(2)}) %collective-permute-start.6) | collective-permute-done | bytes 288 | tf_op jit(solution)/shard_map/ppermute | solution.py:28
  60.3 3.9 %collective-permute-done.7 = f32[8,8]{0,1:T(8,128)S(1)} collective-permute-done((f32[8,8]{0,1:T(8,128)S(1)}, f32[8,8]{0,1:T(8,128)S(1)}, u32[]{:S(2)}, u32[]{:S(2)}) %collective-permute-start.7) | collective-permute-done | bytes 288 | tf_op jit(solution)/shard_map/ppermute | solution.py:28
  64.2 5.8 %collective-permute-start.8 = (f32[8,8]{0,1:T(8,128)S(1)}, f32[8,8]{0,1:T(8,128)S(1)}, u32[]{:S(2)}, u32[]{:S(2)}) collective-permute-start(f32[8,8]{0,1:T(8,128)S(1)} %add.51), channel_id=1, source_target_pairs={{0,16},{1,17},{2,18},{3,19},{4,20},{5,21},{6,22},{7,23},{8,24},{9,... | collective-permute-start | bytes 776 | tf_op jit(solution)/shard_map/ppermute | solution.py:28
  70.0 1.8 %collective-permute-done.8 = f32[8,8]{0,1:T(8,128)S(1)} collective-permute-done((f32[8,8]{0,1:T(8,128)S(1)}, f32[8,8]{0,1:T(8,128)S(1)}, u32[]{:S(2)}, u32[]{:S(2)}) %collective-permute-start.8) | collective-permute-done | bytes 288 | tf_op jit(solution)/shard_map/ppermute | solution.py:28
  71.7 5.1 %collective-permute-done.9 = f32[8,8]{0,1:T(8,128)S(1)} collective-permute-done((f32[8,8]{0,1:T(8,128)S(1)}, f32[8,8]{0,1:T(8,128)S(1)}, u32[]{:S(2)}, u32[]{:S(2)}) %collective-permute-start.9) | collective-permute-done | bytes 288 | tf_op jit(solution)/shard_map/ppermute | solution.py:28
  77.4 3.1 %collective-permute-done.10 = f32[8,8]{0,1:T(8,128)S(1)} collective-permute-done((f32[8,8]{0,1:T(8,128)S(1)}, f32[8,8]{0,1:T(8,128)S(1)}, u32[]{:S(2)}, u32[]{:S(2)}) %collective-permute-start.10) | collective-permute-done | bytes 288 | tf_op jit(solution)/shard_map/ppermute | solution.py:28
  80.5 1.1 %collective-permute-start.11 = (f32[8,8]{0,1:T(8,128)S(1)}, f32[8,8]{0,1:T(8,128)S(1)}, u32[]{:S(2)}, u32[]{:S(2)}) collective-permute-start(f32[8,8]{0,1:T(8,128)S(1)} %add.54), channel_id=1, source_target_pairs={{0,128},{32,160},{64,192},{96,224},{128,0},{160,32},{192,64},{224,... | collective-permute-start | bytes 776 | tf_op jit(solution)/shard_map/ppermute | solution.py:28
  81.6 4.0 %collective-permute-done.11 = f32[8,8]{0,1:T(8,128)S(1)} collective-permute-done((f32[8,8]{0,1:T(8,128)S(1)}, f32[8,8]{0,1:T(8,128)S(1)}, u32[]{:S(2)}, u32[]{:S(2)}) %collective-permute-start.11) | collective-permute-done | bytes 288 | tf_op jit(solution)/shard_map/ppermute | solution.py:28
  85.7 0.7 cholesky.17
  86.4 0.6 compare_reduce_fusion
  87.1 0.6 multiply_bitcast_fusion
  88.3 0.8 fusion.3.inv_ref
  89.1 0.7 copy.53
  89.8 3.5 %shard_map.60 = f32[8,4,64,128]{3,2,1,0:T(8,128)} custom-call(f32[8,8]{1,0:T(8,128)} %fusion.3.inv_ref, f32[1,1]{1,0:T(1,128)} %constant.65.clone.1.scale_ref, f32[8,4,64,128]{3,2,1,0:T(8,128)} %get-tuple-element.5.z_ref), custom_call_target="tpu_custom_call" | custom-call | tf_op jit(solution)/shard_map/pallas_call | solution.py:182
  (63 shorter events, 7.0 us)
Async XLA Ops:
  0.6 1.7 %copy-start.4 = (f32[4,64,128]{2,1,0:T(8,128)S(1)}, f32[4,64,128]{2,1,0:T(8,128)}, u32[]{:S(2)}) copy-start(f32[4,64,128]{2,1,0:T(8,128)} %ob_ref.1) | copy-start | bytes 393220
  0.6 2.6 %copy-start = (f32[8,4,64,128]{3,2,1,0:T(8,128)S(1)}, f32[8,4,64,128]{3,2,1,0:T(8,128)}, u32[]{:S(2)}) copy-start(f32[8,4,64,128]{3,2,1,0:T(8,128)} %pr_ref.1) | copy-start | bytes 3145732
  2.4 0.7 copy-start.3
  4.0 11.1 %collective-permute-start.1 = (f32[4,13,8,128]{3,2,1,0:T(8,128)}, f32[4,13,8,128]{3,2,1,0:T(8,128)}, u32[]{:S(2)}, u32[]{:S(2)}) collective-permute-start(f32[4,13,8,128]{3,2,1,0:T(8,128)} %pad_maximum_fusion.1), channel_id=1, source_target_pairs={{0,1},{1,2},{2,3},{3,4},{4,5},{5,6},{6,7},{7,8},{8,9},{9,10},{10,1... | collective-permute-start | bytes 638984 | tf_op jit(solution)/shard_map/ppermute | solution.py:212
  4.9 11.7 %collective-permute-start = (f32[4,13,8,128]{3,2,1,0:T(8,128)}, f32[4,13,8,128]{3,2,1,0:T(8,128)}, u32[]{:S(2)}, u32[]{:S(2)}) collective-permute-start(f32[4,13,8,128]{3,2,1,0:T(8,128)} %pad_maximum_fusion), channel_id=1, source_target_pairs={{1,0},{2,1},{3,2},{4,3},{5,4},{6,5},{7,6},{8,7},{9,8},{10,9},{11,1... | collective-permute-start | bytes 638984 | tf_op jit(solution)/shard_map/ppermute | solution.py:211
  11.2 0.9 %copy-start.1 = (f32[2,4,64,128]{3,2,1,0:T(8,128)S(1)}, f32[2,4,64,128]{3,2,1,0:T(8,128)}, u32[]{:S(2)}) copy-start(f32[2,4,64,128]{3,2,1,0:T(8,128)} %wi_ref.1) | copy-start | bytes 786436
  12.1 0.9 %copy-start.2 = (f32[2,4,64,128]{3,2,1,0:T(8,128)S(1)}, f32[2,4,64,128]{3,2,1,0:T(8,128)}, u32[]{:S(2)}) copy-start(f32[2,4,64,128]{3,2,1,0:T(8,128)} %te_ref.1) | copy-start | bytes 786436
  18.3 9.2 %collective-permute-start.2 = (f32[4,13,8,128]{3,2,1,0:T(8,128)S(1)}, f32[4,13,8,128]{3,2,1,0:T(8,128)S(1)}, u32[]{:S(2)}, u32[]{:S(2)}) collective-permute-start(f32[4,13,8,128]{3,2,1,0:T(8,128)S(1)} %get-tuple-element.33), channel_id=1, source_target_pairs={{32,0},{64,32},{96,64},{128,96},{160,128},{192,160},{224,192},{33,... | collective-permute-start | bytes 638984 | tf_op jit(solution)/shard_map/ppermute | solution.py:221
  23.4 10.1 %collective-permute-start.3 = (f32[4,13,8,128]{3,2,1,0:T(8,128)S(1)}, f32[4,13,8,128]{3,2,1,0:T(8,128)S(1)}, u32[]{:S(2)}, u32[]{:S(2)}) collective-permute-start(f32[4,13,8,128]{3,2,1,0:T(8,128)S(1)} %get-tuple-element.32), channel_id=1, source_target_pairs={{0,32},{32,64},{64,96},{96,128},{128,160},{160,192},{192,224},{1,3... | collective-permute-start | bytes 638984 | tf_op jit(solution)/shard_map/ppermute | solution.py:222
  27.5 6.0 %copy-start.5 = (f32[4,13,8,128]{3,2,1,0:T(8,128)}, f32[4,13,8,128]{3,2,1,0:T(8,128)S(1)}, u32[]{:S(2)}) copy-start(f32[4,13,8,128]{3,2,1,0:T(8,128)S(1)} %collective-permute-done.2.un_ref) | copy-start | bytes 638980
  33.5 0.7 copy-start.6
  51.3 1.2 %collective-permute-start.4 = (f32[8,8]{0,1:T(8,128)S(1)}, f32[8,8]{0,1:T(8,128)S(1)}, u32[]{:S(2)}, u32[]{:S(2)}) collective-permute-start(f32[8,8]{0,1:T(8,128)S(1)} %copy.50), channel_id=1, source_target_pairs={{0,1},{1,0},{2,3},{3,2},{4,5},{5,4},{6,7},{7,6},{8,9},{9,8},{10,11... | collective-permute-start | bytes 776 | tf_op jit(solution)/shard_map/ppermute | solution.py:28
  52.5 3.6 %collective-permute-start.5 = (f32[8,8]{0,1:T(8,128)S(1)}, f32[8,8]{0,1:T(8,128)S(1)}, u32[]{:S(2)}, u32[]{:S(2)}) collective-permute-start(f32[8,8]{0,1:T(8,128)S(1)} %add.48), channel_id=1, source_target_pairs={{0,2},{1,3},{2,0},{3,1},{4,6},{5,7},{6,4},{7,5},{8,10},{9,11},{10,... | collective-permute-start | bytes 776 | tf_op jit(solution)/shard_map/ppermute | solution.py:28
  56.1 3.6 %collective-permute-start.6 = (f32[8,8]{0,1:T(8,128)S(1)}, f32[8,8]{0,1:T(8,128)S(1)}, u32[]{:S(2)}, u32[]{:S(2)}) collective-permute-start(f32[8,8]{0,1:T(8,128)S(1)} %add.49), channel_id=1, source_target_pairs={{0,4},{1,5},{2,6},{3,7},{4,0},{5,1},{6,2},{7,3},{8,12},{9,13},{10,... | collective-permute-start | bytes 776 | tf_op jit(solution)/shard_map/ppermute | solution.py:28
  59.7 4.5 %collective-permute-start.7 = (f32[8,8]{0,1:T(8,128)S(1)}, f32[8,8]{0,1:T(8,128)S(1)}, u32[]{:S(2)}, u32[]{:S(2)}) collective-permute-start(f32[8,8]{0,1:T(8,128)S(1)} %add.50), channel_id=1, source_target_pairs={{0,8},{1,9},{2,10},{3,11},{4,12},{5,13},{6,14},{7,15},{8,0},{9,1},... | collective-permute-start | bytes 776 | tf_op jit(solution)/shard_map/ppermute | solution.py:28
  64.2 7.5 %collective-permute-start.8 = (f32[8,8]{0,1:T(8,128)S(1)}, f32[8,8]{0,1:T(8,128)S(1)}, u32[]{:S(2)}, u32[]{:S(2)}) collective-permute-start(f32[8,8]{0,1:T(8,128)S(1)} %add.51), channel_id=1, source_target_pairs={{0,16},{1,17},{2,18},{3,19},{4,20},{5,21},{6,22},{7,23},{8,24},{9,... | collective-permute-start | bytes 776 | tf_op jit(solution)/shard_map/ppermute | solution.py:28
  71.7 5.1 %collective-permute-start.9 = (f32[8,8]{0,1:T(8,128)S(1)}, f32[8,8]{0,1:T(8,128)S(1)}, u32[]{:S(2)}, u32[]{:S(2)}) collective-permute-start(f32[8,8]{0,1:T(8,128)S(1)} %add.52), channel_id=1, source_target_pairs={{0,32},{32,0},{64,96},{96,64},{128,160},{160,128},{192,224},{224,1... | collective-permute-start | bytes 776 | tf_op jit(solution)/shard_map/ppermute | solution.py:28
  76.8 3.6 %collective-permute-start.10 = (f32[8,8]{0,1:T(8,128)S(1)}, f32[8,8]{0,1:T(8,128)S(1)}, u32[]{:S(2)}, u32[]{:S(2)}) collective-permute-start(f32[8,8]{0,1:T(8,128)S(1)} %add.53), channel_id=1, source_target_pairs={{0,64},{32,96},{64,0},{96,32},{128,192},{160,224},{192,128},{224,1... | collective-permute-start | bytes 776 | tf_op jit(solution)/shard_map/ppermute | solution.py:28
  80.5 5.1 %collective-permute-start.11 = (f32[8,8]{0,1:T(8,128)S(1)}, f32[8,8]{0,1:T(8,128)S(1)}, u32[]{:S(2)}, u32[]{:S(2)}) collective-permute-start(f32[8,8]{0,1:T(8,128)S(1)} %add.54), channel_id=1, source_target_pairs={{0,128},{32,160},{64,192},{96,224},{128,0},{160,32},{192,64},{224,... | collective-permute-start | bytes 776 | tf_op jit(solution)/shard_map/ppermute | solution.py:28

commit v12 on v11

--- a/solution.py
+++ b/solution.py
@@ -109,13 +109,17 @@
         return carry
 
     lax.fori_loop(0, probes // GROUP, probe_pair, 0)
+    @pl.when(pl.program_id(0) == 0)
+    def _():
+        g_ref[...] = jnp.zeros(g_ref.shape, jnp.float32)
+
     for p in range(probes):
         for q in range(p, probes):
             prod = (o_ref[p, 0] * o_ref[q, 0]).reshape(rows // 8, 8, lanes)
             part = jnp.sum(jnp.sum(prod, axis=0), axis=0, keepdims=True)
-            g_ref[0, pl.ds(p * probes + q, 1), :] = part
+            g_ref[pl.ds(p * probes + q, 1), :] += part
             if q != p:
-                g_ref[0, pl.ds(q * probes + p, 1), :] = part
+                g_ref[pl.ds(q * probes + p, 1), :] += part
 
 
 def transport(mask, probes, wind, wind_tend, obs_weight, lon_next, lon_prev, lat_next, lat_prev):
@@ -146,11 +150,11 @@
         ],
         out_specs=[
             level_block(n_probes),
-            pl.BlockSpec((1, n_probes * n_probes, lanes), lambda l: (l, 0, 0)),
+            pl.BlockSpec((n_probes * n_probes, lanes), lambda l: (0, 0)),
         ],
         out_shape=[
             jax.ShapeDtypeStruct((n_probes, levels, rows, lanes), jnp.float32),
-            jax.ShapeDtypeStruct((levels, n_probes * n_probes, lanes), jnp.float32),
+            jax.ShapeDtypeStruct((n_probes * n_probes, lanes), jnp.float32),
         ],
         scratch_shapes=[
             pltpu.VMEM((STEPS + 1, 8, full_rows, full_lanes), jnp.float32),
@@ -232,7 +236,7 @@
         mask, probes, wind, wind_tend, obs_weight, lon_next, lon_prev, lat_next, lat_prev
     )
 
-    gram = jnp.sum(partial, axis=(0, 2)).reshape(n_probes, n_probes)
+    gram = jnp.sum(partial, axis=1).reshape(n_probes, n_probes)
     gram = all_sum(gram, ("lon", "lat"))
     lower = jnp.linalg.cholesky(gram)
     upper = lower.T

time: 93.7 us -> 94.1 us (level)
  no operation moved by 1% of the time
where the time goes in v12:
time: 94.1 us; the launch traced here: 93.6 us
  waiting for transfers between devices  33.5 us (36%)
  starting transfers between devices  21.7 us (23%)
  Pallas kernels  19.9 us (21%)
  local copies, waits for them, and re-layouts  11 us (12%)
  other arithmetic  5.87 us (6%)
    ppermute x8, waiting for transfers between devices, all_sum(): lax.ppermute(value, axis, [(i, i ^ stride) for i in range(count)])  26.2 us
    pallas_call x1, Pallas kernels, transport(): pl.pallas_call(transport_kernel, grid=(levels,), in_specs=[pl.BlockSpec((...  16.5 us
    ppermute x8, starting transfers between devices, all_sum(): lax.ppermute(value, axis, [(i, i ^ stride) for i in range(count)])  8.05 us
    ppermute x1, starting transfers between devices, body(): lax.ppermute(heads, 'lon', [((i + 1) % n_lon, i) for i in range(n_lon)])  6.31 us
    ppermute x1, waiting for transfers between devices, body(): lax.ppermute(jnp.swapaxes(edge_hi, 2, 3), 'lat', [(j, j + 1) for j in ran...  5.98 us
    ppermute x1, starting transfers between devices, body(): lax.ppermute(jnp.swapaxes(edge_lo, 2, 3), 'lat', [(j + 1, j) for j in ran...  5.07 us
    unnamed x28, local copies, waits for them, and re-layouts  5.02 us
    pallas_call x1, Pallas kernels, basis(): pl.pallas_call(basis_kernel, grid=(1,), in_specs=[pl.BlockSpec(memory_spa...  3.48 us
  transfers between devices with their start and end apart: 12, of which 10 were waited for; matrix products, arithmetic and copies ran while one was open for 6% of the time, Pallas kernels for 0%

profile of v12, /device:TPU:6, one launch (start us, length us, event | category | flops | bytes accessed | tf_op | source)
XLA Modules:
  0.0 93.6 jit_solution(14441125260086156055)
XLA Ops:
  0.7 0.9 fusion.10
  1.5 0.8 fusion.11
  3.3 0.7 pad_maximum_fusion.1
  4.2 0.7 pad_maximum_fusion
  4.9 6.3 %collective-permute-start = (f32[4,13,8,128]{3,2,1,0:T(8,128)}, f32[4,13,8,128]{3,2,1,0:T(8,128)}, u32[]{:S(2)}, u32[]{:S(2)}) collective-permute-start(f32[4,13,8,128]{3,2,1,0:T(8,128)} %pad_maximum_fusion), channel_id=1, source_target_pairs={{1,0},{2,1},{3,2},{4,3},{5,4},{6,5},{7,6},{8,7},{9,8},{10,9},{11,1... | collective-permute-start | bytes 638984 | tf_op jit(solution)/shard_map/ppermute | solution.py:215
  12.2 0.8 copy-done.2
  14.4 0.7 slice_bitcast_fusion.2
  15.2 1.1 %fusion.13 = (f32[4,13,8,8]{3,2,1,0:T(8,128)S(1)}, f32[4,13,8,8]{3,2,1,0:T(8,128)S(1)}) fusion(f32[4,13,8,128]{3,2,1,0:T(8,128)} %collective-permute-done.1.lp_ref), kind=kLoop, calls=%fused_computation.41 | loop fusion | bytes 53248 | tf_op jit(solution)/shard_map/slice | solution.py:222
  16.6 1.1 %fusion.12 = (f32[4,13,8,8]{3,2,1,0:T(8,128)S(1)}, f32[4,13,8,8]{3,2,1,0:T(8,128)S(1)}) fusion(f32[4,13,8,128]{3,2,1,0:T(8,128)} %collective-permute-done.ln_ref), kind=kLoop, calls=%fused_computation.40 | loop fusion | bytes 53248 | tf_op jit(solution)/shard_map/slice | solution.py:222
  18.3 5.1 %collective-permute-start.2 = (f32[4,13,8,128]{3,2,1,0:T(8,128)S(1)}, f32[4,13,8,128]{3,2,1,0:T(8,128)S(1)}, u32[]{:S(2)}, u32[]{:S(2)}) collective-permute-start(f32[4,13,8,128]{3,2,1,0:T(8,128)S(1)} %get-tuple-element.33), channel_id=1, source_target_pairs={{32,0},{64,32},{96,64},{128,96},{160,128},{192,160},{224,192},{33,... | collective-permute-start | bytes 638984 | tf_op jit(solution)/shard_map/ppermute | solution.py:225
  23.4 2.3 %collective-permute-start.3 = (f32[4,13,8,128]{3,2,1,0:T(8,128)S(1)}, f32[4,13,8,128]{3,2,1,0:T(8,128)S(1)}, u32[]{:S(2)}, u32[]{:S(2)}) collective-permute-start(f32[4,13,8,128]{3,2,1,0:T(8,128)S(1)} %get-tuple-element.32), channel_id=1, source_target_pairs={{0,32},{32,64},{64,96},{96,128},{128,160},{160,192},{192,224},{1,3... | collective-permute-start | bytes 638984 | tf_op jit(solution)/shard_map/ppermute | solution.py:226
  26.2 1.3 %collective-permute-done.2.un_ref = f32[4,13,8,128]{3,2,1,0:T(8,128)S(1)} collective-permute-done((f32[4,13,8,128]{3,2,1,0:T(8,128)S(1)}, f32[4,13,8,128]{3,2,1,0:T(8,128)S(1)}, u32[]{:S(2)}, u32[]{:S(2)}) %collective-permute-start.2) | collective-permute-done | bytes 213024 | tf_op jit(solution)/shard_map/ppermute | solution.py:225
  27.5 6.0 %collective-permute-done.3.up_ref = f32[4,13,8,128]{3,2,1,0:T(8,128)S(1)} collective-permute-done((f32[4,13,8,128]{3,2,1,0:T(8,128)S(1)}, f32[4,13,8,128]{3,2,1,0:T(8,128)S(1)}, u32[]{:S(2)}, u32[]{:S(2)}) %collective-permute-start.3) | collective-permute-done | bytes 213024 | tf_op jit(solution)/shard_map/ppermute | solution.py:226
  33.5 0.7 copy-done.6
  34.2 16.5 %shard_map.59 = (f32[8,4,64,128]{3,2,1,0:T(8,128)}, f32[64,128]{1,0:T(8,128)}) custom-call(f32[8,256]{1,0:T(8,128)} %fusion.2.mask_ref, f32[8,4,64,128]{3,2,1,0:T(8,128)} %pr_ref.1, f32[2,4,64,128]{3,2,1,0:T(8,128)} %wi_ref.1, f32[2,4,64,128]{3,2,1,0:T(8,128)} %te_ref.1, f32[4,64,128]{2,1,0:T(8,128)} %ob_ref.1, ...), custom_call_target="tpu_custom_call" | custom-call | tf_op jit(solution)/shard_map/pallas_call | solution.py:137
  50.6 0.9 reduce_sum.9
  51.7 1.2 %collective-permute-done.4 = f32[8,8]{0,1:T(8,128)S(1)} collective-permute-done((f32[8,8]{0,1:T(8,128)S(1)}, f32[8,8]{0,1:T(8,128)S(1)}, u32[]{:S(2)}, u32[]{:S(2)}) %collective-permute-start.4) | collective-permute-done | bytes 288 | tf_op jit(solution)/shard_map/ppermute | solution.py:28
  52.8 3.6 %collective-permute-done.5 = f32[8,8]{0,1:T(8,128)S(1)} collective-permute-done((f32[8,8]{0,1:T(8,128)S(1)}, f32[8,8]{0,1:T(8,128)S(1)}, u32[]{:S(2)}, u32[]{:S(2)}) %collective-permute-start.5) | collective-permute-done | bytes 288 | tf_op jit(solution)/shard_map/ppermute | solution.py:28
  56.5 3.6 %collective-permute-done.6 = f32[8,8]{0,1:T(8,128)S(1)} collective-permute-done((f32[8,8]{0,1:T(8,128)S(1)}, f32[8,8]{0,1:T(8,128)S(1)}, u32[]{:S(2)}, u32[]{:S(2)}) %collective-permute-start.6) | collective-permute-done | bytes 288 | tf_op jit(solution)/shard_map/ppermute | solution.py:28
  60.7 3.9 %collective-permute-done.7 = f32[8,8]{0,1:T(8,128)S(1)} collective-permute-done((f32[8,8]{0,1:T(8,128)S(1)}, f32[8,8]{0,1:T(8,128)S(1)}, u32[]{:S(2)}, u32[]{:S(2)}) %collective-permute-start.7) | collective-permute-done | bytes 288 | tf_op jit(solution)/shard_map/ppermute | solution.py:28
  64.6 5.8 %collective-permute-start.8 = (f32[8,8]{0,1:T(8,128)S(1)}, f32[8,8]{0,1:T(8,128)S(1)}, u32[]{:S(2)}, u32[]{:S(2)}) collective-permute-start(f32[8,8]{0,1:T(8,128)S(1)} %add.51), channel_id=1, source_target_pairs={{0,16},{1,17},{2,18},{3,19},{4,20},{5,21},{6,22},{7,23},{8,24},{9,... | collective-permute-start | bytes 776 | tf_op jit(solution)/shard_map/ppermute | solution.py:28
  70.3 1.8 %collective-permute-done.8 = f32[8,8]{0,1:T(8,128)S(1)} collective-permute-done((f32[8,8]{0,1:T(8,128)S(1)}, f32[8,8]{0,1:T(8,128)S(1)}, u32[]{:S(2)}, u32[]{:S(2)}) %collective-permute-start.8) | collective-permute-done | bytes 288 | tf_op jit(solution)/shard_map/ppermute | solution.py:28
  72.1 5.1 %collective-permute-done.9 = f32[8,8]{0,1:T(8,128)S(1)} collective-permute-done((f32[8,8]{0,1:T(8,128)S(1)}, f32[8,8]{0,1:T(8,128)S(1)}, u32[]{:S(2)}, u32[]{:S(2)}) %collective-permute-start.9) | collective-permute-done | bytes 288 | tf_op jit(solution)/shard_map/ppermute | solution.py:28
  77.7 3.1 %collective-permute-done.10 = f32[8,8]{0,1:T(8,128)S(1)} collective-permute-done((f32[8,8]{0,1:T(8,128)S(1)}, f32[8,8]{0,1:T(8,128)S(1)}, u32[]{:S(2)}, u32[]{:S(2)}) %collective-permute-start.10) | collective-permute-done | bytes 288 | tf_op jit(solution)/shard_map/ppermute | solution.py:28
  80.8 1.1 %collective-permute-start.11 = (f32[8,8]{0,1:T(8,128)S(1)}, f32[8,8]{0,1:T(8,128)S(1)}, u32[]{:S(2)}, u32[]{:S(2)}) collective-permute-start(f32[8,8]{0,1:T(8,128)S(1)} %add.54), channel_id=1, source_target_pairs={{0,128},{32,160},{64,192},{96,224},{128,0},{160,32},{192,64},{224,... | collective-permute-start | bytes 776 | tf_op jit(solution)/shard_map/ppermute | solution.py:28
  81.9 4.0 %collective-permute-done.11 = f32[8,8]{0,1:T(8,128)S(1)} collective-permute-done((f32[8,8]{0,1:T(8,128)S(1)}, f32[8,8]{0,1:T(8,128)S(1)}, u32[]{:S(2)}, u32[]{:S(2)}) %collective-permute-start.11) | collective-permute-done | bytes 288 | tf_op jit(solution)/shard_map/ppermute | solution.py:28
  86.0 0.7 cholesky.17
  86.8 0.6 compare_reduce_fusion
  87.4 0.6 multiply_bitcast_fusion
  88.7 0.8 fusion.3.inv_ref
  89.5 0.7 copy.53
  90.1 3.5 %shard_map.60 = f32[8,4,64,128]{3,2,1,0:T(8,128)} custom-call(f32[8,8]{1,0:T(8,128)} %fusion.3.inv_ref, f32[1,1]{1,0:T(1,128)} %constant.65.clone.1.scale_ref, f32[8,4,64,128]{3,2,1,0:T(8,128)} %get-tuple-element.5.z_ref), custom_call_target="tpu_custom_call" | custom-call | tf_op jit(solution)/shard_map/pallas_call | solution.py:186
  (63 shorter events, 7.0 us)
Async XLA Ops:
  0.6 1.7 %copy-start.4 = (f32[4,64,128]{2,1,0:T(8,128)S(1)}, f32[4,64,128]{2,1,0:T(8,128)}, u32[]{:S(2)}) copy-start(f32[4,64,128]{2,1,0:T(8,128)} %ob_ref.1) | copy-start | bytes 393220
  0.6 2.6 %copy-start = (f32[8,4,64,128]{3,2,1,0:T(8,128)S(1)}, f32[8,4,64,128]{3,2,1,0:T(8,128)}, u32[]{:S(2)}) copy-start(f32[8,4,64,128]{3,2,1,0:T(8,128)} %pr_ref.1) | copy-start | bytes 3145732
  2.4 0.7 copy-start.3
  4.0 11.1 %collective-permute-start.1 = (f32[4,13,8,128]{3,2,1,0:T(8,128)}, f32[4,13,8,128]{3,2,1,0:T(8,128)}, u32[]{:S(2)}, u32[]{:S(2)}) collective-permute-start(f32[4,13,8,128]{3,2,1,0:T(8,128)} %pad_maximum_fusion.1), channel_id=1, source_target_pairs={{0,1},{1,2},{2,3},{3,4},{4,5},{5,6},{6,7},{7,8},{8,9},{9,10},{10,1... | collective-permute-start | bytes 638984 | tf_op jit(solution)/shard_map/ppermute | solution.py:216
  4.9 11.7 %collective-permute-start = (f32[4,13,8,128]{3,2,1,0:T(8,128)}, f32[4,13,8,128]{3,2,1,0:T(8,128)}, u32[]{:S(2)}, u32[]{:S(2)}) collective-permute-start(f32[4,13,8,128]{3,2,1,0:T(8,128)} %pad_maximum_fusion), channel_id=1, source_target_pairs={{1,0},{2,1},{3,2},{4,3},{5,4},{6,5},{7,6},{8,7},{9,8},{10,9},{11,1... | collective-permute-start | bytes 638984 | tf_op jit(solution)/shard_map/ppermute | solution.py:215
  11.2 0.9 %copy-start.1 = (f32[2,4,64,128]{3,2,1,0:T(8,128)S(1)}, f32[2,4,64,128]{3,2,1,0:T(8,128)}, u32[]{:S(2)}) copy-start(f32[2,4,64,128]{3,2,1,0:T(8,128)} %wi_ref.1) | copy-start | bytes 786436
  12.1 0.9 %copy-start.2 = (f32[2,4,64,128]{3,2,1,0:T(8,128)S(1)}, f32[2,4,64,128]{3,2,1,0:T(8,128)}, u32[]{:S(2)}) copy-start(f32[2,4,64,128]{3,2,1,0:T(8,128)} %te_ref.1) | copy-start | bytes 786436
  18.3 9.2 %collective-permute-start.2 = (f32[4,13,8,128]{3,2,1,0:T(8,128)S(1)}, f32[4,13,8,128]{3,2,1,0:T(8,128)S(1)}, u32[]{:S(2)}, u32[]{:S(2)}) collective-permute-start(f32[4,13,8,128]{3,2,1,0:T(8,128)S(1)} %get-tuple-element.33), channel_id=1, source_target_pairs={{32,0},{64,32},{96,64},{128,96},{160,128},{192,160},{224,192},{33,... | collective-permute-start | bytes 638984 | tf_op jit(solution)/shard_map/ppermute | solution.py:225
  23.4 10.1 %collective-permute-start.3 = (f32[4,13,8,128]{3,2,1,0:T(8,128)S(1)}, f32[4,13,8,128]{3,2,1,0:T(8,128)S(1)}, u32[]{:S(2)}, u32[]{:S(2)}) collective-permute-start(f32[4,13,8,128]{3,2,1,0:T(8,128)S(1)} %get-tuple-element.32), channel_id=1, source_target_pairs={{0,32},{32,64},{64,96},{96,128},{128,160},{160,192},{192,224},{1,3... | collective-permute-start | bytes 638984 | tf_op jit(solution)/shard_map/ppermute | solution.py:226
  27.5 6.0 %copy-start.5 = (f32[4,13,8,128]{3,2,1,0:T(8,128)}, f32[4,13,8,128]{3,2,1,0:T(8,128)S(1)}, u32[]{:S(2)}) copy-start(f32[4,13,8,128]{3,2,1,0:T(8,128)S(1)} %collective-permute-done.2.un_ref) | copy-start | bytes 638980
  33.5 0.7 copy-start.6
  51.7 1.2 %collective-permute-start.4 = (f32[8,8]{0,1:T(8,128)S(1)}, f32[8,8]{0,1:T(8,128)S(1)}, u32[]{:S(2)}, u32[]{:S(2)}) collective-permute-start(f32[8,8]{0,1:T(8,128)S(1)} %copy.50), channel_id=1, source_target_pairs={{0,1},{1,0},{2,3},{3,2},{4,5},{5,4},{6,7},{7,6},{8,9},{9,8},{10,11... | collective-permute-start | bytes 776 | tf_op jit(solution)/shard_map/ppermute | solution.py:28
  52.8 3.6 %collective-permute-start.5 = (f32[8,8]{0,1:T(8,128)S(1)}, f32[8,8]{0,1:T(8,128)S(1)}, u32[]{:S(2)}, u32[]{:S(2)}) collective-permute-start(f32[8,8]{0,1:T(8,128)S(1)} %add.48), channel_id=1, source_target_pairs={{0,2},{1,3},{2,0},{3,1},{4,6},{5,7},{6,4},{7,5},{8,10},{9,11},{10,... | collective-permute-start | bytes 776 | tf_op jit(solution)/shard_map/ppermute | solution.py:28
  56.5 3.6 %collective-permute-start.6 = (f32[8,8]{0,1:T(8,128)S(1)}, f32[8,8]{0,1:T(8,128)S(1)}, u32[]{:S(2)}, u32[]{:S(2)}) collective-permute-start(f32[8,8]{0,1:T(8,128)S(1)} %add.49), channel_id=1, source_target_pairs={{0,4},{1,5},{2,6},{3,7},{4,0},{5,1},{6,2},{7,3},{8,12},{9,13},{10,... | collective-permute-start | bytes 776 | tf_op jit(solution)/shard_map/ppermute | solution.py:28
  60.1 4.5 %collective-permute-start.7 = (f32[8,8]{0,1:T(8,128)S(1)}, f32[8,8]{0,1:T(8,128)S(1)}, u32[]{:S(2)}, u32[]{:S(2)}) collective-permute-start(f32[8,8]{0,1:T(8,128)S(1)} %add.50), channel_id=1, source_target_pairs={{0,8},{1,9},{2,10},{3,11},{4,12},{5,13},{6,14},{7,15},{8,0},{9,1},... | collective-permute-start | bytes 776 | tf_op jit(solution)/shard_map/ppermute | solution.py:28
  64.6 7.5 %collective-permute-start.8 = (f32[8,8]{0,1:T(8,128)S(1)}, f32[8,8]{0,1:T(8,128)S(1)}, u32[]{:S(2)}, u32[]{:S(2)}) collective-permute-start(f32[8,8]{0,1:T(8,128)S(1)} %add.51), channel_id=1, source_target_pairs={{0,16},{1,17},{2,18},{3,19},{4,20},{5,21},{6,22},{7,23},{8,24},{9,... | collective-permute-start | bytes 776 | tf_op jit(solution)/shard_map/ppermute | solution.py:28
  72.1 5.1 %collective-permute-start.9 = (f32[8,8]{0,1:T(8,128)S(1)}, f32[8,8]{0,1:T(8,128)S(1)}, u32[]{:S(2)}, u32[]{:S(2)}) collective-permute-start(f32[8,8]{0,1:T(8,128)S(1)} %add.52), channel_id=1, source_target_pairs={{0,32},{32,0},{64,96},{96,64},{128,160},{160,128},{192,224},{224,1... | collective-permute-start | bytes 776 | tf_op jit(solution)/shard_map/ppermute | solution.py:28
  77.2 3.6 %collective-permute-start.10 = (f32[8,8]{0,1:T(8,128)S(1)}, f32[8,8]{0,1:T(8,128)S(1)}, u32[]{:S(2)}, u32[]{:S(2)}) collective-permute-start(f32[8,8]{0,1:T(8,128)S(1)} %add.53), channel_id=1, source_target_pairs={{0,64},{32,96},{64,0},{96,32},{128,192},{160,224},{192,128},{224,1... | collective-permute-start | bytes 776 | tf_op jit(solution)/shard_map/ppermute | solution.py:28
  80.8 5.1 %collective-permute-start.11 = (f32[8,8]{0,1:T(8,128)S(1)}, f32[8,8]{0,1:T(8,128)S(1)}, u32[]{:S(2)}, u32[]{:S(2)}) collective-permute-start(f32[8,8]{0,1:T(8,128)S(1)} %add.54), channel_id=1, source_target_pairs={{0,128},{32,160},{64,192},{96,224},{128,0},{160,32},{192,64},{224,... | collective-permute-start | bytes 776 | tf_op jit(solution)/shard_map/ppermute | solution.py:28

commit v13 on v11

--- a/solution.py
+++ b/solution.py
@@ -1,3 +1,6 @@
+import functools
+
+import numpy as np
 import jax
 import jax.numpy as jnp
 from jax import lax
@@ -158,9 +161,8 @@
         ],
     )(mask, probes, wind, wind_tend, obs_weight, lon_next, lon_prev, lat_next, lat_prev)
 
-def basis_kernel(inv_ref, scale_ref, z_ref, o_ref):
+def basis_kernel(inv_ref, z_ref, o_ref, *, scale):
     probes, levels, rows = z_ref.shape[:3]
-    scale = scale_ref[0, 0]
     chunks = rows // 8
 
     def chunk(c, carry):
@@ -180,16 +182,15 @@
 def basis(inverse, scale, field):
     whole = pl.BlockSpec(field.shape, lambda i: (0, 0, 0, 0))
     return pl.pallas_call(
-        basis_kernel,
+        functools.partial(basis_kernel, scale=scale),
         grid=(1,),
         in_specs=[
             pl.BlockSpec(memory_space=pltpu.SMEM),
-            pl.BlockSpec(memory_space=pltpu.SMEM),
             whole,
         ],
         out_specs=whole,
         out_shape=jax.ShapeDtypeStruct(field.shape, jnp.float32),
-    )(inverse, scale, field)
+    )(inverse, field)
 
 def body(probes, wind, wind_tend, obs_weight):
     n_probes, levels, width_lon, width_lat = probes.shape
@@ -238,7 +239,7 @@
     upper = lower.T
     cells = field.shape[1] * width_lon * width_lat * lax.axis_size("lat") * lax.axis_size("lon")
     scale = jnp.sqrt(jnp.float32(cells))
-    result = basis(lower_inverse(lower), scale.reshape(1, 1), field)
+    result = basis(lower_inverse(lower), float(np.sqrt(np.float32(cells))), field)
     return (result, upper / scale)
 
 

time: 93.7 us -> 93.7 us (level)
  no operation moved by 1% of the time
where the time goes in v13:
time: 93.7 us; the launch traced here: 93.3 us
  waiting for transfers between devices  33.4 us (36%)
  starting transfers between devices  21.7 us (23%)
  Pallas kernels  19.4 us (21%)
  local copies, waits for them, and re-layouts  11 us (12%)
  other arithmetic  6.03 us (6%)
    ppermute x8, waiting for transfers between devices, all_sum(): lax.ppermute(value, axis, [(i, i ^ stride) for i in range(count)])  26.2 us
    pallas_call x1, Pallas kernels, transport(): pl.pallas_call(transport_kernel, grid=(levels,), in_specs=[pl.BlockSpec((...  15.9 us
    ppermute x8, starting transfers between devices, all_sum(): lax.ppermute(value, axis, [(i, i ^ stride) for i in range(count)])  8.05 us
    ppermute x1, starting transfers between devices, body(): lax.ppermute(heads, 'lon', [((i + 1) % n_lon, i) for i in range(n_lon)])  6.31 us
    ppermute x1, waiting for transfers between devices, body(): lax.ppermute(jnp.swapaxes(edge_hi, 2, 3), 'lat', [(j, j + 1) for j in ran...  5.98 us
    ppermute x1, starting transfers between devices, body(): lax.ppermute(jnp.swapaxes(edge_lo, 2, 3), 'lat', [(j + 1, j) for j in ran...  5.07 us
    unnamed x28, local copies, waits for them, and re-layouts  5.02 us
    pallas_call x1, Pallas kernels, basis(): pl.pallas_call(functools.partial(basis_kernel, scale=scale), grid=(1,), i...  3.48 us
  transfers between devices with their start and end apart: 12, of which 10 were waited for; matrix products, arithmetic and copies ran while one was open for 6% of the time, Pallas kernels for 0%

profile of v13, /device:TPU:6, one launch (start us, length us, event | category | flops | bytes accessed | tf_op | source)
XLA Modules:
  0.0 93.3 jit_solution(8396272598595227539)
XLA Ops:
  0.7 0.9 fusion.10
  1.5 0.8 fusion.11
  3.3 0.7 pad_maximum_fusion.1
  4.2 0.7 pad_maximum_fusion
  4.9 6.3 %collective-permute-start = (f32[4,13,8,128]{3,2,1,0:T(8,128)}, f32[4,13,8,128]{3,2,1,0:T(8,128)}, u32[]{:S(2)}, u32[]{:S(2)}) collective-permute-start(f32[4,13,8,128]{3,2,1,0:T(8,128)} %pad_maximum_fusion), channel_id=1, source_target_pairs={{1,0},{2,1},{3,2},{4,3},{5,4},{6,5},{7,6},{8,7},{9,8},{10,9},{11,1... | collective-permute-start | bytes 638984 | tf_op jit(solution)/shard_map/ppermute | solution.py:212
  12.2 0.8 copy-done.2
  14.4 0.7 slice_bitcast_fusion.2
  15.2 1.1 %fusion.13 = (f32[4,13,8,8]{3,2,1,0:T(8,128)S(1)}, f32[4,13,8,8]{3,2,1,0:T(8,128)S(1)}) fusion(f32[4,13,8,128]{3,2,1,0:T(8,128)} %collective-permute-done.1.lp_ref), kind=kLoop, calls=%fused_computation.41 | loop fusion | bytes 53248 | tf_op jit(solution)/shard_map/slice | solution.py:219
  16.6 1.1 %fusion.12 = (f32[4,13,8,8]{3,2,1,0:T(8,128)S(1)}, f32[4,13,8,8]{3,2,1,0:T(8,128)S(1)}) fusion(f32[4,13,8,128]{3,2,1,0:T(8,128)} %collective-permute-done.ln_ref), kind=kLoop, calls=%fused_computation.40 | loop fusion | bytes 53248 | tf_op jit(solution)/shard_map/slice | solution.py:219
  18.3 5.1 %collective-permute-start.2 = (f32[4,13,8,128]{3,2,1,0:T(8,128)S(1)}, f32[4,13,8,128]{3,2,1,0:T(8,128)S(1)}, u32[]{:S(2)}, u32[]{:S(2)}) collective-permute-start(f32[4,13,8,128]{3,2,1,0:T(8,128)S(1)} %get-tuple-element.33), channel_id=1, source_target_pairs={{32,0},{64,32},{96,64},{128,96},{160,128},{192,160},{224,192},{33,... | collective-permute-start | bytes 638984 | tf_op jit(solution)/shard_map/ppermute | solution.py:222
  23.4 2.3 %collective-permute-start.3 = (f32[4,13,8,128]{3,2,1,0:T(8,128)S(1)}, f32[4,13,8,128]{3,2,1,0:T(8,128)S(1)}, u32[]{:S(2)}, u32[]{:S(2)}) collective-permute-start(f32[4,13,8,128]{3,2,1,0:T(8,128)S(1)} %get-tuple-element.32), channel_id=1, source_target_pairs={{0,32},{32,64},{64,96},{96,128},{128,160},{160,192},{192,224},{1,3... | collective-permute-start | bytes 638984 | tf_op jit(solution)/shard_map/ppermute | solution.py:223
  26.3 1.3 %collective-permute-done.2.un_ref = f32[4,13,8,128]{3,2,1,0:T(8,128)S(1)} collective-permute-done((f32[4,13,8,128]{3,2,1,0:T(8,128)S(1)}, f32[4,13,8,128]{3,2,1,0:T(8,128)S(1)}, u32[]{:S(2)}, u32[]{:S(2)}) %collective-permute-start.2) | collective-permute-done | bytes 213024 | tf_op jit(solution)/shard_map/ppermute | solution.py:222
  27.5 6.0 %collective-permute-done.3.up_ref = f32[4,13,8,128]{3,2,1,0:T(8,128)S(1)} collective-permute-done((f32[4,13,8,128]{3,2,1,0:T(8,128)S(1)}, f32[4,13,8,128]{3,2,1,0:T(8,128)S(1)}, u32[]{:S(2)}, u32[]{:S(2)}) %collective-permute-start.3) | collective-permute-done | bytes 213024 | tf_op jit(solution)/shard_map/ppermute | solution.py:223
  33.5 0.7 copy-done.6
  34.2 15.9 %shard_map.59 = (f32[8,4,64,128]{3,2,1,0:T(8,128)}, f32[4,64,128]{2,1,0:T(8,128)}) custom-call(f32[8,256]{1,0:T(8,128)} %fusion.2.mask_ref, f32[8,4,64,128]{3,2,1,0:T(8,128)} %pr_ref.1, f32[2,4,64,128]{3,2,1,0:T(8,128)} %wi_ref.1, f32[2,4,64,128]{3,2,1,0:T(8,128)} %te_ref.1, f32[4,64,128]{2,1,0:T(8,128)} %ob_ref.1, ...), custom_call_target="tpu_custom_call" | custom-call | tf_op jit(solution)/shard_map/pallas_call | solution.py:136
  50.1 1.0 %reduce_sum.9 = f32[64]{0:T(128)S(1)} reduce(f32[4,64,128]{2,1,0:T(8,128)} %get-tuple-element.4, f32[]{:T(128)} %constant.60.clone.1), dimensions={0,2}, to_apply=%region_0.1 | reduce | flops 32704 | bytes 131332 | tf_op jit(solution)/shard_map/reduce_sum | solution.py:236
  51.3 1.2 %collective-permute-done.4 = f32[8,8]{0,1:T(8,128)S(1)} collective-permute-done((f32[8,8]{0,1:T(8,128)S(1)}, f32[8,8]{0,1:T(8,128)S(1)}, u32[]{:S(2)}, u32[]{:S(2)}) %collective-permute-start.4) | collective-permute-done | bytes 288 | tf_op jit(solution)/shard_map/ppermute | solution.py:31
  52.5 3.6 %collective-permute-done.5 = f32[8,8]{0,1:T(8,128)S(1)} collective-permute-done((f32[8,8]{0,1:T(8,128)S(1)}, f32[8,8]{0,1:T(8,128)S(1)}, u32[]{:S(2)}, u32[]{:S(2)}) %collective-permute-start.5) | collective-permute-done | bytes 288 | tf_op jit(solution)/shard_map/ppermute | solution.py:31
  56.1 3.6 %collective-permute-done.6 = f32[8,8]{0,1:T(8,128)S(1)} collective-permute-done((f32[8,8]{0,1:T(8,128)S(1)}, f32[8,8]{0,1:T(8,128)S(1)}, u32[]{:S(2)}, u32[]{:S(2)}) %collective-permute-start.6) | collective-permute-done | bytes 288 | tf_op jit(solution)/shard_map/ppermute | solution.py:31
  60.3 3.9 %collective-permute-done.7 = f32[8,8]{0,1:T(8,128)S(1)} collective-permute-done((f32[8,8]{0,1:T(8,128)S(1)}, f32[8,8]{0,1:T(8,128)S(1)}, u32[]{:S(2)}, u32[]{:S(2)}) %collective-permute-start.7) | collective-permute-done | bytes 288 | tf_op jit(solution)/shard_map/ppermute | solution.py:31
  64.2 5.8 %collective-permute-start.8 = (f32[8,8]{0,1:T(8,128)S(1)}, f32[8,8]{0,1:T(8,128)S(1)}, u32[]{:S(2)}, u32[]{:S(2)}) collective-permute-start(f32[8,8]{0,1:T(8,128)S(1)} %add.51), channel_id=1, source_target_pairs={{0,16},{1,17},{2,18},{3,19},{4,20},{5,21},{6,22},{7,23},{8,24},{9,... | collective-permute-start | bytes 776 | tf_op jit(solution)/shard_map/ppermute | solution.py:31
  70.0 1.8 %collective-permute-done.8 = f32[8,8]{0,1:T(8,128)S(1)} collective-permute-done((f32[8,8]{0,1:T(8,128)S(1)}, f32[8,8]{0,1:T(8,128)S(1)}, u32[]{:S(2)}, u32[]{:S(2)}) %collective-permute-start.8) | collective-permute-done | bytes 288 | tf_op jit(solution)/shard_map/ppermute | solution.py:31
  71.7 5.1 %collective-permute-done.9 = f32[8,8]{0,1:T(8,128)S(1)} collective-permute-done((f32[8,8]{0,1:T(8,128)S(1)}, f32[8,8]{0,1:T(8,128)S(1)}, u32[]{:S(2)}, u32[]{:S(2)}) %collective-permute-start.9) | collective-permute-done | bytes 288 | tf_op jit(solution)/shard_map/ppermute | solution.py:31
  77.4 3.1 %collective-permute-done.10 = f32[8,8]{0,1:T(8,128)S(1)} collective-permute-done((f32[8,8]{0,1:T(8,128)S(1)}, f32[8,8]{0,1:T(8,128)S(1)}, u32[]{:S(2)}, u32[]{:S(2)}) %collective-permute-start.10) | collective-permute-done | bytes 288 | tf_op jit(solution)/shard_map/ppermute | solution.py:31
  80.5 1.1 %collective-permute-start.11 = (f32[8,8]{0,1:T(8,128)S(1)}, f32[8,8]{0,1:T(8,128)S(1)}, u32[]{:S(2)}, u32[]{:S(2)}) collective-permute-start(f32[8,8]{0,1:T(8,128)S(1)} %add.54), channel_id=1, source_target_pairs={{0,128},{32,160},{64,192},{96,224},{128,0},{160,32},{192,64},{224,... | collective-permute-start | bytes 776 | tf_op jit(solution)/shard_map/ppermute | solution.py:31
  81.6 4.0 %collective-permute-done.11 = f32[8,8]{0,1:T(8,128)S(1)} collective-permute-done((f32[8,8]{0,1:T(8,128)S(1)}, f32[8,8]{0,1:T(8,128)S(1)}, u32[]{:S(2)}, u32[]{:S(2)}) %collective-permute-start.11) | collective-permute-done | bytes 288 | tf_op jit(solution)/shard_map/ppermute | solution.py:31
  85.7 0.7 cholesky.17
  86.4 0.6 compare_reduce_fusion
  87.1 0.6 multiply_bitcast_fusion
  88.3 0.8 fusion.3.inv_ref
  89.1 0.7 copy.53
  89.8 3.5 %shard_map.60 = f32[8,4,64,128]{3,2,1,0:T(8,128)} custom-call(f32[8,8]{1,0:T(8,128)} %fusion.3.inv_ref, f32[8,4,64,128]{3,2,1,0:T(8,128)} %get-tuple-element.5.z_ref), custom_call_target="tpu_custom_call" | custom-call | tf_op jit(solution)/shard_map/pallas_call | solution.py:184
  (63 shorter events, 7.0 us)
Async XLA Ops:
  0.6 1.7 %copy-start.4 = (f32[4,64,128]{2,1,0:T(8,128)S(1)}, f32[4,64,128]{2,1,0:T(8,128)}, u32[]{:S(2)}) copy-start(f32[4,64,128]{2,1,0:T(8,128)} %ob_ref.1) | copy-start | bytes 393220
  0.6 2.6 %copy-start = (f32[8,4,64,128]{3,2,1,0:T(8,128)S(1)}, f32[8,4,64,128]{3,2,1,0:T(8,128)}, u32[]{:S(2)}) copy-start(f32[8,4,64,128]{3,2,1,0:T(8,128)} %pr_ref.1) | copy-start | bytes 3145732
  2.4 0.7 copy-start.3
  4.0 11.1 %collective-permute-start.1 = (f32[4,13,8,128]{3,2,1,0:T(8,128)}, f32[4,13,8,128]{3,2,1,0:T(8,128)}, u32[]{:S(2)}, u32[]{:S(2)}) collective-permute-start(f32[4,13,8,128]{3,2,1,0:T(8,128)} %pad_maximum_fusion.1), channel_id=1, source_target_pairs={{0,1},{1,2},{2,3},{3,4},{4,5},{5,6},{6,7},{7,8},{8,9},{9,10},{10,1... | collective-permute-start | bytes 638984 | tf_op jit(solution)/shard_map/ppermute | solution.py:213
  4.9 11.7 %collective-permute-start = (f32[4,13,8,128]{3,2,1,0:T(8,128)}, f32[4,13,8,128]{3,2,1,0:T(8,128)}, u32[]{:S(2)}, u32[]{:S(2)}) collective-permute-start(f32[4,13,8,128]{3,2,1,0:T(8,128)} %pad_maximum_fusion), channel_id=1, source_target_pairs={{1,0},{2,1},{3,2},{4,3},{5,4},{6,5},{7,6},{8,7},{9,8},{10,9},{11,1... | collective-permute-start | bytes 638984 | tf_op jit(solution)/shard_map/ppermute | solution.py:212
  11.2 0.9 %copy-start.1 = (f32[2,4,64,128]{3,2,1,0:T(8,128)S(1)}, f32[2,4,64,128]{3,2,1,0:T(8,128)}, u32[]{:S(2)}) copy-start(f32[2,4,64,128]{3,2,1,0:T(8,128)} %wi_ref.1) | copy-start | bytes 786436
  12.1 0.9 %copy-start.2 = (f32[2,4,64,128]{3,2,1,0:T(8,128)S(1)}, f32[2,4,64,128]{3,2,1,0:T(8,128)}, u32[]{:S(2)}) copy-start(f32[2,4,64,128]{3,2,1,0:T(8,128)} %te_ref.1) | copy-start | bytes 786436
  18.3 9.2 %collective-permute-start.2 = (f32[4,13,8,128]{3,2,1,0:T(8,128)S(1)}, f32[4,13,8,128]{3,2,1,0:T(8,128)S(1)}, u32[]{:S(2)}, u32[]{:S(2)}) collective-permute-start(f32[4,13,8,128]{3,2,1,0:T(8,128)S(1)} %get-tuple-element.33), channel_id=1, source_target_pairs={{32,0},{64,32},{96,64},{128,96},{160,128},{192,160},{224,192},{33,... | collective-permute-start | bytes 638984 | tf_op jit(solution)/shard_map/ppermute | solution.py:222
  23.4 10.1 %collective-permute-start.3 = (f32[4,13,8,128]{3,2,1,0:T(8,128)S(1)}, f32[4,13,8,128]{3,2,1,0:T(8,128)S(1)}, u32[]{:S(2)}, u32[]{:S(2)}) collective-permute-start(f32[4,13,8,128]{3,2,1,0:T(8,128)S(1)} %get-tuple-element.32), channel_id=1, source_target_pairs={{0,32},{32,64},{64,96},{96,128},{128,160},{160,192},{192,224},{1,3... | collective-permute-start | bytes 638984 | tf_op jit(solution)/shard_map/ppermute | solution.py:223
  27.5 6.0 %copy-start.5 = (f32[4,13,8,128]{3,2,1,0:T(8,128)}, f32[4,13,8,128]{3,2,1,0:T(8,128)S(1)}, u32[]{:S(2)}) copy-start(f32[4,13,8,128]{3,2,1,0:T(8,128)S(1)} %collective-permute-done.2.un_ref) | copy-start | bytes 638980
  33.5 0.7 copy-start.6
  51.3 1.2 %collective-permute-start.4 = (f32[8,8]{0,1:T(8,128)S(1)}, f32[8,8]{0,1:T(8,128)S(1)}, u32[]{:S(2)}, u32[]{:S(2)}) collective-permute-start(f32[8,8]{0,1:T(8,128)S(1)} %copy.50), channel_id=1, source_target_pairs={{0,1},{1,0},{2,3},{3,2},{4,5},{5,4},{6,7},{7,6},{8,9},{9,8},{10,11... | collective-permute-start | bytes 776 | tf_op jit(solution)/shard_map/ppermute | solution.py:31
  52.5 3.6 %collective-permute-start.5 = (f32[8,8]{0,1:T(8,128)S(1)}, f32[8,8]{0,1:T(8,128)S(1)}, u32[]{:S(2)}, u32[]{:S(2)}) collective-permute-start(f32[8,8]{0,1:T(8,128)S(1)} %add.48), channel_id=1, source_target_pairs={{0,2},{1,3},{2,0},{3,1},{4,6},{5,7},{6,4},{7,5},{8,10},{9,11},{10,... | collective-permute-start | bytes 776 | tf_op jit(solution)/shard_map/ppermute | solution.py:31
  56.1 3.6 %collective-permute-start.6 = (f32[8,8]{0,1:T(8,128)S(1)}, f32[8,8]{0,1:T(8,128)S(1)}, u32[]{:S(2)}, u32[]{:S(2)}) collective-permute-start(f32[8,8]{0,1:T(8,128)S(1)} %add.49), channel_id=1, source_target_pairs={{0,4},{1,5},{2,6},{3,7},{4,0},{5,1},{6,2},{7,3},{8,12},{9,13},{10,... | collective-permute-start | bytes 776 | tf_op jit(solution)/shard_map/ppermute | solution.py:31
  59.7 4.5 %collective-permute-start.7 = (f32[8,8]{0,1:T(8,128)S(1)}, f32[8,8]{0,1:T(8,128)S(1)}, u32[]{:S(2)}, u32[]{:S(2)}) collective-permute-start(f32[8,8]{0,1:T(8,128)S(1)} %add.50), channel_id=1, source_target_pairs={{0,8},{1,9},{2,10},{3,11},{4,12},{5,13},{6,14},{7,15},{8,0},{9,1},... | collective-permute-start | bytes 776 | tf_op jit(solution)/shard_map/ppermute | solution.py:31
  64.2 7.5 %collective-permute-start.8 = (f32[8,8]{0,1:T(8,128)S(1)}, f32[8,8]{0,1:T(8,128)S(1)}, u32[]{:S(2)}, u32[]{:S(2)}) collective-permute-start(f32[8,8]{0,1:T(8,128)S(1)} %add.51), channel_id=1, source_target_pairs={{0,16},{1,17},{2,18},{3,19},{4,20},{5,21},{6,22},{7,23},{8,24},{9,... | collective-permute-start | bytes 776 | tf_op jit(solution)/shard_map/ppermute | solution.py:31
  71.7 5.1 %collective-permute-start.9 = (f32[8,8]{0,1:T(8,128)S(1)}, f32[8,8]{0,1:T(8,128)S(1)}, u32[]{:S(2)}, u32[]{:S(2)}) collective-permute-start(f32[8,8]{0,1:T(8,128)S(1)} %add.52), channel_id=1, source_target_pairs={{0,32},{32,0},{64,96},{96,64},{128,160},{160,128},{192,224},{224,1... | collective-permute-start | bytes 776 | tf_op jit(solution)/shard_map/ppermute | solution.py:31
  76.8 3.6 %collective-permute-start.10 = (f32[8,8]{0,1:T(8,128)S(1)}, f32[8,8]{0,1:T(8,128)S(1)}, u32[]{:S(2)}, u32[]{:S(2)}) collective-permute-start(f32[8,8]{0,1:T(8,128)S(1)} %add.53), channel_id=1, source_target_pairs={{0,64},{32,96},{64,0},{96,32},{128,192},{160,224},{192,128},{224,1... | collective-permute-start | bytes 776 | tf_op jit(solution)/shard_map/ppermute | solution.py:31
  80.5 5.1 %collective-permute-start.11 = (f32[8,8]{0,1:T(8,128)S(1)}, f32[8,8]{0,1:T(8,128)S(1)}, u32[]{:S(2)}, u32[]{:S(2)}) collective-permute-start(f32[8,8]{0,1:T(8,128)S(1)} %add.54), channel_id=1, source_target_pairs={{0,128},{32,160},{64,192},{96,224},{128,0},{160,32},{192,64},{224,... | collective-permute-start | bytes 776 | tf_op jit(solution)/shard_map/ppermute | solution.py:31
